TPU v7x, 256 devices: a whole 4x4x8 slice. The times are simulated.
256 devices in a mesh: dp: 32 (over z_lo, y, x), tensor: 8 (over z_hi, core).
Axes of the slice: x: 4, y: 4, z: 8 (z_hi: 4, z_lo: 2; z = z_hi * 2 + z_lo), core: 2. Of those that a mesh axis runs over, the one named last changes fastest.
Arguments:
- embeds: bfloat16 [512, 4608], P('dp'), may hold values from -6 to 6
- owner: int32 [64, 8], P('dp'), may hold values from 0 to 7, each once within a row
- pairs: int32 [64, 56, 2], P('dp'), may hold values from 0 to 7, as said below
- pref_weight: bfloat16 [2, 4608, 4608], P(None, 'dp', 'tensor'), may hold values from -0.0625 to 0.0625
- pref_bias: float32 [4608], P('tensor'), may hold values from -3 to 3
- pref_out: float32 [4608], P('tensor'), may hold values from -0.375 to 0.375
- logratio: float32 [512], P('dp'), may hold values from -3 to 3
- attn_out: bfloat16 [32768, 4096], P('dp', 'tensor'), may hold values from -6 to 6
- grad_out: bfloat16 [32768, 4608], P('dp', 'tensor'), may hold values from -6 to 6
- w_out: bfloat16 [4608, 4096], P('dp', 'tensor'), may hold values from -0.09375 to 0.09375
Outputs:
- d_attn: bfloat16 [32768, 4096], P('dp', 'tensor')
- o_grad: float32 [4608, 4096], P('dp', 'tensor')
Inputs may be any that keep to these rules, and one draw needn't show every extreme that they name: `pairs`: the two numbers of a pair differ. Each row of owner names every number once.
All inputs are finite; a program needn't handle non-finite values.
Results may differ from a plain program's by a relative error of at most 0.0049.
Values may be sent and summed in bfloat16 or wider, within the bound.
No kernel may reach another device: no remote copies, remote signals or barrier semaphores. Data moves between devices by JAX's collectives and lax.ppermute only.
A program may use at most 128 MiB of HBM per device.

v0:
```python
import jax
import jax.numpy as jnp
from jax import lax
from jax.sharding import PartitionSpec as P

eta_scale = 2.0


def shards(
    embeds, owner, pairs, pref_weight, pref_bias, pref_out, logratio, attn_out, grad_out, w_out
):
    resp_dev = embeds.shape[0]
    prompts_dev = owner.shape[0]
    groups = owner.shape[1]
    npairs = pairs.shape[1]
    width_local = pref_weight.shape[2]
    features = lax.all_gather(grad_out, "tensor", axis=1, tiled=True)
    base = (jnp.arange(prompts_dev, dtype=jnp.int32) * groups)[:, None]
    row_a = base + jnp.take_along_axis(owner, pairs[:, :, 0], axis=1)
    row_b = base + jnp.take_along_axis(owner, pairs[:, :, 1], axis=1)
    left = embeds[row_a.reshape(-1)]
    right = embeds[row_b.reshape(-1)]
    piece = lax.all_gather(pref_weight, "dp", axis=1, tiled=True)
    upper = jnp.dot(left, piece[0], preferred_element_type=jnp.float32)
    lower = jnp.dot(right, piece[1], preferred_element_type=jnp.float32)
    pre = (upper + lower).reshape(prompts_dev, npairs, width_local)
    hidden = jax.nn.gelu(pre + pref_bias)
    partial_logit = jnp.sum(hidden * pref_out, axis=-1)
    logit = lax.psum(partial_logit, "tensor")
    prob = jax.nn.sigmoid(logit)
    numbers = jnp.arange(groups, dtype=jnp.int32)
    first = (pairs[:, :, 0][:, :, None] == numbers).astype(jnp.float32)
    second = (pairs[:, :, 1][:, :, None] == numbers).astype(jnp.float32)
    wins = jnp.sum(prob[:, :, None] * first + (1.0 - prob)[:, :, None] * second, axis=1)
    count = jnp.sum(first + second, axis=1)
    winrate = (wins + 1.0) / (count + 2.0)
    placed = (owner[:, :, None] == numbers).astype(jnp.float32)
    rowrate = jnp.sum(winrate[:, :, None] * placed, axis=1).reshape(-1)
    coef = 2.0 * (logratio - eta_scale * (rowrate - 0.5))
    weighted = (
        (
            features.astype(jnp.float32).reshape(resp_dev, -1, features.shape[1])
            * coef[:, None, None]
        )
        .reshape(features.shape)
        .astype(jnp.bfloat16)
    )
    piece = lax.all_gather(w_out, "dp", axis=0, tiled=True)
    block = weighted
    d_attn = jnp.dot(block, piece, preferred_element_type=jnp.float32).astype(jnp.bfloat16)
    total_resp = resp_dev * lax.axis_size("dp")
    block = weighted
    o_grad = (
        lax.psum_scatter(
            lax.dot_general(
                block, attn_out, (((0,), (0,)), ((), ())), preferred_element_type=jnp.float32
            ),
            "dp",
            scatter_dimension=0,
            tiled=True,
        )
        / total_resp
    )
    return (d_attn, o_grad)


def solution(mesh):
    return jax.shard_map(
        shards,
        mesh=mesh,
        in_specs=(
            P("dp", None),
            P("dp", None),
            P("dp", None, None),
            P(None, "dp", "tensor"),
            P("tensor"),
            P("tensor"),
            P("dp"),
            P("dp", "tensor"),
            P("dp", "tensor"),
            P("dp", "tensor"),
        ),
        out_specs=(P("dp", "tensor"), P("dp", "tensor")),
        check_vma=False,
    )
```

profile of v0, /device:TPU:96, one launch (start us, length us, event | category | flops | bytes accessed | tf_op | source)
XLA Modules:
  0.0 641.2 jit_solution(11647005601567376183)
XLA Ops:
  7.2 0.0 copy-start
  7.2 0.0 copy-start.2
  7.2 0.0 all-gather.6.cloned.1.call-start
  7.2 0.7 all-gather.6.cloned.1.call-update
  7.9 0.0 all-gather.4.cloned.1.call-start
  8.0 0.7 all-gather.4.cloned.1.call-update
  8.7 0.0 all-gather.8.cloned.1.call-start
  8.7 0.7 all-gather.8.cloned.1.call-update
  9.4 0.0 reduce-scatter.2.cloned.1.call-start
  9.5 0.8 fusion.20
  10.2 0.1 reshape.143
  10.3 2.2 gather_fusion.2
  12.5 0.1 reshape.146
  12.6 0.1 reshape.148
  12.7 2.2 gather_fusion.3
  14.9 0.1 reshape.151
  15.0 0.1 fusion.16
  15.0 0.1 reshape.102
  15.1 0.1 reshape.101
  15.2 0.0 copy-done.2
  15.2 1.2 gather_fusion.1
  16.4 0.0 copy-start.3
  16.4 0.0 copy-start.4
  16.5 1.2 gather_fusion
  17.6 0.0 copy-start.1
  17.6 0.0 copy-start.5
  17.7 168.1 %all-gather.6.cloned.1.call-done = bf16[2,4608,576]{2,1,0:T(8,128)(2,1)} async-done(((bf16[2,144,576]{2,1,0:T(8,128)(2,1)}), bf16[2,4608,576]{2,1,0:T(8,128)(2,1)}) %all-gather.6.cloned.1.call-update) | async-done | bytes 10616848 | tf_op jit(solution)/shard_map/all_gather | solution.py:23
  185.8 3.8 fusion.2
  189.5 0.0 copy-done.3
  189.6 0.0 copy-done.4
  189.6 3.9 fusion.15
  193.5 0.1 reduce_sum.39
  193.6 13.4 %psum.7 = f32[2,56]{1,0:T(2,128)S(1)} all-reduce(f32[2,56]{1,0:T(2,128)S(1)} %reduce_sum.39), channel_id=1, replica_groups=mesh['dp'=32,'tensor'=8] {'tensor'}, use_global_device_ids=true, to_apply=%region_1.0 | all-reduce | flops 112 | bytes 896 | tf_op jit(solution)/shard_map/psum | solution.py:29
  207.0 0.1 add_reduce_fusion.1
  207.1 0.0 copy-done.1
  207.1 0.1 select_reduce_fusion
  207.2 0.1 mul.106
  207.2 0.0 copy-done.5
  207.2 0.1 mul.108
  207.3 0.1 mul.109
  207.4 75.9 %all-gather.4.cloned.1.call-done = bf16[1024,4608]{0,1:T(8,128)(2,1)} async-done(((bf16[1024,576]{0,1:T(8,128)(2,1)}), bf16[1024,4608]{0,1:T(8,128)(2,1)}) %all-gather.4.cloned.1.call-update) | async-done | bytes 9437200 | tf_op jit(solution)/shard_map/all_gather | solution.py:17
  283.3 0.0 copy-done
  283.3 11.2 %fusion = f32[4608,512]{1,0:T(8,128)} fusion(bf16[1024,512]{1,0:T(8,128)(2,1)S(1)} %copy-done, bf16[1024,4608]{0,1:T(8,128)(2,1)} %all-gather.4.cloned.1.call-done, f32[1024]{0:T(1024)S(1)} %mul.109), kind=kOutput, calls=%fused_computation.5 | convolution fusion | flops 4845993984 | bytes 19927040 | tf_op jit(solution)/shard_map/dot_general | solution.py:55
  294.5 0.0 reduce-scatter.2.cloned.1.call-update
  294.6 149.2 %all-gather.8.cloned.1.call-done = bf16[4608,512]{1,0:T(8,128)(2,1)} async-done(((bf16[144,512]{1,0:T(8,128)(2,1)}), bf16[4608,512]{1,0:T(8,128)(2,1)}) %all-gather.8.cloned.1.call-update) | async-done | bytes 4718608 | tf_op jit(solution)/shard_map/all_gather | solution.py:48
  443.7 9.8 %fusion.4 = bf16[1024,512]{1,0:T(8,128)(2,1)} fusion(bf16[4608,512]{1,0:T(8,128)(2,1)} %all-gather.8.cloned.1.call-done, bf16[1024,4608]{0,1:T(8,128)(2,1)} %all-gather.4.cloned.1.call-done, f32[1024]{0:T(1024)S(1)} %mul.109), kind=kOutput, calls=%fused_computation.11 | convolution fusion | flops 4846518272 | bytes 15208448 | tf_op jit(solution)/shard_map/dot_general | solution.py:50
  453.6 179.4 %reduce-scatter.2.cloned.1.call-done = f32[144,512]{1,0:T(8,128)} async-done(((f32[4608,512]{1,0:T(8,128)}), f32[144,512]{1,0:T(8,128)}) %reduce-scatter.2.cloned.1.call-update) | async-done | bytes 294928 | tf_op jit(solution)/shard_map/reduce_scatter | solution.py:54
  633.0 1.7 broadcast_multiply_fusion
  (11 shorter events, 0.1 us)
Async XLA Ops:
  7.2 276.1 %copy-start = (bf16[1024,512]{1,0:T(8,128)(2,1)S(1)}, bf16[1024,512]{1,0:T(8,128)(2,1)}, u32[]{:S(2)}) copy-start(bf16[1024,512]{1,0:T(8,128)(2,1)} %param.19) | copy-start | bytes 3145732
  7.2 8.0 %copy-start.2 = (bf16[16,4608]{1,0:T(8,128)(2,1)S(1)}, bf16[16,4608]{1,0:T(8,128)(2,1)}, u32[]{:S(2)}) copy-start(bf16[16,4608]{1,0:T(8,128)(2,1)} %param.12) | copy-start | bytes 442372
  7.2 178.6 %all-gather.6.cloned.1.call-start = ((), (), s32[]{:S(2)}) async-start(), calls=%async_computation.2 | async-start | bytes 12165120 | tf_op jit(solution)/shard_map/all_gather | solution.py:23
  7.9 275.4 %all-gather.4.cloned.1.call-start = ((), (), s32[]{:S(2)}) async-start(), calls=%async_computation.1 | async-start | bytes 10616832 | tf_op jit(solution)/shard_map/all_gather | solution.py:17
  8.7 435.1 %all-gather.8.cloned.1.call-start = ((), (), s32[]{:S(2)}) async-start(), calls=%async_computation.3 | async-start | bytes 4866048 | tf_op jit(solution)/shard_map/all_gather | solution.py:48
  9.4 623.6 %reduce-scatter.2.cloned.1.call-start = ((), (), s32[]{:S(2)}) async-start(), calls=%async_computation.4 | async-start | bytes 9732096 | tf_op jit(solution)/shard_map/reduce_scatter | solution.py:54
  16.4 173.1 %copy-start.3 = (f32[576]{0:T(1024)S(1)}, f32[576]{0:T(1024)}, u32[]{:S(2)}) copy-start(f32[576]{0:T(1024)} %param.17) | copy-start | bytes 6916
  16.4 173.1 %copy-start.4 = (f32[576]{0:T(1024)S(1)}, f32[576]{0:T(1024)}, u32[]{:S(2)}) copy-start(f32[576]{0:T(1024)} %param.16) | copy-start | bytes 6916
  17.6 189.4 %copy-start.1 = (s32[2,8]{1,0:T(2,128)S(1)}, s32[2,8]{1,0:T(2,128)}, u32[]{:S(2)}) copy-start(s32[2,8]{1,0:T(2,128)} %param.13) | copy-start | bytes 196
  17.6 189.6 %copy-start.5 = (f32[16]{0:T(128)S(1)}, f32[16]{0:T(128)}, u32[]{:S(2)}) copy-start(f32[16]{0:T(128)} %param.18) | copy-start | bytes 196
Sparse Core Ops, SparseCore 0:
  9.8 175.9 all-gather.5
  187.6 95.6 all-gather.3
  285.1 158.6 all-gather.7
  446.2 186.7 reduce-scatter.1
where the time goes:
time: 642 us; the launch traced here: 641 us
  waiting for transfers between devices  575 us (90%)
  matrix products  28.8 us (4%)
  between operations  13.9 us (2%)
  blocking collectives  13.4 us (2%)
  local copies, waits for them, and re-layouts  8.34 us (1%)
    reduce_scatter x1, waiting for transfers between devices, shards(): lax.psum_scatter(lax.dot_general(block, attn_out, (((0,), (0,)), ((), ())...  179 us
    all_gather x1, waiting for transfers between devices, shards(): piece = lax.all_gather(pref_weight, 'dp', axis=1, tiled=True)  168 us
    all_gather x1, waiting for transfers between devices, shards(): piece = lax.all_gather(w_out, 'dp', axis=0, tiled=True)  149 us
    all_gather x1, waiting for transfers between devices, shards(): features = lax.all_gather(grad_out, 'tensor', axis=1, tiled=True)  75.9 us
    psum x1, blocking collectives, shards(): logit = lax.psum(partial_logit, 'tensor')  13.4 us
  transfers between devices with their start and end apart: 4, of which 4 were waited for; matrix products, arithmetic and copies ran while one was open for 6% of the time, Pallas kernels for 0%

commit v1 on v0

--- a/solution.py
+++ b/solution.py
@@ -14,15 +14,23 @@
     groups = owner.shape[1]
     npairs = pairs.shape[1]
     width_local = pref_weight.shape[2]
+    n_dp = lax.axis_size("dp")
     features = lax.all_gather(grad_out, "tensor", axis=1, tiled=True)
+    cols = lax.all_to_all(embeds, "dp", 1, 0, tiled=True)
+    part = jnp.concatenate(
+        [
+            jnp.dot(cols, pref_weight[0], preferred_element_type=jnp.float32),
+            jnp.dot(cols, pref_weight[1], preferred_element_type=jnp.float32),
+        ],
+        axis=1,
+    )
+    part = part.reshape(n_dp, resp_dev, part.shape[1])
+    proj = jnp.sum(lax.all_to_all(part, "dp", 0, 0, tiled=True), axis=0)
     base = (jnp.arange(prompts_dev, dtype=jnp.int32) * groups)[:, None]
     row_a = base + jnp.take_along_axis(owner, pairs[:, :, 0], axis=1)
     row_b = base + jnp.take_along_axis(owner, pairs[:, :, 1], axis=1)
-    left = embeds[row_a.reshape(-1)]
-    right = embeds[row_b.reshape(-1)]
-    piece = lax.all_gather(pref_weight, "dp", axis=1, tiled=True)
-    upper = jnp.dot(left, piece[0], preferred_element_type=jnp.float32)
-    lower = jnp.dot(right, piece[1], preferred_element_type=jnp.float32)
+    upper = proj[:, :width_local][row_a.reshape(-1)]
+    lower = proj[:, width_local:][row_b.reshape(-1)]
     pre = (upper + lower).reshape(prompts_dev, npairs, width_local)
     hidden = jax.nn.gelu(pre + pref_bias)
     partial_logit = jnp.sum(hidden * pref_out, axis=-1)
@@ -45,22 +53,16 @@
         .reshape(features.shape)
         .astype(jnp.bfloat16)
     )
-    piece = lax.all_gather(w_out, "dp", axis=0, tiled=True)
-    block = weighted
-    d_attn = jnp.dot(block, piece, preferred_element_type=jnp.float32).astype(jnp.bfloat16)
-    total_resp = resp_dev * lax.axis_size("dp")
-    block = weighted
-    o_grad = (
-        lax.psum_scatter(
-            lax.dot_general(
-                block, attn_out, (((0,), (0,)), ((), ())), preferred_element_type=jnp.float32
-            ),
-            "dp",
-            scatter_dimension=0,
-            tiled=True,
-        )
-        / total_resp
+    copies = jnp.broadcast_to(w_out[None], (n_dp,) + w_out.shape)
+    piece = lax.all_to_all(copies, "dp", 0, 0, tiled=True).reshape(-1, w_out.shape[1])
+    d_attn = jnp.dot(weighted, piece, preferred_element_type=jnp.float32).astype(jnp.bfloat16)
+    total_resp = resp_dev * n_dp
+    full = lax.dot_general(
+        weighted, attn_out, (((0,), (0,)), ((), ())), preferred_element_type=jnp.float32
     )
+    full = full.astype(jnp.bfloat16).reshape(n_dp, -1, full.shape[1])
+    shares = lax.all_to_all(full, "dp", 0, 0, tiled=True)
+    o_grad = jnp.sum(shares.astype(jnp.float32), axis=0) / total_resp
     return (d_attn, o_grad)
 
 

time: 642 us -> 300 us (0.47)
  the two profiles are of different devices: /device:TPU:96 before, /device:TPU:85 now
where the time goes in v1:
time: 300 us
  blocking collectives  160 us (53%)
  waiting for transfers between devices  58.2 us (19%)
  starting transfers between devices  26.7 us (9%)
  matrix products  23 us (8%)
  between operations  14.2 us (5%)
  local copies, waits for them, and re-layouts  12.7 us (4%)
  other arithmetic  4.65 us (2%)
    all_to_all x1, blocking collectives, shards(): proj = jnp.sum(lax.all_to_all(part, 'dp', 0, 0, tiled=True), axis=0)  96.4 us
    all_to_all x1, waiting for transfers between devices, shards(): shares = lax.all_to_all(full, 'dp', 0, 0, tiled=True)  57.5 us
    psum x1, blocking collectives, shards(): logit = lax.psum(partial_logit, 'tensor')  51.7 us
    all_to_all x1, starting transfers between devices, shards(): shares = lax.all_to_all(full, 'dp', 0, 0, tiled=True)  18.7 us
    all_to_all x1, blocking collectives, shards(): cols = lax.all_to_all(embeds, 'dp', 1, 0, tiled=True)  12.3 us
    dot_general x1, matrix products, shards(): lax.dot_general(weighted, attn_out, (((0,), (0,)), ((), ())), preferred_e...  10.5 us
    dot_general x1, matrix products, shards(): jnp.dot(weighted, piece, preferred_element_type=jnp.float32)  9.86 us
    all_to_all x1, starting transfers between devices, shards(): lax.all_to_all(copies, 'dp', 0, 0, tiled=True).reshape(-1, w_out.shape[1])  7.94 us
  transfers between devices with their start and end apart: 3, of which 1 were waited for; matrix products, arithmetic and copies ran while one was open for 12% of the time, Pallas kernels for 0%

profile of v1, /device:TPU:85, one launch (start us, length us, event | category | flops | bytes accessed | tf_op | source)
XLA Modules:
  0.0 299.8 jit_solution(8687693406414650)
XLA Ops:
  7.2 0.0 copy-start
  7.2 0.0 all-gather.2.cloned.1.call-start
  7.2 0.7 all-gather.2.cloned.1.call-update
  7.9 1.3 all_to_all.23
  9.2 0.2 copy.14
  9.4 12.3 %all_to_all.34 = bf16[16,32,144]{2,0,1:T(8,128)(2,1)S(1)} all-to-all(bf16[16,32,144]{2,0,1:T(8,128)(2,1)S(1)} %copy.14), channel_id=1, replica_groups=mesh['dp'=32,'tensor'=8] {'dp'}, dimensions={1} | all-to-all | bytes 294912 | tf_op jit(solution)/shard_map/all_to_all | solution.py:19
  21.7 1.3 fusion.13
  23.0 1.4 fusion.15
  24.4 0.2 pad_maximum_fusion
  24.6 2.0 copy.15
  26.6 96.4 %all_to_all.35 = f32[32,16,1152]{2,1,0:T(8,128)S(1)} all-to-all(f32[32,16,1152]{2,1,0:T(8,128)} %bitcast.30), channel_id=1, replica_groups=mesh['dp'=32,'tensor'=8] {'dp'}, dimensions={0} | all-to-all | bytes 4718592 | tf_op jit(solution)/shard_map/all_to_all | solution.py:28
  123.0 0.0 copy-done.2
  123.0 2.7 broadcast_in_dim.5
  125.7 7.9 %all-to-all-start.2 = ((bf16[32,144,512]{2,1,0:T(8,128)(2,1)}), bf16[32,144,512]{2,1,0:T(8,128)(2,1)}, u32[]{:S(2)}, u32[]{:S(2)}) async-start(bf16[32,144,512]{2,1,0:T(8,128)(2,1)} %broadcast_in_dim.5), calls=%async_computation.2 | async-start | bytes 9437184 | tf_op jit(solution)/shard_map/all_to_all | solution.py:57
  133.7 0.0 copy-done.5
  133.7 0.1 reshape.166
  133.8 0.0 copy-done.1
  133.8 2.0 gather_fusion.3
  135.8 0.0 copy-start.3
  135.8 0.0 copy-start.4
  135.8 0.1 reshape.169
  135.9 0.1 reshape.161
  136.0 2.0 gather_fusion.2
  138.1 0.1 reshape.164
  138.1 0.1 fusion.20
  138.2 0.1 reshape.117
  138.3 0.1 reshape.118
  138.4 0.1 reduce_sum.56
  138.5 0.1 fusion.23
  138.6 0.8 gather_fusion
  139.4 0.8 gather_fusion.1
  140.2 0.0 copy-done.3
  140.2 0.0 copy-done.4
  140.2 0.2 fusion.12
  140.4 0.1 reduce_sum.58
  140.5 51.7 %psum.7 = f32[2,56]{1,0:T(2,128)S(1)} all-reduce(f32[2,56]{1,0:T(2,128)S(1)} %reduce_sum.58), channel_id=1, replica_groups=mesh['dp'=32,'tensor'=8] {'tensor'}, use_global_device_ids=true, to_apply=%region_2.0 | all-reduce | flops 112 | bytes 896 | tf_op jit(solution)/shard_map/psum | solution.py:37
  192.2 0.1 add_reduce_fusion.1
  192.3 0.1 select_reduce_fusion
  192.4 0.1 mul.106
  192.5 0.1 mul.108
  192.6 0.1 mul.109
  192.6 10.5 %fusion.2 = bf16[4608,512]{1,0:T(8,128)(2,1)} fusion(bf16[1024,512]{1,0:T(8,128)(2,1)S(1)} %copy-done, bf16[1024,4608]{0,1:T(8,128)(2,1)} %all-gather.2.cloned.1.call-done, f32[1024]{0:T(1024)S(1)} %mul.109), kind=kOutput, calls=%fused_computation.8 | convolution fusion | flops 4848353280 | bytes 15208448 | tf_op jit(solution)/shard_map/dot_general | solution.py:60
  203.1 0.0 all-to-all-done.2
  203.1 18.7 %all-to-all-start.3 = ((bf16[32,144,512]{2,1,0:T(8,128)(2,1)}), bf16[32,144,512]{2,1,0:T(8,128)(2,1)}, u32[]{:S(2)}, u32[]{:S(2)}) async-start(bf16[32,144,512]{2,1,0:T(8,128)(2,1)} %bitcast.31), calls=%async_computation.3 | async-start | bytes 9437184 | tf_op jit(solution)/shard_map/all_to_all | solution.py:64
  221.8 9.9 %fusion.3 = bf16[1024,512]{1,0:T(8,128)(2,1)} fusion(bf16[4608,512]{1,0:T(8,128)(2,1)} %bitcast.12, bf16[1024,4608]{0,1:T(8,128)(2,1)} %all-gather.2.cloned.1.call-done, f32[1024]{0:T(1024)S(1)} %mul.109), kind=kOutput, calls=%fused_computation.10 | convolution fusion | flops 4846518272 | bytes 15208448 | tf_op jit(solution)/shard_map/dot_general | solution.py:58
  231.7 57.5 %all-to-all-done.3 = bf16[32,144,512]{2,1,0:T(8,128)(2,1)} async-done(((bf16[32,144,512]{2,1,0:T(8,128)(2,1)}), bf16[32,144,512]{2,1,0:T(8,128)(2,1)}, u32[]{:S(2)}, u32[]{:S(2)}) %all-to-all-start.3) | async-done | bytes 4718624 | tf_op jit(solution)/shard_map/all_to_all | solution.py:64
  289.2 3.0 %convert_reduce_fusion = f32[144,512]{1,0:T(8,128)S(1)} fusion(bf16[32,144,512]{2,1,0:T(8,128)(2,1)} %all-to-all-done.3), kind=kLoop, calls=%fused_computation.5 | loop fusion | flops 4644864 | bytes 5013504 | tf_op jit(solution)/shard_map/reduce_sum | solution.py:65
  292.2 0.7 broadcast_multiply_fusion
  (19 shorter events, 0.1 us)
Async XLA Ops:
  7.2 185.5 %copy-start = (bf16[1024,512]{1,0:T(8,128)(2,1)S(1)}, bf16[1024,512]{1,0:T(8,128)(2,1)}, u32[]{:S(2)}) copy-start(bf16[1024,512]{1,0:T(8,128)(2,1)} %param.19) | copy-start | bytes 3145732
  7.2 185.5 %all-gather.2.cloned.1.call-start = ((), (), s32[]{:S(2)}) async-start(), calls=%async_computation.4 | async-start | bytes 10616832 | tf_op jit(solution)/shard_map/all_gather | solution.py:18
  26.6 96.4 %copy-start.2 = (bf16[144,512]{1,0:T(8,128)(2,1)S(1)}, bf16[144,512]{1,0:T(8,128)(2,1)}, u32[]{:S(2)}) copy-start(bf16[144,512]{1,0:T(8,128)(2,1)} %param.21) | copy-start | bytes 442372
  125.7 8.0 %copy-start.5 = (s32[2,56,2]{1,2,0:T(2,128)S(1)}, s32[2,56,2]{1,2,0:T(2,128)}, u32[]{:S(2)}) copy-start(s32[2,56,2]{1,2,0:T(2,128)} %param.14) | copy-start | bytes 2692
  125.7 8.1 %copy-start.1 = (s32[2,8]{1,0:T(2,128)S(1)}, s32[2,8]{1,0:T(2,128)}, u32[]{:S(2)}) copy-start(s32[2,8]{1,0:T(2,128)} %param.13) | copy-start | bytes 196
  125.7 77.4 %all-to-all-start.2 = ((bf16[32,144,512]{2,1,0:T(8,128)(2,1)}), bf16[32,144,512]{2,1,0:T(8,128)(2,1)}, u32[]{:S(2)}, u32[]{:S(2)}) async-start(bf16[32,144,512]{2,1,0:T(8,128)(2,1)} %broadcast_in_dim.5), calls=%async_computation.2 | async-start | bytes 9437184 | tf_op jit(solution)/shard_map/all_to_all | solution.py:57
  135.8 4.4 %copy-start.3 = (f32[576]{0:T(1024)S(1)}, f32[576]{0:T(1024)}, u32[]{:S(2)}) copy-start(f32[576]{0:T(1024)} %param.17) | copy-start | bytes 6916
  135.8 4.4 %copy-start.4 = (f32[576]{0:T(1024)S(1)}, f32[576]{0:T(1024)}, u32[]{:S(2)}) copy-start(f32[576]{0:T(1024)} %param.16) | copy-start | bytes 6916
  136.0 56.5 %copy-start.6 = (f32[16]{0:T(128)S(1)}, f32[16]{0:T(128)}, u32[]{:S(2)}) copy-start(f32[16]{0:T(128)} %param.18) | copy-start | bytes 196
  203.1 86.1 %all-to-all-start.3 = ((bf16[32,144,512]{2,1,0:T(8,128)(2,1)}), bf16[32,144,512]{2,1,0:T(8,128)(2,1)}, u32[]{:S(2)}, u32[]{:S(2)}) async-start(bf16[32,144,512]{2,1,0:T(8,128)(2,1)} %bitcast.31), calls=%async_computation.3 | async-start | bytes 9437184 | tf_op jit(solution)/shard_map/all_to_all | solution.py:64
Sparse Core Ops, SparseCore 0:
  9.8 119.9 all-gather.1

commit v2 on v1

v2 whole, which is shorter than its diff:
```python
import jax
import jax.numpy as jnp
from jax import lax
from jax.sharding import Mesh
from jax.sharding import PartitionSpec as P

eta_scale = 2.0

DP = ("zl", "y", "x")
TP = ("zh", "c")
PLANE = ("y", "x")


def shards(
    embeds, owner, pairs, pref_weight, pref_bias, pref_out, logratio, attn_out, grad_out, w_out
):
    resp_dev = embeds.shape[0]
    prompts_dev = owner.shape[0]
    groups = owner.shape[1]
    npairs = pairs.shape[1]
    width_local = pref_weight.shape[2]
    rows_w = pref_weight.shape[1]
    n_dp = lax.axis_size(DP)
    n_zl = lax.axis_size("zl")
    n_plane = lax.axis_size(PLANE)
    features = lax.all_gather(grad_out, TP, axis=1, tiled=True)
    copies = jnp.broadcast_to(w_out[None], (n_dp,) + w_out.shape)
    piece = lax.all_to_all(copies, DP, 0, 0, tiled=True).reshape(-1, w_out.shape[1])

    zl = lax.axis_index("zl")
    other = lax.ppermute(pref_weight, "zl", [(k, (k + 1) % n_zl) for k in range(n_zl)])
    pair_w = jnp.where(
        zl == 0,
        jnp.concatenate([pref_weight, other], axis=1),
        jnp.concatenate([other, pref_weight], axis=1),
    )
    cols = embeds.reshape(resp_dev, n_zl, n_plane, rows_w).transpose(2, 0, 1, 3)
    cols = lax.all_to_all(cols, PLANE, 0, 0, tiled=True).reshape(n_plane * resp_dev, n_zl * rows_w)
    part = jnp.concatenate(
        [
            jnp.dot(cols, pair_w[0], preferred_element_type=jnp.float32),
            jnp.dot(cols, pair_w[1], preferred_element_type=jnp.float32),
        ],
        axis=1,
    )
    part = part.reshape(n_plane, resp_dev, part.shape[1])
    proj = jnp.sum(lax.all_to_all(part, PLANE, 0, 0, tiled=True), axis=0)

    base = (jnp.arange(prompts_dev, dtype=jnp.int32) * groups)[:, None]
    row_a = base + jnp.take_along_axis(owner, pairs[:, :, 0], axis=1)
    row_b = base + jnp.take_along_axis(owner, pairs[:, :, 1], axis=1)
    upper = proj[:, :width_local][row_a.reshape(-1)]
    lower = proj[:, width_local:][row_b.reshape(-1)]
    pre = (upper + lower).reshape(prompts_dev, npairs, width_local)
    hidden = jax.nn.gelu(pre + pref_bias)
    partial_logit = jnp.sum(hidden * pref_out, axis=-1)
    logit = lax.psum(partial_logit, TP)
    prob = jax.nn.sigmoid(logit)
    numbers = jnp.arange(groups, dtype=jnp.int32)
    first = (pairs[:, :, 0][:, :, None] == numbers).astype(jnp.float32)
    second = (pairs[:, :, 1][:, :, None] == numbers).astype(jnp.float32)
    wins = jnp.sum(prob[:, :, None] * first + (1.0 - prob)[:, :, None] * second, axis=1)
    count = jnp.sum(first + second, axis=1)
    winrate = (wins + 1.0) / (count + 2.0)
    placed = (owner[:, :, None] == numbers).astype(jnp.float32)
    rowrate = jnp.sum(winrate[:, :, None] * placed, axis=1).reshape(-1)
    coef = 2.0 * (logratio - eta_scale * (rowrate - 0.5))
    weighted = (
        (
            features.astype(jnp.float32).reshape(resp_dev, -1, features.shape[1])
            * coef[:, None, None]
        )
        .reshape(features.shape)
        .astype(jnp.bfloat16)
    )
    total_resp = resp_dev * n_dp
    full = lax.dot_general(
        weighted, attn_out, (((0,), (0,)), ((), ())), preferred_element_type=jnp.float32
    )
    full = full.astype(jnp.bfloat16).reshape(n_dp, -1, full.shape[1])
    shares = lax.all_to_all(full, DP, 0, 0, tiled=True)
    d_attn = jnp.dot(weighted, piece, preferred_element_type=jnp.float32).astype(jnp.bfloat16)
    o_grad = jnp.sum(shares.astype(jnp.float32), axis=0) / total_resp
    return (d_attn, o_grad)


def solution(mesh):
    n_zl = 2
    fine = Mesh(
        mesh.devices.reshape(
            n_zl, mesh.shape["dp"] // (n_zl * 4), 4, mesh.shape["tensor"] // 2, 2
        ),
        ("zl", "y", "x", "zh", "c"),
    )
    return jax.shard_map(
        shards,
        mesh=fine,
        in_specs=(
            P(DP, None),
            P(DP, None),
            P(DP, None, None),
            P(None, DP, TP),
            P(TP),
            P(TP),
            P(DP),
            P(DP, TP),
            P(DP, TP),
            P(DP, TP),
        ),
        out_specs=(P(DP, TP), P(DP, TP)),
        check_vma=False,
    )
```

time: 300 us -> 272 us (0.907)
  the two profiles are of different devices: /device:TPU:85 before, /device:TPU:96 now
where the time goes in v2:
time: 272 us; the launch traced here: 271 us
  blocking collectives  118 us (43%)
  waiting for transfers between devices  74.3 us (27%)
  starting transfers between devices  24.3 us (9%)
  matrix products  21 us (8%)
  between operations  14.2 us (5%)
  local copies, waits for them, and re-layouts  12.9 us (5%)
  other arithmetic  5.85 us (2%)
    psum x1, blocking collectives, shards(): logit = lax.psum(partial_logit, TP)  97.4 us
    all_to_all x1, waiting for transfers between devices, shards(): shares = lax.all_to_all(full, DP, 0, 0, tiled=True)  65 us
    all_to_all x1, blocking collectives, shards(): proj = jnp.sum(lax.all_to_all(part, PLANE, 0, 0, tiled=True), axis=0)  20.5 us
    all_to_all x1, starting transfers between devices, shards(): shares = lax.all_to_all(full, DP, 0, 0, tiled=True)  10.5 us
    dot_general x1, matrix products, shards(): lax.dot_general(weighted, attn_out, (((0,), (0,)), ((), ())), preferred_e...  10.5 us
    dot_general x1, matrix products, shards(): jnp.dot(weighted, piece, preferred_element_type=jnp.float32)  9.86 us
    all_to_all x1, waiting for transfers between devices, shards(): lax.all_to_all(cols, PLANE, 0, 0, tiled=True)  8.69 us
    all_to_all x1, starting transfers between devices, shards(): lax.all_to_all(cols, PLANE, 0, 0, tiled=True)  7.03 us
  transfers between devices with their start and end apart: 5, of which 2 were waited for; matrix products, arithmetic and copies ran while one was open for 13% of the time, Pallas kernels for 0%

profile of v2, /device:TPU:96, one launch (start us, length us, event | category | flops | bytes accessed | tf_op | source)
XLA Modules:
  0.0 270.6 jit_solution(1768910867197362661)
XLA Ops:
  7.2 0.0 copy-start
  7.2 0.0 all-gather.2.cloned.1.call-start
  7.2 0.7 all-gather.2.cloned.1.call-update
  7.9 0.2 collective-permute-start
  8.1 1.3 reshape.119
  9.4 0.9 copy.17
  10.4 7.0 %all-to-all-start = ((bf16[16,16,2,144]{3,2,1,0:T(2,128)(2,1)}), bf16[16,16,2,144]{3,2,1,0:T(2,128)(2,1)S(1)}, u32[]{:S(2)}, u32[]{:S(2)}) async-start(bf16[16,16,2,144]{3,2,1,0:T(2,128)(2,1)} %bitcast.33), calls=%async_computation | async-start | bytes 524288 | tf_op jit(solution)/shard_map/all_to_all | solution.py:38
  17.4 8.7 %all-to-all-done = bf16[16,16,2,144]{3,2,1,0:T(2,128)(2,1)S(1)} async-done(((bf16[16,16,2,144]{3,2,1,0:T(2,128)(2,1)}), bf16[16,16,2,144]{3,2,1,0:T(2,128)(2,1)S(1)}, u32[]{:S(2)}, u32[]{:S(2)}) %all-to-all-start) | async-done | bytes 147488 | tf_op jit(solution)/shard_map/all_to_all | solution.py:38
  26.1 0.2 reshape.120
  26.3 0.0 collective-permute-done
  26.3 1.4 maximum_select_fusion
  27.7 0.4 convolution_bitcast_fusion
  28.0 0.4 convolution_bitcast_fusion.1
  28.4 0.1 pad_maximum_fusion
  28.5 0.4 copy.15
  28.9 20.5 %all_to_all.20 = f32[16,16,1152]{2,1,0:T(8,128)S(1)} all-to-all(f32[16,16,1152]{2,1,0:T(8,128)S(1)} %bitcast.35), channel_id=1, replica_groups=mesh['zl'=2,'y'=4,'x'=4,'zh'=4,'c'=2] {'y','x'}, dimensions={0} | all-to-all | bytes 2359296 | tf_op jit(solution)/shard_map/all_to_all | solution.py:47
  49.4 3.6 %broadcast_in_dim.4 = bf16[32,144,512]{2,1,0:T(8,128)(2,1)} broadcast(bf16[144,512]{1,0:T(8,128)(2,1)} %param.21), dimensions={1,2} | broadcast | bytes 4866048 | tf_op jit(solution)/shard_map/broadcast_in_dim | solution.py:27
  53.0 6.5 %all-to-all-start.2 = ((bf16[32,144,512]{2,1,0:T(8,128)(2,1)}), bf16[32,144,512]{2,1,0:T(8,128)(2,1)}, u32[]{:S(2)}, u32[]{:S(2)}) async-start(bf16[32,144,512]{2,1,0:T(8,128)(2,1)} %broadcast_in_dim.4), calls=%async_computation.2 | async-start | bytes 9437184 | tf_op jit(solution)/shard_map/all_to_all | solution.py:28
  59.5 0.0 copy-start.2
  59.5 0.0 copy-start.3
  59.5 0.1 reshape.171
  59.6 2.0 gather_fusion.3
  61.6 0.1 reshape.174
  61.7 0.1 reshape.166
  61.8 2.0 gather_fusion.2
  63.8 0.1 reshape.169
  63.9 0.1 fusion.14
  64.0 0.1 reshape.122
  64.1 0.1 reshape.123
  64.2 0.1 reduce_sum.56
  64.3 0.1 fusion.17
  64.4 0.8 gather_fusion
  65.1 0.8 gather_fusion.1
  65.9 0.2 fusion.12
  66.2 0.1 reduce_sum.58
  66.3 97.4 %psum.7 = f32[2,56]{1,0:T(2,128)S(1)} all-reduce(f32[2,56]{1,0:T(2,128)S(1)} %reduce_sum.58), channel_id=1, replica_groups=mesh['zl'=2,'y'=4,'x'=4,'zh'=4,'c'=2] {'zh','c'}, use_global_device_ids=true, to_apply=%region_2.4 | all-reduce | flops 112 | bytes 896 | tf_op jit(solution)/shard_map/psum | solution.py:57
  163.7 0.1 add_reduce_fusion.1
  163.8 0.1 select_reduce_fusion
  163.9 0.1 mul.106
  164.0 0.1 mul.108
  164.1 0.1 mul.109
  164.1 10.5 %fusion.2 = bf16[4608,512]{1,0:T(8,128)(2,1)} fusion(bf16[1024,512]{1,0:T(8,128)(2,1)S(1)} %copy-done, bf16[1024,4608]{0,1:T(8,128)(2,1)} %all-gather.2.cloned.1.call-done, f32[1024]{0:T(1024)S(1)} %mul.109), kind=kOutput, calls=%fused_computation.8 | convolution fusion | flops 4848353280 | bytes 15208448 | tf_op jit(solution)/shard_map/dot_general | solution.py:77
  174.6 0.0 all-to-all-done.2
  174.6 10.5 %all-to-all-start.3 = ((bf16[32,144,512]{2,1,0:T(8,128)(2,1)}), bf16[32,144,512]{2,1,0:T(8,128)(2,1)}, u32[]{:S(2)}, u32[]{:S(2)}) async-start(bf16[32,144,512]{2,1,0:T(8,128)(2,1)} %bitcast.34), calls=%async_computation.3 | async-start | bytes 9437184 | tf_op jit(solution)/shard_map/all_to_all | solution.py:81
  185.2 9.9 %fusion.3 = bf16[1024,512]{1,0:T(8,128)(2,1)} fusion(bf16[4608,512]{1,0:T(8,128)(2,1)} %bitcast.12, bf16[1024,4608]{0,1:T(8,128)(2,1)} %all-gather.2.cloned.1.call-done, f32[1024]{0:T(1024)S(1)} %mul.109), kind=kOutput, calls=%fused_computation.9 | convolution fusion | flops 4846518272 | bytes 15208448 | tf_op jit(solution)/shard_map/dot_general | solution.py:82
  195.0 65.0 %all-to-all-done.3 = bf16[32,144,512]{2,1,0:T(8,128)(2,1)} async-done(((bf16[32,144,512]{2,1,0:T(8,128)(2,1)}), bf16[32,144,512]{2,1,0:T(8,128)(2,1)}, u32[]{:S(2)}, u32[]{:S(2)}) %all-to-all-start.3) | async-done | bytes 4718624 | tf_op jit(solution)/shard_map/all_to_all | solution.py:81
  260.0 3.0 %convert_reduce_fusion = f32[144,512]{1,0:T(8,128)S(1)} fusion(bf16[32,144,512]{2,1,0:T(8,128)(2,1)} %all-to-all-done.3), kind=kLoop, calls=%fused_computation.5 | loop fusion | flops 4644864 | bytes 5013504 | tf_op jit(solution)/shard_map/reduce_sum | solution.py:83
  263.0 0.7 broadcast_multiply_fusion
  (22 shorter events, 0.1 us)
Async XLA Ops:
  7.2 157.0 %copy-start = (bf16[1024,512]{1,0:T(8,128)(2,1)S(1)}, bf16[1024,512]{1,0:T(8,128)(2,1)}, u32[]{:S(2)}) copy-start(bf16[1024,512]{1,0:T(8,128)(2,1)} %param.19) | copy-start | bytes 3145732
  7.2 156.9 %all-gather.2.cloned.1.call-start = ((), (), s32[]{:S(2)}) async-start(), calls=%async_computation.4 | async-start | bytes 10616832 | tf_op jit(solution)/shard_map/all_gather | solution.py:26
  7.9 18.4 %collective-permute-start = (bf16[2,144,576]{2,1,0:T(8,128)(2,1)}, bf16[2,144,576]{2,1,0:T(8,128)(2,1)S(1)}, u32[]{:S(2)}, u32[]{:S(2)}) collective-permute-start(bf16[2,144,576]{2,1,0:T(8,128)(2,1)} %param.15), channel_id=1, source_target_pairs={{0,128},{128,0},{1,129},{129,1},{2,130},{130,2},{3,131},{131,3},{4... | collective-permute-start | bytes 995336 | tf_op jit(solution)/shard_map/ppermute | solution.py:31
  10.4 15.7 %all-to-all-start = ((bf16[16,16,2,144]{3,2,1,0:T(2,128)(2,1)}), bf16[16,16,2,144]{3,2,1,0:T(2,128)(2,1)S(1)}, u32[]{:S(2)}, u32[]{:S(2)}) async-start(bf16[16,16,2,144]{3,2,1,0:T(2,128)(2,1)} %bitcast.33), calls=%async_computation | async-start | bytes 524288 | tf_op jit(solution)/shard_map/all_to_all | solution.py:38
  52.9 6.5 %copy-start.4 = (s32[2,56,2]{1,2,0:T(2,128)S(1)}, s32[2,56,2]{1,2,0:T(2,128)}, u32[]{:S(2)}) copy-start(s32[2,56,2]{1,2,0:T(2,128)} %param.14) | copy-start | bytes 2692
  53.0 6.7 %copy-start.1 = (s32[2,8]{1,0:T(2,128)S(1)}, s32[2,8]{1,0:T(2,128)}, u32[]{:S(2)}) copy-start(s32[2,8]{1,0:T(2,128)} %param.13) | copy-start | bytes 196
  53.0 121.6 %all-to-all-start.2 = ((bf16[32,144,512]{2,1,0:T(8,128)(2,1)}), bf16[32,144,512]{2,1,0:T(8,128)(2,1)}, u32[]{:S(2)}, u32[]{:S(2)}) async-start(bf16[32,144,512]{2,1,0:T(8,128)(2,1)} %broadcast_in_dim.4), calls=%async_computation.2 | async-start | bytes 9437184 | tf_op jit(solution)/shard_map/all_to_all | solution.py:28
  59.5 6.5 %copy-start.2 = (f32[576]{0:T(1024)S(1)}, f32[576]{0:T(1024)}, u32[]{:S(2)}) copy-start(f32[576]{0:T(1024)} %param.17) | copy-start | bytes 6916
  59.5 6.5 %copy-start.3 = (f32[576]{0:T(1024)S(1)}, f32[576]{0:T(1024)}, u32[]{:S(2)}) copy-start(f32[576]{0:T(1024)} %param.16) | copy-start | bytes 6916
  59.6 104.4 %copy-start.5 = (f32[16]{0:T(128)S(1)}, f32[16]{0:T(128)}, u32[]{:S(2)}) copy-start(f32[16]{0:T(128)} %param.18) | copy-start | bytes 196
  174.6 85.4 %all-to-all-start.3 = ((bf16[32,144,512]{2,1,0:T(8,128)(2,1)}), bf16[32,144,512]{2,1,0:T(8,128)(2,1)}, u32[]{:S(2)}, u32[]{:S(2)}) async-start(bf16[32,144,512]{2,1,0:T(8,128)(2,1)} %bitcast.34), calls=%async_computation.3 | async-start | bytes 9437184 | tf_op jit(solution)/shard_map/all_to_all | solution.py:81
Sparse Core Ops, SparseCore 0:
  9.8 116.5 all-gather.1

commit v3 on v2

--- a/solution.py
+++ b/solution.py
@@ -24,8 +24,6 @@
     n_zl = lax.axis_size("zl")
     n_plane = lax.axis_size(PLANE)
     features = lax.all_gather(grad_out, TP, axis=1, tiled=True)
-    copies = jnp.broadcast_to(w_out[None], (n_dp,) + w_out.shape)
-    piece = lax.all_to_all(copies, DP, 0, 0, tiled=True).reshape(-1, w_out.shape[1])
 
     zl = lax.axis_index("zl")
     other = lax.ppermute(pref_weight, "zl", [(k, (k + 1) % n_zl) for k in range(n_zl)])
@@ -55,6 +53,9 @@
     hidden = jax.nn.gelu(pre + pref_bias)
     partial_logit = jnp.sum(hidden * pref_out, axis=-1)
     logit = lax.psum(partial_logit, TP)
+    copies = jnp.broadcast_to(w_out[None], (n_dp,) + w_out.shape)
+    copies, logit = lax.optimization_barrier((copies, logit))
+    piece = lax.all_to_all(copies, DP, 0, 0, tiled=True).reshape(-1, w_out.shape[1])
     prob = jax.nn.sigmoid(logit)
     numbers = jnp.arange(groups, dtype=jnp.int32)
     first = (pairs[:, :, 0][:, :, None] == numbers).astype(jnp.float32)

time: 272 us -> 280 us (1.029)
  the two profiles are of different devices: /device:TPU:96 before, /device:TPU:84 now
where the time goes in v3:
time: 280 us
  waiting for transfers between devices  148 us (53%)
  starting transfers between devices  56.3 us (20%)
  matrix products  21.1 us (8%)
  blocking collectives  20.9 us (7%)
  between operations  14.2 us (5%)
  local copies, waits for them, and re-layouts  13.8 us (5%)
  other arithmetic  5.78 us (2%)
    all_to_all x1, waiting for transfers between devices, shards(): lax.all_to_all(copies, DP, 0, 0, tiled=True).reshape(-1, w_out.shape[1])  66.3 us
    all_to_all x1, waiting for transfers between devices, shards(): shares = lax.all_to_all(full, DP, 0, 0, tiled=True)  58.2 us
    all_to_all x1, starting transfers between devices, shards(): lax.all_to_all(copies, DP, 0, 0, tiled=True).reshape(-1, w_out.shape[1])  24.4 us
    psum x1, blocking collectives, shards(): logit = lax.psum(partial_logit, TP)  20.9 us
    ppermute x1, waiting for transfers between devices, shards(): lax.ppermute(pref_weight, 'zl', [(k, (k + 1) % n_zl) for k in range(n_zl)])  15.7 us
    all_to_all x1, starting transfers between devices, shards(): proj = jnp.sum(lax.all_to_all(part, PLANE, 0, 0, tiled=True), axis=0)  15.3 us
    dot_general x1, matrix products, shards(): lax.dot_general(weighted, attn_out, (((0,), (0,)), ((), ())), preferred_e...  10.5 us
    dot_general x1, matrix products, shards(): jnp.dot(weighted, piece, preferred_element_type=jnp.float32)  9.86 us
  transfers between devices with their start and end apart: 6, of which 5 were waited for; matrix products, arithmetic and copies ran while one was open for 13% of the time, Pallas kernels for 0%

profile of v3, /device:TPU:84, one launch (start us, length us, event | category | flops | bytes accessed | tf_op | source)
XLA Modules:
  0.0 279.9 jit_solution(9416793560332465723)
XLA Ops:
  7.2 0.0 copy-start
  7.2 0.0 all-gather.2.cloned.1.call-start
  7.2 0.7 all-gather.2.cloned.1.call-update
  7.9 1.3 reshape.119
  9.2 0.9 copy.17
  10.2 7.2 %all-to-all-start = ((bf16[16,16,2,144]{3,2,1,0:T(2,128)(2,1)}), bf16[16,16,2,144]{3,2,1,0:T(2,128)(2,1)S(1)}, u32[]{:S(2)}, u32[]{:S(2)}) async-start(bf16[16,16,2,144]{3,2,1,0:T(2,128)(2,1)} %bitcast.33), calls=%async_computation | async-start | bytes 524288 | tf_op jit(solution)/shard_map/all_to_all | solution.py:36
  17.4 1.9 collective-permute-start
  19.3 0.8 fusion.18
  20.1 1.9 all-to-all-done
  22.0 0.2 reshape.120
  22.1 15.7 %collective-permute-done = bf16[2,144,576]{2,1,0:T(8,128)(2,1)S(1)} collective-permute-done((bf16[2,144,576]{2,1,0:T(8,128)(2,1)}, bf16[2,144,576]{2,1,0:T(8,128)(2,1)S(1)}, u32[]{:S(2)}, u32[]{:S(2)}) %collective-permute-start) | collective-permute-done | bytes 331808 | tf_op jit(solution)/shard_map/ppermute | solution.py:29
  37.8 1.3 maximum_select_fusion
  39.1 0.4 convolution_bitcast_fusion
  39.5 0.4 convolution_bitcast_fusion.1
  39.9 0.1 pad_maximum_fusion
  39.9 1.4 copy.15
  41.3 15.3 %all-to-all-start.1 = ((f32[16,16,1152]{2,1,0:T(8,128)}), f32[16,16,1152]{2,1,0:T(8,128)S(1)}, u32[]{:S(2)}, u32[]{:S(2)}) async-start(f32[16,16,1152]{2,1,0:T(8,128)} %bitcast.6), calls=%async_computation.1 | async-start | bytes 2359296 | tf_op jit(solution)/shard_map/all_to_all | solution.py:45
  56.7 0.1 reshape.171
  56.7 2.0 gather_fusion.3
  58.8 0.1 reshape.174
  58.8 0.1 reshape.166
  58.9 2.0 gather_fusion.2
  61.0 0.1 reshape.169
  61.0 0.1 fusion.14
  61.1 0.1 reshape.122
  61.2 0.1 reshape.123
  61.3 5.2 %all-to-all-done.1 = f32[16,16,1152]{2,1,0:T(8,128)S(1)} async-done(((f32[16,16,1152]{2,1,0:T(8,128)}), f32[16,16,1152]{2,1,0:T(8,128)S(1)}, u32[]{:S(2)}, u32[]{:S(2)}) %all-to-all-start.1) | async-done | bytes 1179680 | tf_op jit(solution)/shard_map/all_to_all | solution.py:45
  66.5 0.1 reduce_sum.56
  66.6 0.1 fusion.17
  66.6 0.8 gather_fusion
  67.4 0.8 gather_fusion.1
  68.2 0.2 fusion.12
  68.4 0.1 reduce_sum.58
  68.5 20.9 %psum.7 = f32[2,56]{1,0:T(2,128)S(1)} all-reduce(f32[2,56]{1,0:T(2,128)S(1)} %reduce_sum.58), channel_id=1, replica_groups=mesh['zl'=2,'y'=4,'x'=4,'zh'=4,'c'=2] {'zh','c'}, use_global_device_ids=true, to_apply=%region_2.4 | all-reduce | flops 112 | bytes 896 | tf_op jit(solution)/shard_map/psum | solution.py:55
  89.5 2.7 broadcast_in_dim.5
  92.2 24.4 %all-to-all-start.2 = ((bf16[32,144,512]{2,1,0:T(8,128)(2,1)}), bf16[32,144,512]{2,1,0:T(8,128)(2,1)}, u32[]{:S(2)}, u32[]{:S(2)}) async-start(bf16[32,144,512]{2,1,0:T(8,128)(2,1)} %broadcast_in_dim.5), calls=%async_computation.2 | async-start | bytes 9437184 | tf_op jit(solution)/shard_map/all_to_all | solution.py:58
  116.6 0.1 add_reduce_fusion.1
  116.7 0.1 select_reduce_fusion
  116.8 0.1 mul.106
  116.9 0.1 mul.108
  116.9 0.1 mul.109
  117.0 10.5 %fusion.2 = bf16[4608,512]{1,0:T(8,128)(2,1)} fusion(bf16[1024,512]{1,0:T(8,128)(2,1)S(1)} %copy-done, bf16[1024,4608]{0,1:T(8,128)(2,1)} %all-gather.2.cloned.1.call-done, f32[1024]{0:T(1024)S(1)} %mul.109), kind=kOutput, calls=%fused_computation.8 | convolution fusion | flops 4848353280 | bytes 15208448 | tf_op jit(solution)/shard_map/dot_general | solution.py:78
  127.5 66.3 %all-to-all-done.2 = bf16[32,144,512]{2,1,0:T(8,128)(2,1)} async-done(((bf16[32,144,512]{2,1,0:T(8,128)(2,1)}), bf16[32,144,512]{2,1,0:T(8,128)(2,1)}, u32[]{:S(2)}, u32[]{:S(2)}) %all-to-all-start.2) | async-done | bytes 4718624 | tf_op jit(solution)/shard_map/all_to_all | solution.py:58
  193.8 7.4 %all-to-all-start.3 = ((bf16[32,144,512]{2,1,0:T(8,128)(2,1)}), bf16[32,144,512]{2,1,0:T(8,128)(2,1)}, u32[]{:S(2)}, u32[]{:S(2)}) async-start(bf16[32,144,512]{2,1,0:T(8,128)(2,1)} %bitcast.34), calls=%async_computation.3 | async-start | bytes 9437184 | tf_op jit(solution)/shard_map/all_to_all | solution.py:82
  201.2 9.9 %fusion.3 = bf16[1024,512]{1,0:T(8,128)(2,1)} fusion(bf16[4608,512]{1,0:T(8,128)(2,1)} %bitcast.12, bf16[1024,4608]{0,1:T(8,128)(2,1)} %all-gather.2.cloned.1.call-done, f32[1024]{0:T(1024)S(1)} %mul.109), kind=kOutput, calls=%fused_computation.9 | convolution fusion | flops 4846518272 | bytes 15208448 | tf_op jit(solution)/shard_map/dot_general | solution.py:83
  211.1 58.2 %all-to-all-done.3 = bf16[32,144,512]{2,1,0:T(8,128)(2,1)} async-done(((bf16[32,144,512]{2,1,0:T(8,128)(2,1)}), bf16[32,144,512]{2,1,0:T(8,128)(2,1)}, u32[]{:S(2)}, u32[]{:S(2)}) %all-to-all-start.3) | async-done | bytes 4718624 | tf_op jit(solution)/shard_map/all_to_all | solution.py:82
  269.3 3.0 %convert_reduce_fusion = f32[144,512]{1,0:T(8,128)S(1)} fusion(bf16[32,144,512]{2,1,0:T(8,128)(2,1)} %all-to-all-done.3), kind=kLoop, calls=%fused_computation.5 | loop fusion | flops 4644864 | bytes 5013504 | tf_op jit(solution)/shard_map/reduce_sum | solution.py:84
  272.3 0.7 broadcast_multiply_fusion
  (23 shorter events, 0.1 us)
Async XLA Ops:
  7.2 109.9 %copy-start = (bf16[1024,512]{1,0:T(8,128)(2,1)S(1)}, bf16[1024,512]{1,0:T(8,128)(2,1)}, u32[]{:S(2)}) copy-start(bf16[1024,512]{1,0:T(8,128)(2,1)} %param.19) | copy-start | bytes 3145732
  7.2 109.8 %all-gather.2.cloned.1.call-start = ((), (), s32[]{:S(2)}) async-start(), calls=%async_computation.4 | async-start | bytes 10616832 | tf_op jit(solution)/shard_map/all_gather | solution.py:26
  10.2 11.8 %all-to-all-start = ((bf16[16,16,2,144]{3,2,1,0:T(2,128)(2,1)}), bf16[16,16,2,144]{3,2,1,0:T(2,128)(2,1)S(1)}, u32[]{:S(2)}, u32[]{:S(2)}) async-start(bf16[16,16,2,144]{3,2,1,0:T(2,128)(2,1)} %bitcast.33), calls=%async_computation | async-start | bytes 524288 | tf_op jit(solution)/shard_map/all_to_all | solution.py:36
  17.4 20.4 %collective-permute-start = (bf16[2,144,576]{2,1,0:T(8,128)(2,1)}, bf16[2,144,576]{2,1,0:T(8,128)(2,1)S(1)}, u32[]{:S(2)}, u32[]{:S(2)}) collective-permute-start(bf16[2,144,576]{2,1,0:T(8,128)(2,1)} %param.15), channel_id=1, source_target_pairs={{0,128},{128,0},{1,129},{129,1},{2,130},{130,2},{3,131},{131,3},{4... | collective-permute-start | bytes 995336 | tf_op jit(solution)/shard_map/ppermute | solution.py:29
  39.1 17.6 %copy-start.1 = (s32[2,8]{1,0:T(2,128)S(1)}, s32[2,8]{1,0:T(2,128)}, u32[]{:S(2)}) copy-start(s32[2,8]{1,0:T(2,128)} %param.13) | copy-start | bytes 196
  41.3 25.2 %all-to-all-start.1 = ((f32[16,16,1152]{2,1,0:T(8,128)}), f32[16,16,1152]{2,1,0:T(8,128)S(1)}, u32[]{:S(2)}, u32[]{:S(2)}) async-start(f32[16,16,1152]{2,1,0:T(8,128)} %bitcast.6), calls=%async_computation.1 | async-start | bytes 2359296 | tf_op jit(solution)/shard_map/all_to_all | solution.py:45
  56.6 11.6 %copy-start.3 = (f32[576]{0:T(1024)S(1)}, f32[576]{0:T(1024)}, u32[]{:S(2)}) copy-start(f32[576]{0:T(1024)} %param.17) | copy-start | bytes 6916
  56.6 11.6 %copy-start.4 = (f32[576]{0:T(1024)S(1)}, f32[576]{0:T(1024)}, u32[]{:S(2)}) copy-start(f32[576]{0:T(1024)} %param.16) | copy-start | bytes 6916
  56.6 32.8 %copy-start.2 = (bf16[144,512]{1,0:T(8,128)(2,1)S(1)}, bf16[144,512]{1,0:T(8,128)(2,1)}, u32[]{:S(2)}) copy-start(bf16[144,512]{1,0:T(8,128)(2,1)} %param.21) | copy-start | bytes 442372
  92.2 24.7 %copy-start.5 = (f32[16]{0:T(128)S(1)}, f32[16]{0:T(128)}, u32[]{:S(2)}) copy-start(f32[16]{0:T(128)} %param.18) | copy-start | bytes 196
  92.2 101.6 %all-to-all-start.2 = ((bf16[32,144,512]{2,1,0:T(8,128)(2,1)}), bf16[32,144,512]{2,1,0:T(8,128)(2,1)}, u32[]{:S(2)}, u32[]{:S(2)}) async-start(bf16[32,144,512]{2,1,0:T(8,128)(2,1)} %broadcast_in_dim.5), calls=%async_computation.2 | async-start | bytes 9437184 | tf_op jit(solution)/shard_map/all_to_all | solution.py:58
  193.8 75.5 %all-to-all-start.3 = ((bf16[32,144,512]{2,1,0:T(8,128)(2,1)}), bf16[32,144,512]{2,1,0:T(8,128)(2,1)}, u32[]{:S(2)}, u32[]{:S(2)}) async-start(bf16[32,144,512]{2,1,0:T(8,128)(2,1)} %bitcast.34), calls=%async_computation.3 | async-start | bytes 9437184 | tf_op jit(solution)/shard_map/all_to_all | solution.py:82
Sparse Core Ops, SparseCore 0:
  9.8 97.8 all-gather.1

commit v4 on v2

--- a/solution.py
+++ b/solution.py
@@ -24,11 +24,15 @@
     n_zl = lax.axis_size("zl")
     n_plane = lax.axis_size(PLANE)
     features = lax.all_gather(grad_out, TP, axis=1, tiled=True)
-    copies = jnp.broadcast_to(w_out[None], (n_dp,) + w_out.shape)
-    piece = lax.all_to_all(copies, DP, 0, 0, tiled=True).reshape(-1, w_out.shape[1])
+    zl = lax.axis_index("zl")
+    swap = [(k, (k + 1) % n_zl) for k in range(n_zl)]
+    w_other = lax.ppermute(w_out, "zl", swap)
+    w_pair = jnp.where(zl == 0, jnp.stack([w_out, w_other]), jnp.stack([w_other, w_out]))
+    copies = jnp.broadcast_to(w_pair[None], (n_plane,) + w_pair.shape)
+    piece = lax.all_to_all(copies, PLANE, 0, 0, tiled=True)
+    piece = piece.transpose(1, 0, 2, 3).reshape(-1, w_out.shape[1])
 
-    zl = lax.axis_index("zl")
-    other = lax.ppermute(pref_weight, "zl", [(k, (k + 1) % n_zl) for k in range(n_zl)])
+    other = lax.ppermute(pref_weight, "zl", swap)
     pair_w = jnp.where(
         zl == 0,
         jnp.concatenate([pref_weight, other], axis=1),
@@ -77,10 +81,13 @@
     full = lax.dot_general(
         weighted, attn_out, (((0,), (0,)), ((), ())), preferred_element_type=jnp.float32
     )
-    full = full.astype(jnp.bfloat16).reshape(n_dp, -1, full.shape[1])
-    shares = lax.all_to_all(full, DP, 0, 0, tiled=True)
+    full = full.astype(jnp.bfloat16).reshape(n_zl, n_plane, -1, full.shape[1])
+    shares = lax.all_to_all(full.transpose(1, 0, 2, 3), PLANE, 0, 0, tiled=True)
+    plane_sum = jnp.sum(shares.astype(jnp.float32), axis=0)
+    mine = jnp.where(zl == 0, plane_sum[0], plane_sum[1])
+    theirs = jnp.where(zl == 0, plane_sum[1], plane_sum[0])
     d_attn = jnp.dot(weighted, piece, preferred_element_type=jnp.float32).astype(jnp.bfloat16)
-    o_grad = jnp.sum(shares.astype(jnp.float32), axis=0) / total_resp
+    o_grad = (mine + lax.ppermute(theirs, "zl", swap)) / total_resp
     return (d_attn, o_grad)
 
 

time: 272 us -> 238 us (0.88)
  blocking collectives: 118 us -> 27.6 us
  waiting for transfers between devices: 74.3 us -> 122 us
  local copies, waits for them, and re-layouts: 12.9 us -> 20.6 us
    psum x1, blocking collectives: 97.4 us -> 27.6 us  [shards(): logit = lax.psum(partial_logit, TP)]
    ppermute x1 -> x3, waiting for transfers between devices: 0.01 us -> 25.7 us  [the longest x1 25.7 us: shards(): w_other = lax.ppermute(w_out, 'zl', swap)]
    all_to_all x2 -> x3, waiting for transfers between devices: 65 us -> 86.7 us  [the longest x1 62.9 us: shards(): shares = lax.all_to_all(full.transpose(1, 0, 2, 3), PLANE, 0, 0, tiled=True)]
    all_to_all x1 -> x0, blocking collectives: 20.5 us -> none  [shards(): proj = jnp.sum(lax.all_to_all(part, PLANE, 0, 0, tiled=True), axis=0)]
    all_to_all x0 -> x1, local copies, waits for them, and re-layouts: none -> 4.96 us  [shards(): piece = lax.all_to_all(copies, PLANE, 0, 0, tiled=True)]
    all_to_all x2 -> x3, starting transfers between devices: 17 us -> 15.4 us  [the longest x1 7.12 us: shards(): piece = lax.all_to_all(copies, PLANE, 0, 0, tiled=True)]
  transfers between devices with their start and end apart: 5 -> 8, of which waited for: 2 -> 4; matrix products, arithmetic and copies ran while one was open for 13% -> 18% of each run, Pallas kernels for 0% -> 0%
where the time goes in v4:
time: 238 us; the launch traced here: 234 us
  waiting for transfers between devices  122 us (51%)
  blocking collectives  27.6 us (12%)
  starting transfers between devices  24.9 us (10%)
  local copies, waits for them, and re-layouts  20.6 us (9%)
  matrix products  18.6 us (8%)
  between operations  14.3 us (6%)
  other arithmetic  6.17 us (3%)
    all_to_all x1, waiting for transfers between devices, shards(): shares = lax.all_to_all(full.transpose(1, 0, 2, 3), PLANE, 0, 0, tiled=True)  62.9 us
    psum x1, blocking collectives, shards(): logit = lax.psum(partial_logit, TP)  27.6 us
    ppermute x1, waiting for transfers between devices, shards(): w_other = lax.ppermute(w_out, 'zl', swap)  25.7 us
    all_to_all x1, waiting for transfers between devices, shards(): piece = lax.all_to_all(copies, PLANE, 0, 0, tiled=True)  23.9 us
    dot_general x1, matrix products, shards(): lax.dot_general(weighted, attn_out, (((0,), (0,)), ((), ())), preferred_e...  9.06 us
    dot_general x1, matrix products, shards(): jnp.dot(weighted, piece, preferred_element_type=jnp.float32)  8.84 us
    all_to_all x1, waiting for transfers between devices, shards(): lax.all_to_all(cols, PLANE, 0, 0, tiled=True)  8.69 us
    all_to_all x1, starting transfers between devices, shards(): piece = lax.all_to_all(copies, PLANE, 0, 0, tiled=True)  7.12 us
  transfers between devices with their start and end apart: 8, of which 4 were waited for; matrix products, arithmetic and copies ran while one was open for 18% of the time, Pallas kernels for 0%

profile of v4, /device:TPU:96, one launch (start us, length us, event | category | flops | bytes accessed | tf_op | source)
XLA Modules:
  0.0 234.0 jit_solution(1135153115788810141)
XLA Ops:
  7.2 0.7 all-gather.2.cloned.1.call-update
  7.9 0.2 collective-permute-start
  8.1 1.3 reshape.155
  9.4 0.9 copy.25
  10.4 7.0 %all-to-all-start = ((bf16[16,16,2,144]{3,2,1,0:T(2,128)(2,1)}), bf16[16,16,2,144]{3,2,1,0:T(2,128)(2,1)S(1)}, u32[]{:S(2)}, u32[]{:S(2)}) async-start(bf16[16,16,2,144]{3,2,1,0:T(2,128)(2,1)} %bitcast.46), calls=%async_computation | async-start | bytes 524288 | tf_op jit(solution)/shard_map/all_to_all | solution.py:42
  17.4 8.7 %all-to-all-done = bf16[16,16,2,144]{3,2,1,0:T(2,128)(2,1)S(1)} async-done(((bf16[16,16,2,144]{3,2,1,0:T(2,128)(2,1)}), bf16[16,16,2,144]{3,2,1,0:T(2,128)(2,1)S(1)}, u32[]{:S(2)}, u32[]{:S(2)}) %all-to-all-start) | async-done | bytes 147488 | tf_op jit(solution)/shard_map/all_to_all | solution.py:42
  26.1 0.2 reshape.156
  26.3 1.4 maximum_select_fusion
  27.7 0.4 convolution_bitcast_fusion
  28.1 0.3 convolution_bitcast_fusion.1
  28.4 0.1 pad_maximum_fusion
  28.5 1.4 copy.19
  29.9 3.7 %all-to-all-start.1 = ((f32[16,16,1152]{2,1,0:T(8,128)}), f32[16,16,1152]{2,1,0:T(8,128)S(1)}, u32[]{:S(2)}, u32[]{:S(2)}) async-start(f32[16,16,1152]{2,1,0:T(8,128)} %bitcast.6), calls=%async_computation.1 | async-start | bytes 2359296 | tf_op jit(solution)/shard_map/all_to_all | solution.py:51
  33.6 1.9 collective-permute-start.1
  35.6 25.7 %collective-permute-done.1 = bf16[144,512]{1,0:T(8,128)(2,1)S(1)} collective-permute-done((bf16[144,512]{1,0:T(8,128)(2,1)S(1)}, bf16[144,512]{1,0:T(8,128)(2,1)S(1)}, u32[]{:S(2)}, u32[]{:S(2)}) %collective-permute-start.1) | collective-permute-done | bytes 147488 | tf_op jit(solution)/shard_map/ppermute | solution.py:29
  61.3 2.7 %broadcast_in_dim.4 = bf16[16,2,144,512]{3,2,1,0:T(8,128)(2,1)} broadcast(bf16[2,144,512]{2,1,0:T(8,128)(2,1)S(1)} %maximum_select_fusion.1), dimensions={1,2,3} | broadcast | bytes 5013504 | tf_op jit(solution)/shard_map/broadcast_in_dim | solution.py:31
  64.0 7.1 %all-to-all-start.2 = ((bf16[16,2,144,512]{3,2,1,0:T(8,128)(2,1)}), bf16[16,2,144,512]{3,2,1,0:T(8,128)(2,1)}, u32[]{:S(2)}, u32[]{:S(2)}) async-start(bf16[16,2,144,512]{3,2,1,0:T(8,128)(2,1)} %broadcast_in_dim.4), calls=%async_computation.2 | async-start | bytes 9437184 | tf_op jit(solution)/shard_map/all_to_all | solution.py:32
  71.2 0.1 reshape.207
  71.3 2.0 gather_fusion.3
  73.3 0.1 reshape.210
  73.4 0.1 reshape.202
  73.5 2.0 gather_fusion.2
  75.5 0.1 reshape.205
  75.6 0.1 fusion.15
  75.6 0.1 reshape.158
  75.7 0.1 reshape.159
  75.9 0.1 fusion.18
  76.0 0.8 gather_fusion
  76.8 0.8 gather_fusion.1
  77.6 0.2 fusion.13
  77.8 0.1 reduce_sum.58
  77.9 27.6 %psum.7 = f32[2,56]{1,0:T(2,128)S(1)} all-reduce(f32[2,56]{1,0:T(2,128)S(1)} %reduce_sum.58), channel_id=1, replica_groups=mesh['zl'=2,'y'=4,'x'=4,'zh'=4,'c'=2] {'zh','c'}, use_global_device_ids=true, to_apply=%region_2.4 | all-reduce | flops 112 | bytes 896 | tf_op jit(solution)/shard_map/psum | solution.py:61
  105.5 0.1 add_reduce_fusion.1
  105.6 0.1 select_reduce_fusion
  105.7 0.1 mul.106
  105.8 0.1 mul.108
  105.9 0.1 mul.109
  106.0 9.1 %fusion.2 = bf16[4608,512]{1,0:T(8,128)(2,1)S(1)} fusion(bf16[1024,512]{1,0:T(8,128)(2,1)S(1)} %copy-done, bf16[1024,4608]{0,1:T(8,128)(2,1)} %all-gather.2.cloned.1.call-done, f32[1024]{0:T(1024)S(1)} %mul.109), kind=kOutput, calls=%fused_computation.8 | convolution fusion | flops 4848353280 | bytes 15208448 | tf_op jit(solution)/shard_map/dot_general | solution.py:81
  115.0 2.4 %copy.24 = bf16[2,16,144,512]{3,2,0,1:T(8,128)(2,1)} copy(bf16[2,16,144,512]{3,2,1,0:T(8,128)(2,1)S(1)} %bitcast.49) | data formatting | bytes 9437184 | tf_op jit(solution)/shard_map/reshape | solution.py:84
  117.5 23.9 %all-to-all-done.2 = bf16[16,2,144,512]{3,2,1,0:T(8,128)(2,1)} async-done(((bf16[16,2,144,512]{3,2,1,0:T(8,128)(2,1)}), bf16[16,2,144,512]{3,2,1,0:T(8,128)(2,1)}, u32[]{:S(2)}, u32[]{:S(2)}) %all-to-all-start.2) | async-done | bytes 4718624 | tf_op jit(solution)/shard_map/all_to_all | solution.py:32
  141.3 4.6 %all-to-all-start.3 = ((bf16[16,2,144,512]{3,2,1,0:T(8,128)(2,1)}), bf16[16,2,144,512]{3,2,1,0:T(8,128)(2,1)}, u32[]{:S(2)}, u32[]{:S(2)}) async-start(bf16[16,2,144,512]{3,2,1,0:T(8,128)(2,1)} %bitcast.47), calls=%async_computation.3 | async-start | bytes 9437184 | tf_op jit(solution)/shard_map/all_to_all | solution.py:85
  145.9 5.0 %copy.20 = bf16[16,2,144,512]{3,2,0,1:T(8,128)(2,1)} copy(bf16[16,2,144,512]{3,2,1,0:T(8,128)(2,1)} %all-to-all-done.2) | data formatting | bytes 9437184 | tf_op jit(solution)/shard_map/all_to_all | solution.py:32
  150.9 62.9 %all-to-all-done.3 = bf16[16,2,144,512]{3,2,1,0:T(8,128)(2,1)} async-done(((bf16[16,2,144,512]{3,2,1,0:T(8,128)(2,1)}), bf16[16,2,144,512]{3,2,1,0:T(8,128)(2,1)}, u32[]{:S(2)}, u32[]{:S(2)}) %all-to-all-start.3) | async-done | bytes 4718624 | tf_op jit(solution)/shard_map/all_to_all | solution.py:85
  213.8 3.2 %convert_reduce_fusion = f32[2,144,512]{2,1,0:T(8,128)S(1)} fusion(bf16[16,2,144,512]{3,2,1,0:T(8,128)(2,1)} %all-to-all-done.3), kind=kLoop, calls=%fused_computation.5 | loop fusion | flops 4571136 | bytes 5308416 | tf_op jit(solution)/shard_map/reduce_sum | solution.py:86
  217.1 0.3 collective-permute-start.2
  217.4 0.2 copy-done.2
  217.5 8.8 %fusion.3 = bf16[1024,512]{1,0:T(8,128)(2,1)} fusion(bf16[4608,512]{1,0:T(8,128)(2,1)S(1)} %bitcast.48, bf16[1024,4608]{0,1:T(8,128)(2,1)} %all-gather.2.cloned.1.call-done, f32[1024]{0:T(1024)S(1)} %mul.109), kind=kOutput, calls=%fused_computation.10 | convolution fusion | flops 4846518272 | bytes 15208448 | tf_op jit(solution)/shard_map/dot_general | solution.py:89
  226.4 0.8 fusion.4
  (35 shorter events, 0.3 us)
Async XLA Ops:
  7.2 98.8 %copy-start = (bf16[1024,512]{1,0:T(8,128)(2,1)S(1)}, bf16[1024,512]{1,0:T(8,128)(2,1)}, u32[]{:S(2)}) copy-start(bf16[1024,512]{1,0:T(8,128)(2,1)} %param.19) | copy-start | bytes 3145732
  7.2 98.8 %all-gather.2.cloned.1.call-start = ((), (), s32[]{:S(2)}) async-start(), calls=%async_computation.4 | async-start | bytes 10616832 | tf_op jit(solution)/shard_map/all_gather | solution.py:26
  7.9 18.4 %collective-permute-start = (bf16[2,144,576]{2,1,0:T(8,128)(2,1)}, bf16[2,144,576]{2,1,0:T(8,128)(2,1)S(1)}, u32[]{:S(2)}, u32[]{:S(2)}) collective-permute-start(bf16[2,144,576]{2,1,0:T(8,128)(2,1)} %param.15), channel_id=1, source_target_pairs={{0,128},{128,0},{1,129},{129,1},{2,130},{130,2},{3,131},{131,3},{4... | collective-permute-start | bytes 995336 | tf_op jit(solution)/shard_map/ppermute | solution.py:35
  10.4 15.7 %all-to-all-start = ((bf16[16,16,2,144]{3,2,1,0:T(2,128)(2,1)}), bf16[16,16,2,144]{3,2,1,0:T(2,128)(2,1)S(1)}, u32[]{:S(2)}, u32[]{:S(2)}) async-start(bf16[16,16,2,144]{3,2,1,0:T(2,128)(2,1)} %bitcast.46), calls=%async_computation | async-start | bytes 524288 | tf_op jit(solution)/shard_map/all_to_all | solution.py:42
  27.7 5.9 %copy-start.3 = (bf16[144,512]{1,0:T(8,128)(2,1)S(1)}, bf16[144,512]{1,0:T(8,128)(2,1)}, u32[]{:S(2)}) copy-start(bf16[144,512]{1,0:T(8,128)(2,1)} %param.21) | copy-start | bytes 442372
  27.7 7.9 %copy-start.6 = (s32[2,56,2]{1,2,0:T(2,128)S(1)}, s32[2,56,2]{1,2,0:T(2,128)}, u32[]{:S(2)}) copy-start(s32[2,56,2]{1,2,0:T(2,128)} %param.14) | copy-start | bytes 2692
  29.9 31.4 %all-to-all-start.1 = ((f32[16,16,1152]{2,1,0:T(8,128)}), f32[16,16,1152]{2,1,0:T(8,128)S(1)}, u32[]{:S(2)}, u32[]{:S(2)}) async-start(f32[16,16,1152]{2,1,0:T(8,128)} %bitcast.6), calls=%async_computation.1 | async-start | bytes 2359296 | tf_op jit(solution)/shard_map/all_to_all | solution.py:51
  33.6 27.7 %collective-permute-start.1 = (bf16[144,512]{1,0:T(8,128)(2,1)S(1)}, bf16[144,512]{1,0:T(8,128)(2,1)S(1)}, u32[]{:S(2)}, u32[]{:S(2)}) collective-permute-start(bf16[144,512]{1,0:T(8,128)(2,1)S(1)} %copy-done.3), channel_id=1, source_target_pairs={{0,128},{128,0},{1,129},{129,1},{2,130},{130,2},{3,131},{131,3},{4... | collective-permute-start | bytes 442376 | tf_op jit(solution)/shard_map/ppermute | solution.py:29
  64.0 7.3 %copy-start.1 = (s32[2,8]{1,0:T(2,128)S(1)}, s32[2,8]{1,0:T(2,128)}, u32[]{:S(2)}) copy-start(s32[2,8]{1,0:T(2,128)} %param.13) | copy-start | bytes 196
  64.0 77.3 %all-to-all-start.2 = ((bf16[16,2,144,512]{3,2,1,0:T(8,128)(2,1)}), bf16[16,2,144,512]{3,2,1,0:T(8,128)(2,1)}, u32[]{:S(2)}, u32[]{:S(2)}) async-start(bf16[16,2,144,512]{3,2,1,0:T(8,128)(2,1)} %broadcast_in_dim.4), calls=%async_computation.2 | async-start | bytes 9437184 | tf_op jit(solution)/shard_map/all_to_all | solution.py:32
  71.1 6.4 %copy-start.4 = (f32[576]{0:T(1024)S(1)}, f32[576]{0:T(1024)}, u32[]{:S(2)}) copy-start(f32[576]{0:T(1024)} %param.17) | copy-start | bytes 6916
  71.1 6.4 %copy-start.5 = (f32[576]{0:T(1024)S(1)}, f32[576]{0:T(1024)}, u32[]{:S(2)}) copy-start(f32[576]{0:T(1024)} %param.16) | copy-start | bytes 6916
  71.3 34.6 %copy-start.7 = (f32[16]{0:T(128)S(1)}, f32[16]{0:T(128)}, u32[]{:S(2)}) copy-start(f32[16]{0:T(128)} %param.18) | copy-start | bytes 196
  141.3 72.4 %all-to-all-start.3 = ((bf16[16,2,144,512]{3,2,1,0:T(8,128)(2,1)}), bf16[16,2,144,512]{3,2,1,0:T(8,128)(2,1)}, u32[]{:S(2)}, u32[]{:S(2)}) async-start(bf16[16,2,144,512]{3,2,1,0:T(8,128)(2,1)} %bitcast.47), calls=%async_computation.3 | async-start | bytes 9437184 | tf_op jit(solution)/shard_map/all_to_all | solution.py:85
  213.8 3.8 %copy-start.2 = (bf16[16,2,144,512]{3,2,0,1:T(8,128)(2,1)S(1)}, bf16[16,2,144,512]{3,2,0,1:T(8,128)(2,1)}, u32[]{:S(2)}) copy-start(bf16[16,2,144,512]{3,2,0,1:T(8,128)(2,1)} %copy.20) | copy-start | bytes 14155780
  217.1 9.3 %collective-permute-start.2 = (f32[144,512]{1,0:T(8,128)S(1)}, f32[144,512]{1,0:T(8,128)S(1)}, u32[]{:S(2)}, u32[]{:S(2)}) collective-permute-start(f32[144,512]{1,0:T(8,128)S(1)} %select_bitcast_fusion), channel_id=1, source_target_pairs={{0,128},{128,0},{1,129},{129,1},{2,130},{130,2},{3,131},{131,3},{4... | collective-permute-start | bytes 884744 | tf_op jit(solution)/shard_map/ppermute | solution.py:90
Sparse Core Ops, SparseCore 0:
  9.8 86.8 all-gather.1

commit v5 on v4

--- a/solution.py
+++ b/solution.py
@@ -23,16 +23,17 @@
     n_dp = lax.axis_size(DP)
     n_zl = lax.axis_size("zl")
     n_plane = lax.axis_size(PLANE)
-    features = lax.all_gather(grad_out, TP, axis=1, tiled=True)
     zl = lax.axis_index("zl")
     swap = [(k, (k + 1) % n_zl) for k in range(n_zl)]
     w_other = lax.ppermute(w_out, "zl", swap)
+    other = lax.ppermute(pref_weight, "zl", swap)
+    grad_out, w_other, other = lax.optimization_barrier((grad_out, w_other, other))
+    features = lax.all_gather(grad_out, TP, axis=1, tiled=True)
     w_pair = jnp.where(zl == 0, jnp.stack([w_out, w_other]), jnp.stack([w_other, w_out]))
     copies = jnp.broadcast_to(w_pair[None], (n_plane,) + w_pair.shape)
     piece = lax.all_to_all(copies, PLANE, 0, 0, tiled=True)
     piece = piece.transpose(1, 0, 2, 3).reshape(-1, w_out.shape[1])
 
-    other = lax.ppermute(pref_weight, "zl", swap)
     pair_w = jnp.where(
         zl == 0,
         jnp.concatenate([pref_weight, other], axis=1),

time: 238 us -> 232 us (0.975)
  blocking collectives: 27.6 us -> 18.3 us
  waiting for transfers between devices: 122 us -> 128 us
    all_gather x1, waiting for transfers between devices: 0.01 us -> 21.6 us  [shards(): features = lax.all_gather(grad_out, TP, axis=1, tiled=True)]
    all_to_all x1, waiting for transfers between devices: 23.9 us -> 3.7 us  [shards(): piece = lax.all_to_all(copies, PLANE, 0, 0, tiled=True)]
    all_to_all x1, waiting for transfers between devices: 0.01 us -> 17.2 us  [shards(): proj = jnp.sum(lax.all_to_all(part, PLANE, 0, 0, tiled=True), axis=0)]
    ppermute x1, waiting for transfers between devices: 25.7 us -> 11.7 us  [shards(): w_other = lax.ppermute(w_out, 'zl', swap)]
    psum x1, blocking collectives: 27.6 us -> 18.3 us  [shards(): logit = lax.psum(partial_logit, TP)]
    all_to_all x1, starting transfers between devices: 7.12 us -> 4.68 us  [shards(): piece = lax.all_to_all(copies, PLANE, 0, 0, tiled=True)]
  transfers between devices with their start and end apart: 8 -> 8, of which waited for: 4 -> 6; matrix products, arithmetic and copies ran while one was open for 18% -> 18% of each run, Pallas kernels for 0% -> 0%
where the time goes in v5:
time: 232 us; the launch traced here: 229 us
  waiting for transfers between devices  128 us (55%)
  starting transfers between devices  24.1 us (10%)
  local copies, waits for them, and re-layouts  20.4 us (9%)
  matrix products  18.6 us (8%)
  blocking collectives  18.3 us (8%)
  between operations  14.3 us (6%)
  other arithmetic  6.11 us (3%)
    all_to_all x1, waiting for transfers between devices, shards(): shares = lax.all_to_all(full.transpose(1, 0, 2, 3), PLANE, 0, 0, tiled=True)  64.8 us
    all_gather x1, waiting for transfers between devices, shards(): features = lax.all_gather(grad_out, TP, axis=1, tiled=True)  21.6 us
    psum x1, blocking collectives, shards(): logit = lax.psum(partial_logit, TP)  18.3 us
    all_to_all x1, waiting for transfers between devices, shards(): proj = jnp.sum(lax.all_to_all(part, PLANE, 0, 0, tiled=True), axis=0)  17.2 us
    ppermute x1, waiting for transfers between devices, shards(): w_other = lax.ppermute(w_out, 'zl', swap)  11.7 us
    dot_general x1, matrix products, shards(): lax.dot_general(weighted, attn_out, (((0,), (0,)), ((), ())), preferred_e...  9.05 us
    dot_general x1, matrix products, shards(): jnp.dot(weighted, piece, preferred_element_type=jnp.float32)  8.84 us
    all_to_all x1, waiting for transfers between devices, shards(): lax.all_to_all(cols, PLANE, 0, 0, tiled=True)  8.69 us
  transfers between devices with their start and end apart: 8, of which 6 were waited for; matrix products, arithmetic and copies ran while one was open for 18% of the time, Pallas kernels for 0%

profile of v5, /device:TPU:96, one launch (start us, length us, event | category | flops | bytes accessed | tf_op | source)
XLA Modules:
  0.0 229.4 jit_solution(14268883007941229011)
XLA Ops:
  7.2 0.2 collective-permute-start.1
  7.4 1.9 collective-permute-start
  9.3 11.7 %collective-permute-done = bf16[144,512]{1,0:T(8,128)(2,1)S(1)} collective-permute-done((bf16[144,512]{1,0:T(8,128)(2,1)}, bf16[144,512]{1,0:T(8,128)(2,1)S(1)}, u32[]{:S(2)}, u32[]{:S(2)}) %collective-permute-start) | collective-permute-done | bytes 147488 | tf_op jit(solution)/shard_map/ppermute | solution.py:28
  21.0 1.3 reshape.155
  22.4 0.9 copy.25
  23.3 7.0 %all-to-all-start = ((bf16[16,16,2,144]{3,2,1,0:T(2,128)(2,1)}), bf16[16,16,2,144]{3,2,1,0:T(2,128)(2,1)S(1)}, u32[]{:S(2)}, u32[]{:S(2)}) async-start(bf16[16,16,2,144]{3,2,1,0:T(2,128)(2,1)} %bitcast.46), calls=%async_computation | async-start | bytes 524288 | tf_op jit(solution)/shard_map/all_to_all | solution.py:43
  30.4 8.7 %all-to-all-done = bf16[16,16,2,144]{3,2,1,0:T(2,128)(2,1)S(1)} async-done(((bf16[16,16,2,144]{3,2,1,0:T(2,128)(2,1)}), bf16[16,16,2,144]{3,2,1,0:T(2,128)(2,1)S(1)}, u32[]{:S(2)}, u32[]{:S(2)}) %all-to-all-start) | async-done | bytes 147488 | tf_op jit(solution)/shard_map/all_to_all | solution.py:43
  39.0 0.2 reshape.156
  39.2 1.3 maximum_select_fusion
  40.6 0.4 convolution_bitcast_fusion
  40.9 0.3 convolution_bitcast_fusion.1
  41.3 0.1 pad_maximum_fusion
  41.4 1.4 copy.19
  42.7 3.7 %all-to-all-start.1 = ((f32[16,16,1152]{2,1,0:T(8,128)}), f32[16,16,1152]{2,1,0:T(8,128)S(1)}, u32[]{:S(2)}, u32[]{:S(2)}) async-start(f32[16,16,1152]{2,1,0:T(8,128)} %bitcast.6), calls=%async_computation.1 | async-start | bytes 2359296 | tf_op jit(solution)/shard_map/all_to_all | solution.py:52
  46.5 17.2 %all-to-all-done.1 = f32[16,16,1152]{2,1,0:T(8,128)S(1)} async-done(((f32[16,16,1152]{2,1,0:T(8,128)}), f32[16,16,1152]{2,1,0:T(8,128)S(1)}, u32[]{:S(2)}, u32[]{:S(2)}) %all-to-all-start.1) | async-done | bytes 1179680 | tf_op jit(solution)/shard_map/all_to_all | solution.py:52
  63.7 2.7 %broadcast_in_dim.4 = bf16[16,2,144,512]{3,2,1,0:T(8,128)(2,1)} broadcast(bf16[2,144,512]{2,1,0:T(8,128)(2,1)S(1)} %maximum_select_fusion.1), dimensions={1,2,3} | broadcast | bytes 5013504 | tf_op jit(solution)/shard_map/broadcast_in_dim | solution.py:33
  66.4 4.7 %all-to-all-start.2 = ((bf16[16,2,144,512]{3,2,1,0:T(8,128)(2,1)}), bf16[16,2,144,512]{3,2,1,0:T(8,128)(2,1)}, u32[]{:S(2)}, u32[]{:S(2)}) async-start(bf16[16,2,144,512]{3,2,1,0:T(8,128)(2,1)} %broadcast_in_dim.4), calls=%async_computation.2 | async-start | bytes 9437184 | tf_op jit(solution)/shard_map/all_to_all | solution.py:34
  71.1 0.1 reshape.207
  71.2 2.0 gather_fusion.3
  73.2 0.1 reshape.210
  73.3 0.1 reshape.202
  73.4 2.0 gather_fusion.2
  75.4 0.1 reshape.205
  75.5 0.1 fusion.15
  75.6 0.1 reshape.158
  75.7 0.1 reshape.159
  75.9 0.1 fusion.18
  75.9 0.8 gather_fusion
  76.7 0.8 gather_fusion.1
  77.5 0.2 fusion.13
  77.8 0.1 reduce_sum.58
  77.8 18.3 %psum.7 = f32[2,56]{1,0:T(2,128)S(1)} all-reduce(f32[2,56]{1,0:T(2,128)S(1)} %reduce_sum.58), channel_id=1, replica_groups=mesh['zl'=2,'y'=4,'x'=4,'zh'=4,'c'=2] {'zh','c'}, use_global_device_ids=true, to_apply=%region_2.4 | all-reduce | flops 112 | bytes 896 | tf_op jit(solution)/shard_map/psum | solution.py:62
  96.1 0.1 add_reduce_fusion.1
  96.2 0.1 select_reduce_fusion
  96.3 0.1 mul.106
  96.4 0.1 mul.108
  96.5 0.1 mul.109
  96.6 21.6 %all-gather.2.cloned.1.call-done = bf16[1024,4608]{0,1:T(8,128)(2,1)} async-done(((bf16[1024,576]{0,1:T(8,128)(2,1)}), bf16[1024,4608]{0,1:T(8,128)(2,1)}) %all-gather.2.cloned.1.call-update) | async-done | bytes 9437200 | tf_op jit(solution)/shard_map/all_gather | solution.py:31
  118.1 9.1 %fusion.2 = bf16[4608,512]{1,0:T(8,128)(2,1)S(1)} fusion(bf16[1024,512]{1,0:T(8,128)(2,1)S(1)} %copy-done, bf16[1024,4608]{0,1:T(8,128)(2,1)} %all-gather.2.cloned.1.call-done, f32[1024]{0:T(1024)S(1)} %mul.109), kind=kOutput, calls=%fused_computation.8 | convolution fusion | flops 4848353280 | bytes 15208448 | tf_op jit(solution)/shard_map/dot_general | solution.py:82
  127.2 2.4 %copy.24 = bf16[2,16,144,512]{3,2,0,1:T(8,128)(2,1)} copy(bf16[2,16,144,512]{3,2,1,0:T(8,128)(2,1)S(1)} %bitcast.49) | data formatting | bytes 9437184 | tf_op jit(solution)/shard_map/reshape | solution.py:85
  129.6 3.7 %all-to-all-done.2 = bf16[16,2,144,512]{3,2,1,0:T(8,128)(2,1)} async-done(((bf16[16,2,144,512]{3,2,1,0:T(8,128)(2,1)}), bf16[16,2,144,512]{3,2,1,0:T(8,128)(2,1)}, u32[]{:S(2)}, u32[]{:S(2)}) %all-to-all-start.2) | async-done | bytes 4718624 | tf_op jit(solution)/shard_map/all_to_all | solution.py:34
  133.3 4.6 %all-to-all-start.3 = ((bf16[16,2,144,512]{3,2,1,0:T(8,128)(2,1)}), bf16[16,2,144,512]{3,2,1,0:T(8,128)(2,1)}, u32[]{:S(2)}, u32[]{:S(2)}) async-start(bf16[16,2,144,512]{3,2,1,0:T(8,128)(2,1)} %bitcast.47), calls=%async_computation.3 | async-start | bytes 9437184 | tf_op jit(solution)/shard_map/all_to_all | solution.py:86
  137.9 5.0 %copy.20 = bf16[16,2,144,512]{3,2,0,1:T(8,128)(2,1)} copy(bf16[16,2,144,512]{3,2,1,0:T(8,128)(2,1)} %all-to-all-done.2) | data formatting | bytes 9437184 | tf_op jit(solution)/shard_map/all_to_all | solution.py:34
  142.9 64.8 %all-to-all-done.3 = bf16[16,2,144,512]{3,2,1,0:T(8,128)(2,1)} async-done(((bf16[16,2,144,512]{3,2,1,0:T(8,128)(2,1)}), bf16[16,2,144,512]{3,2,1,0:T(8,128)(2,1)}, u32[]{:S(2)}, u32[]{:S(2)}) %all-to-all-start.3) | async-done | bytes 4718624 | tf_op jit(solution)/shard_map/all_to_all | solution.py:86
  207.6 3.2 %convert_reduce_fusion = f32[2,144,512]{2,1,0:T(8,128)S(1)} fusion(bf16[16,2,144,512]{3,2,1,0:T(8,128)(2,1)} %all-to-all-done.3), kind=kLoop, calls=%fused_computation.5 | loop fusion | flops 4571136 | bytes 5308416 | tf_op jit(solution)/shard_map/reduce_sum | solution.py:87
  210.9 2.0 collective-permute-start.2
  212.9 8.8 %fusion.3 = bf16[1024,512]{1,0:T(8,128)(2,1)} fusion(bf16[4608,512]{1,0:T(8,128)(2,1)S(1)} %bitcast.48, bf16[1024,4608]{0,1:T(8,128)(2,1)} %all-gather.2.cloned.1.call-done, f32[1024]{0:T(1024)S(1)} %mul.109), kind=kOutput, calls=%fused_computation.10 | convolution fusion | flops 4846518272 | bytes 15208448 | tf_op jit(solution)/shard_map/dot_general | solution.py:90
  221.7 0.8 fusion.4
  (35 shorter events, 0.3 us)
Async XLA Ops:
  7.2 111.0 %copy-start = (bf16[1024,512]{1,0:T(8,128)(2,1)S(1)}, bf16[1024,512]{1,0:T(8,128)(2,1)}, u32[]{:S(2)}) copy-start(bf16[1024,512]{1,0:T(8,128)(2,1)} %param.19) | copy-start | bytes 3145732
  7.2 111.0 %all-gather.2.cloned.1.call-start = ((), (), s32[]{:S(2)}) async-start(), calls=%async_computation.4 | async-start | bytes 10616832 | tf_op jit(solution)/shard_map/all_gather | solution.py:31
  7.2 13.8 %collective-permute-start.1 = (bf16[2,144,576]{2,1,0:T(8,128)(2,1)}, bf16[2,144,576]{2,1,0:T(8,128)(2,1)S(1)}, u32[]{:S(2)}, u32[]{:S(2)}) collective-permute-start(bf16[2,144,576]{2,1,0:T(8,128)(2,1)} %param.15), channel_id=1, source_target_pairs={{0,128},{128,0},{1,129},{129,1},{2,130},{130,2},{3,131},{131,3},{4... | collective-permute-start | bytes 995336 | tf_op jit(solution)/shard_map/ppermute | solution.py:29
  7.4 13.6 %collective-permute-start = (bf16[144,512]{1,0:T(8,128)(2,1)}, bf16[144,512]{1,0:T(8,128)(2,1)S(1)}, u32[]{:S(2)}, u32[]{:S(2)}) collective-permute-start(bf16[144,512]{1,0:T(8,128)(2,1)} %param.21), channel_id=1, source_target_pairs={{0,128},{128,0},{1,129},{129,1},{2,130},{130,2},{3,131},{131,3},{4... | collective-permute-start | bytes 442376 | tf_op jit(solution)/shard_map/ppermute | solution.py:28
  23.3 15.7 %all-to-all-start = ((bf16[16,16,2,144]{3,2,1,0:T(2,128)(2,1)}), bf16[16,16,2,144]{3,2,1,0:T(2,128)(2,1)S(1)}, u32[]{:S(2)}, u32[]{:S(2)}) async-start(bf16[16,16,2,144]{3,2,1,0:T(2,128)(2,1)} %bitcast.46), calls=%async_computation | async-start | bytes 524288 | tf_op jit(solution)/shard_map/all_to_all | solution.py:43
  40.5 5.9 %copy-start.6 = (s32[2,56,2]{1,2,0:T(2,128)S(1)}, s32[2,56,2]{1,2,0:T(2,128)}, u32[]{:S(2)}) copy-start(s32[2,56,2]{1,2,0:T(2,128)} %param.14) | copy-start | bytes 2692
  40.5 5.9 %copy-start.3 = (bf16[144,512]{1,0:T(8,128)(2,1)S(1)}, bf16[144,512]{1,0:T(8,128)(2,1)}, u32[]{:S(2)}) copy-start(bf16[144,512]{1,0:T(8,128)(2,1)} %param.21) | copy-start | bytes 442372
  42.7 20.9 %all-to-all-start.1 = ((f32[16,16,1152]{2,1,0:T(8,128)}), f32[16,16,1152]{2,1,0:T(8,128)S(1)}, u32[]{:S(2)}, u32[]{:S(2)}) async-start(f32[16,16,1152]{2,1,0:T(8,128)} %bitcast.6), calls=%async_computation.1 | async-start | bytes 2359296 | tf_op jit(solution)/shard_map/all_to_all | solution.py:52
  66.4 4.8 %copy-start.1 = (s32[2,8]{1,0:T(2,128)S(1)}, s32[2,8]{1,0:T(2,128)}, u32[]{:S(2)}) copy-start(s32[2,8]{1,0:T(2,128)} %param.13) | copy-start | bytes 196
  66.4 66.9 %all-to-all-start.2 = ((bf16[16,2,144,512]{3,2,1,0:T(8,128)(2,1)}), bf16[16,2,144,512]{3,2,1,0:T(8,128)(2,1)}, u32[]{:S(2)}, u32[]{:S(2)}) async-start(bf16[16,2,144,512]{3,2,1,0:T(8,128)(2,1)} %broadcast_in_dim.4), calls=%async_computation.2 | async-start | bytes 9437184 | tf_op jit(solution)/shard_map/all_to_all | solution.py:34
  71.1 6.4 %copy-start.4 = (f32[576]{0:T(1024)S(1)}, f32[576]{0:T(1024)}, u32[]{:S(2)}) copy-start(f32[576]{0:T(1024)} %param.17) | copy-start | bytes 6916
  71.1 6.4 %copy-start.5 = (f32[576]{0:T(1024)S(1)}, f32[576]{0:T(1024)}, u32[]{:S(2)}) copy-start(f32[576]{0:T(1024)} %param.16) | copy-start | bytes 6916
  71.2 25.2 %copy-start.7 = (f32[16]{0:T(128)S(1)}, f32[16]{0:T(128)}, u32[]{:S(2)}) copy-start(f32[16]{0:T(128)} %param.18) | copy-start | bytes 196
  133.3 74.3 %all-to-all-start.3 = ((bf16[16,2,144,512]{3,2,1,0:T(8,128)(2,1)}), bf16[16,2,144,512]{3,2,1,0:T(8,128)(2,1)}, u32[]{:S(2)}, u32[]{:S(2)}) async-start(bf16[16,2,144,512]{3,2,1,0:T(8,128)(2,1)} %bitcast.47), calls=%async_computation.3 | async-start | bytes 9437184 | tf_op jit(solution)/shard_map/all_to_all | solution.py:86
  207.6 5.3 %copy-start.2 = (bf16[16,2,144,512]{3,2,0,1:T(8,128)(2,1)S(1)}, bf16[16,2,144,512]{3,2,0,1:T(8,128)(2,1)}, u32[]{:S(2)}) copy-start(bf16[16,2,144,512]{3,2,0,1:T(8,128)(2,1)} %copy.20) | copy-start | bytes 14155780
  210.9 10.8 %collective-permute-start.2 = (f32[144,512]{1,0:T(8,128)S(1)}, f32[144,512]{1,0:T(8,128)S(1)}, u32[]{:S(2)}, u32[]{:S(2)}) collective-permute-start(f32[144,512]{1,0:T(8,128)S(1)} %select_bitcast_fusion), channel_id=1, source_target_pairs={{0,128},{128,0},{1,129},{129,1},{2,130},{130,2},{3,131},{131,3},{4... | collective-permute-start | bytes 884744 | tf_op jit(solution)/shard_map/ppermute | solution.py:91
Sparse Core Ops, SparseCore 0:
  21.2 96.9 all-gather.1

commit v6 on v5

--- a/solution.py
+++ b/solution.py
@@ -84,10 +84,11 @@
     )
     full = full.astype(jnp.bfloat16).reshape(n_zl, n_plane, -1, full.shape[1])
     shares = lax.all_to_all(full.transpose(1, 0, 2, 3), PLANE, 0, 0, tiled=True)
+    d_attn = jnp.dot(weighted, piece, preferred_element_type=jnp.float32).astype(jnp.bfloat16)
+    shares, d_attn = lax.optimization_barrier((shares, d_attn))
     plane_sum = jnp.sum(shares.astype(jnp.float32), axis=0)
     mine = jnp.where(zl == 0, plane_sum[0], plane_sum[1])
     theirs = jnp.where(zl == 0, plane_sum[1], plane_sum[0])
-    d_attn = jnp.dot(weighted, piece, preferred_element_type=jnp.float32).astype(jnp.bfloat16)
     o_grad = (mine + lax.ppermute(theirs, "zl", swap)) / total_resp
     return (d_attn, o_grad)
 

time: 232 us -> 230 us (level)
    ppermute x1, waiting for transfers between devices: 0.01 us -> 6.32 us  [shards(): o_grad = (mine + lax.ppermute(theirs, 'zl', swap)) / total_resp]
    all_to_all x1, waiting for transfers between devices: 64.8 us -> 58.5 us  [shards(): shares = lax.all_to_all(full.transpose(1, 0, 2, 3), PLANE, 0, 0, tiled=True)]
    all_to_all x1, local copies, waits for them, and re-layouts: 4.96 us -> 2.64 us  [shards(): piece = lax.all_to_all(copies, PLANE, 0, 0, tiled=True)]
  transfers between devices with their start and end apart: 8 -> 8, of which waited for: 6 -> 7; matrix products, arithmetic and copies ran while one was open for 18% -> 17% of each run, Pallas kernels for 0% -> 0%
where the time goes in v6:
time: 230 us; the launch traced here: 227 us
  waiting for transfers between devices  128 us (56%)
  starting transfers between devices  23.8 us (10%)
  matrix products  18.6 us (8%)
  blocking collectives  18.3 us (8%)
  local copies, waits for them, and re-layouts  18.2 us (8%)
  between operations  14.3 us (6%)
  other arithmetic  5.94 us (3%)
    all_to_all x1, waiting for transfers between devices, shards(): shares = lax.all_to_all(full.transpose(1, 0, 2, 3), PLANE, 0, 0, tiled=True)  58.5 us
    all_gather x1, waiting for transfers between devices, shards(): features = lax.all_gather(grad_out, TP, axis=1, tiled=True)  21.6 us
    psum x1, blocking collectives, shards(): logit = lax.psum(partial_logit, TP)  18.3 us
    all_to_all x1, waiting for transfers between devices, shards(): proj = jnp.sum(lax.all_to_all(part, PLANE, 0, 0, tiled=True), axis=0)  17.2 us
    ppermute x1, waiting for transfers between devices, shards(): w_other = lax.ppermute(w_out, 'zl', swap)  11.7 us
    dot_general x1, matrix products, shards(): lax.dot_general(weighted, attn_out, (((0,), (0,)), ((), ())), preferred_e...  9.05 us
    dot_general x1, matrix products, shards(): jnp.dot(weighted, piece, preferred_element_type=jnp.float32)  8.85 us
    all_to_all x1, waiting for transfers between devices, shards(): lax.all_to_all(cols, PLANE, 0, 0, tiled=True)  8.69 us
  transfers between devices with their start and end apart: 8, of which 7 were waited for; matrix products, arithmetic and copies ran while one was open for 17% of the time, Pallas kernels for 0%

profile of v6, /device:TPU:96, one launch (start us, length us, event | category | flops | bytes accessed | tf_op | source)
XLA Modules:
  0.0 226.6 jit_solution(13292656224055831891)
XLA Ops:
  7.2 0.2 collective-permute-start.1
  7.4 1.9 collective-permute-start
  9.3 11.7 %collective-permute-done = bf16[144,512]{1,0:T(8,128)(2,1)S(1)} collective-permute-done((bf16[144,512]{1,0:T(8,128)(2,1)}, bf16[144,512]{1,0:T(8,128)(2,1)S(1)}, u32[]{:S(2)}, u32[]{:S(2)}) %collective-permute-start) | collective-permute-done | bytes 147488 | tf_op jit(solution)/shard_map/ppermute | solution.py:28
  21.0 1.3 reshape.155
  22.4 0.9 copy.25
  23.3 7.0 %all-to-all-start = ((bf16[16,16,2,144]{3,2,1,0:T(2,128)(2,1)}), bf16[16,16,2,144]{3,2,1,0:T(2,128)(2,1)S(1)}, u32[]{:S(2)}, u32[]{:S(2)}) async-start(bf16[16,16,2,144]{3,2,1,0:T(2,128)(2,1)} %bitcast.46), calls=%async_computation | async-start | bytes 524288 | tf_op jit(solution)/shard_map/all_to_all | solution.py:43
  30.4 8.7 %all-to-all-done = bf16[16,16,2,144]{3,2,1,0:T(2,128)(2,1)S(1)} async-done(((bf16[16,16,2,144]{3,2,1,0:T(2,128)(2,1)}), bf16[16,16,2,144]{3,2,1,0:T(2,128)(2,1)S(1)}, u32[]{:S(2)}, u32[]{:S(2)}) %all-to-all-start) | async-done | bytes 147488 | tf_op jit(solution)/shard_map/all_to_all | solution.py:43
  39.0 0.2 reshape.156
  39.2 1.3 maximum_select_fusion
  40.6 0.4 convolution_bitcast_fusion
  40.9 0.3 convolution_bitcast_fusion.1
  41.3 0.1 pad_maximum_fusion
  41.4 1.4 copy.19
  42.7 3.7 %all-to-all-start.1 = ((f32[16,16,1152]{2,1,0:T(8,128)}), f32[16,16,1152]{2,1,0:T(8,128)S(1)}, u32[]{:S(2)}, u32[]{:S(2)}) async-start(f32[16,16,1152]{2,1,0:T(8,128)} %bitcast.6), calls=%async_computation.1 | async-start | bytes 2359296 | tf_op jit(solution)/shard_map/all_to_all | solution.py:52
  46.5 17.2 %all-to-all-done.1 = f32[16,16,1152]{2,1,0:T(8,128)S(1)} async-done(((f32[16,16,1152]{2,1,0:T(8,128)}), f32[16,16,1152]{2,1,0:T(8,128)S(1)}, u32[]{:S(2)}, u32[]{:S(2)}) %all-to-all-start.1) | async-done | bytes 1179680 | tf_op jit(solution)/shard_map/all_to_all | solution.py:52
  63.7 2.7 %broadcast_in_dim.4 = bf16[16,2,144,512]{3,2,1,0:T(8,128)(2,1)} broadcast(bf16[2,144,512]{2,1,0:T(8,128)(2,1)S(1)} %maximum_select_fusion.1), dimensions={1,2,3} | broadcast | bytes 5013504 | tf_op jit(solution)/shard_map/broadcast_in_dim | solution.py:33
  66.3 4.7 %all-to-all-start.3 = ((bf16[16,2,144,512]{3,2,1,0:T(8,128)(2,1)}), bf16[16,2,144,512]{3,2,1,0:T(8,128)(2,1)}, u32[]{:S(2)}, u32[]{:S(2)}) async-start(bf16[16,2,144,512]{3,2,1,0:T(8,128)(2,1)} %broadcast_in_dim.4), calls=%async_computation.3 | async-start | bytes 9437184 | tf_op jit(solution)/shard_map/all_to_all | solution.py:34
  71.1 0.1 reshape.202
  71.2 2.0 gather_fusion.2
  73.2 0.1 reshape.205
  73.3 0.1 reshape.207
  73.4 2.0 gather_fusion.3
  75.4 0.1 reshape.210
  75.5 0.1 fusion.15
  75.5 0.1 reshape.159
  75.6 0.1 reshape.158
  75.8 0.1 fusion.18
  75.9 0.8 gather_fusion.1
  76.7 0.8 gather_fusion
  77.5 0.2 fusion.13
  77.7 0.1 reduce_sum.58
  77.8 18.3 %psum.7 = f32[2,56]{1,0:T(2,128)S(1)} all-reduce(f32[2,56]{1,0:T(2,128)S(1)} %reduce_sum.58), channel_id=1, replica_groups=mesh['zl'=2,'y'=4,'x'=4,'zh'=4,'c'=2] {'zh','c'}, use_global_device_ids=true, to_apply=%region_2.4 | all-reduce | flops 112 | bytes 896 | tf_op jit(solution)/shard_map/psum | solution.py:62
  96.1 0.1 add_reduce_fusion.1
  96.2 0.1 select_reduce_fusion
  96.3 0.1 mul.106
  96.4 0.1 mul.108
  96.6 21.6 %all-gather.2.cloned.1.call-done = bf16[1024,4608]{0,1:T(8,128)(2,1)} async-done(((bf16[1024,576]{0,1:T(8,128)(2,1)}), bf16[1024,4608]{0,1:T(8,128)(2,1)}) %all-gather.2.cloned.1.call-update) | async-done | bytes 9437200 | tf_op jit(solution)/shard_map/all_gather | solution.py:31
  118.1 9.1 %fusion.2 = bf16[4608,512]{1,0:T(8,128)(2,1)S(1)} fusion(bf16[1024,512]{1,0:T(8,128)(2,1)S(1)} %copy-done, bf16[1024,4608]{0,1:T(8,128)(2,1)} %all-gather.2.cloned.1.call-done, f32[1024]{0:T(1024)S(1)} %mul.109), kind=kOutput, calls=%fused_computation.8 | convolution fusion | flops 4848353280 | bytes 15208448 | tf_op jit(solution)/shard_map/dot_general | solution.py:82
  127.2 2.5 %copy.24 = bf16[2,16,144,512]{3,2,0,1:T(8,128)(2,1)} copy(bf16[2,16,144,512]{3,2,1,0:T(8,128)(2,1)S(1)} %bitcast.49) | data formatting | bytes 9437184 | tf_op jit(solution)/shard_map/reshape | solution.py:85
  129.7 3.5 %all-to-all-done.3 = bf16[16,2,144,512]{3,2,1,0:T(8,128)(2,1)} async-done(((bf16[16,2,144,512]{3,2,1,0:T(8,128)(2,1)}), bf16[16,2,144,512]{3,2,1,0:T(8,128)(2,1)}, u32[]{:S(2)}, u32[]{:S(2)}) %all-to-all-start.3) | async-done | bytes 4718624 | tf_op jit(solution)/shard_map/all_to_all | solution.py:34
  133.3 4.7 %all-to-all-start.2 = ((bf16[16,2,144,512]{3,2,1,0:T(8,128)(2,1)}), bf16[16,2,144,512]{3,2,1,0:T(8,128)(2,1)}, u32[]{:S(2)}, u32[]{:S(2)}) async-start(bf16[16,2,144,512]{3,2,1,0:T(8,128)(2,1)} %bitcast.47), calls=%async_computation.2 | async-start | bytes 9437184 | tf_op jit(solution)/shard_map/all_to_all | solution.py:86
  138.0 2.6 %copy.21 = bf16[16,2,144,512]{3,2,0,1:T(8,128)(2,1)S(1)} copy(bf16[16,2,144,512]{3,2,1,0:T(8,128)(2,1)} %all-to-all-done.3) | data formatting | bytes 9437184 | tf_op jit(solution)/shard_map/all_to_all | solution.py:34
  140.7 8.8 %fusion.3 = bf16[1024,512]{1,0:T(8,128)(2,1)} fusion(bf16[4608,512]{1,0:T(8,128)(2,1)S(1)} %bitcast.48, bf16[1024,4608]{0,1:T(8,128)(2,1)} %all-gather.2.cloned.1.call-done, f32[1024]{0:T(1024)S(1)} %mul.109), kind=kOutput, calls=%fused_computation.10 | convolution fusion | flops 4846518272 | bytes 15208448 | tf_op jit(solution)/shard_map/dot_general | solution.py:87
  149.5 58.5 %all-to-all-done.2 = bf16[16,2,144,512]{3,2,1,0:T(8,128)(2,1)} async-done(((bf16[16,2,144,512]{3,2,1,0:T(8,128)(2,1)}), bf16[16,2,144,512]{3,2,1,0:T(8,128)(2,1)}, u32[]{:S(2)}, u32[]{:S(2)}) %all-to-all-start.2) | async-done | bytes 4718624 | tf_op jit(solution)/shard_map/all_to_all | solution.py:86
  208.1 3.1 %convert_reduce_fusion = f32[2,144,512]{2,1,0:T(8,128)S(1)} fusion(bf16[16,2,144,512]{3,2,1,0:T(8,128)(2,1)} %all-to-all-done.2), kind=kLoop, calls=%fused_computation.5 | loop fusion | flops 4571136 | bytes 5308416 | tf_op jit(solution)/shard_map/reduce_sum | solution.py:89
  211.2 1.5 collective-permute-start.2
  212.7 6.3 %collective-permute-done.2 = f32[144,512]{1,0:T(8,128)S(1)} collective-permute-done((f32[144,512]{1,0:T(8,128)S(1)}, f32[144,512]{1,0:T(8,128)S(1)}, u32[]{:S(2)}, u32[]{:S(2)}) %collective-permute-start.2) | collective-permute-done | bytes 294944 | tf_op jit(solution)/shard_map/ppermute | solution.py:92
  219.0 0.8 fusion.4
  (33 shorter events, 0.4 us)
Async XLA Ops:
  7.2 111.0 %copy-start = (bf16[1024,512]{1,0:T(8,128)(2,1)S(1)}, bf16[1024,512]{1,0:T(8,128)(2,1)}, u32[]{:S(2)}) copy-start(bf16[1024,512]{1,0:T(8,128)(2,1)} %param.19) | copy-start | bytes 3145732
  7.2 111.0 %all-gather.2.cloned.1.call-start = ((), (), s32[]{:S(2)}) async-start(), calls=%async_computation.4 | async-start | bytes 10616832 | tf_op jit(solution)/shard_map/all_gather | solution.py:31
  7.2 13.8 %collective-permute-start.1 = (bf16[2,144,576]{2,1,0:T(8,128)(2,1)}, bf16[2,144,576]{2,1,0:T(8,128)(2,1)S(1)}, u32[]{:S(2)}, u32[]{:S(2)}) collective-permute-start(bf16[2,144,576]{2,1,0:T(8,128)(2,1)} %param.15), channel_id=1, source_target_pairs={{0,128},{128,0},{1,129},{129,1},{2,130},{130,2},{3,131},{131,3},{4... | collective-permute-start | bytes 995336 | tf_op jit(solution)/shard_map/ppermute | solution.py:29
  7.4 13.6 %collective-permute-start = (bf16[144,512]{1,0:T(8,128)(2,1)}, bf16[144,512]{1,0:T(8,128)(2,1)S(1)}, u32[]{:S(2)}, u32[]{:S(2)}) collective-permute-start(bf16[144,512]{1,0:T(8,128)(2,1)} %param.21), channel_id=1, source_target_pairs={{0,128},{128,0},{1,129},{129,1},{2,130},{130,2},{3,131},{131,3},{4... | collective-permute-start | bytes 442376 | tf_op jit(solution)/shard_map/ppermute | solution.py:28
  23.3 15.7 %all-to-all-start = ((bf16[16,16,2,144]{3,2,1,0:T(2,128)(2,1)}), bf16[16,16,2,144]{3,2,1,0:T(2,128)(2,1)S(1)}, u32[]{:S(2)}, u32[]{:S(2)}) async-start(bf16[16,16,2,144]{3,2,1,0:T(2,128)(2,1)} %bitcast.46), calls=%async_computation | async-start | bytes 524288 | tf_op jit(solution)/shard_map/all_to_all | solution.py:43
  40.5 5.9 %copy-start.5 = (s32[2,56,2]{1,2,0:T(2,128)S(1)}, s32[2,56,2]{1,2,0:T(2,128)}, u32[]{:S(2)}) copy-start(s32[2,56,2]{1,2,0:T(2,128)} %param.14) | copy-start | bytes 2692
  40.5 5.9 %copy-start.2 = (bf16[144,512]{1,0:T(8,128)(2,1)S(1)}, bf16[144,512]{1,0:T(8,128)(2,1)}, u32[]{:S(2)}) copy-start(bf16[144,512]{1,0:T(8,128)(2,1)} %param.21) | copy-start | bytes 442372
  42.7 20.9 %all-to-all-start.1 = ((f32[16,16,1152]{2,1,0:T(8,128)}), f32[16,16,1152]{2,1,0:T(8,128)S(1)}, u32[]{:S(2)}, u32[]{:S(2)}) async-start(f32[16,16,1152]{2,1,0:T(8,128)} %bitcast.6), calls=%async_computation.1 | async-start | bytes 2359296 | tf_op jit(solution)/shard_map/all_to_all | solution.py:52
  66.3 4.8 %copy-start.1 = (s32[2,8]{1,0:T(2,128)S(1)}, s32[2,8]{1,0:T(2,128)}, u32[]{:S(2)}) copy-start(s32[2,8]{1,0:T(2,128)} %param.13) | copy-start | bytes 196
  66.3 66.9 %all-to-all-start.3 = ((bf16[16,2,144,512]{3,2,1,0:T(8,128)(2,1)}), bf16[16,2,144,512]{3,2,1,0:T(8,128)(2,1)}, u32[]{:S(2)}, u32[]{:S(2)}) async-start(bf16[16,2,144,512]{3,2,1,0:T(8,128)(2,1)} %broadcast_in_dim.4), calls=%async_computation.3 | async-start | bytes 9437184 | tf_op jit(solution)/shard_map/all_to_all | solution.py:34
  71.0 6.4 %copy-start.3 = (f32[576]{0:T(1024)S(1)}, f32[576]{0:T(1024)}, u32[]{:S(2)}) copy-start(f32[576]{0:T(1024)} %param.17) | copy-start | bytes 6916
  71.0 6.4 %copy-start.4 = (f32[576]{0:T(1024)S(1)}, f32[576]{0:T(1024)}, u32[]{:S(2)}) copy-start(f32[576]{0:T(1024)} %param.16) | copy-start | bytes 6916
  71.1 25.3 %copy-start.6 = (f32[16]{0:T(128)S(1)}, f32[16]{0:T(128)}, u32[]{:S(2)}) copy-start(f32[16]{0:T(128)} %param.18) | copy-start | bytes 196
  133.3 74.8 %all-to-all-start.2 = ((bf16[16,2,144,512]{3,2,1,0:T(8,128)(2,1)}), bf16[16,2,144,512]{3,2,1,0:T(8,128)(2,1)}, u32[]{:S(2)}, u32[]{:S(2)}) async-start(bf16[16,2,144,512]{3,2,1,0:T(8,128)(2,1)} %bitcast.47), calls=%async_computation.2 | async-start | bytes 9437184 | tf_op jit(solution)/shard_map/all_to_all | solution.py:86
  211.2 7.8 %collective-permute-start.2 = (f32[144,512]{1,0:T(8,128)S(1)}, f32[144,512]{1,0:T(8,128)S(1)}, u32[]{:S(2)}, u32[]{:S(2)}) collective-permute-start(f32[144,512]{1,0:T(8,128)S(1)} %select_bitcast_fusion), channel_id=1, source_target_pairs={{0,128},{128,0},{1,129},{129,1},{2,130},{130,2},{3,131},{131,3},{4... | collective-permute-start | bytes 884744 | tf_op jit(solution)/shard_map/ppermute | solution.py:92
Sparse Core Ops, SparseCore 0:
  21.2 96.9 all-gather.1

commit v7 on v6

--- a/solution.py
+++ b/solution.py
@@ -83,13 +83,15 @@
         weighted, attn_out, (((0,), (0,)), ((), ())), preferred_element_type=jnp.float32
     )
     full = full.astype(jnp.bfloat16).reshape(n_zl, n_plane, -1, full.shape[1])
-    shares = lax.all_to_all(full.transpose(1, 0, 2, 3), PLANE, 0, 0, tiled=True)
+    first_half = jnp.where(zl == 0, full[1], full[0])
+    own_half = jnp.where(zl == 0, full[0], full[1])
+    theirs = jnp.sum(lax.all_to_all(first_half, PLANE, 0, 0, tiled=True).astype(jnp.float32), axis=0)
+    got = lax.ppermute(theirs, "zl", swap)
+    shares = lax.all_to_all(own_half, PLANE, 0, 0, tiled=True)
     d_attn = jnp.dot(weighted, piece, preferred_element_type=jnp.float32).astype(jnp.bfloat16)
     shares, d_attn = lax.optimization_barrier((shares, d_attn))
-    plane_sum = jnp.sum(shares.astype(jnp.float32), axis=0)
-    mine = jnp.where(zl == 0, plane_sum[0], plane_sum[1])
-    theirs = jnp.where(zl == 0, plane_sum[1], plane_sum[0])
-    o_grad = (mine + lax.ppermute(theirs, "zl", swap)) / total_resp
+    mine = jnp.sum(shares.astype(jnp.float32), axis=0)
+    o_grad = (mine + got) / total_resp
     return (d_attn, o_grad)
 
 

time: 230 us -> 217 us (0.943)
  waiting for transfers between devices: 128 us -> 81.8 us
  blocking collectives: 18.3 us -> 52.2 us
    all_to_all x1, waiting for transfers between devices: 58.5 us -> 18.3 us  [shards(): shares = lax.all_to_all(own_half, PLANE, 0, 0, tiled=True)]
    all_to_all x0 -> x1, blocking collectives: none -> 34.6 us  [shards(): lax.all_to_all(first_half, PLANE, 0, 0, tiled=True).astype(jnp.float32)]
    ppermute x1, waiting for transfers between devices: 6.32 us -> 0.01 us  [shards(): got = lax.ppermute(theirs, 'zl', swap)]
    all_gather x1, waiting for transfers between devices: 21.6 us -> 27.2 us  [shards(): features = lax.all_gather(grad_out, TP, axis=1, tiled=True)]
    all_to_all x1, waiting for transfers between devices: 17.2 us -> 12.5 us  [shards(): proj = jnp.sum(lax.all_to_all(part, PLANE, 0, 0, tiled=True), axis=0)]
    reshape x1 -> x0, local copies, waits for them, and re-layouts: 2.55 us -> none  [shards(): full = full.astype(jnp.bfloat16).reshape(n_zl, n_plane, -1, full.shape[1])]
  transfers between devices with their start and end apart: 8 -> 8, of which waited for: 7 -> 6; matrix products, arithmetic and copies ran while one was open for 17% -> 19% of each run, Pallas kernels for 0% -> 0%
where the time goes in v7:
time: 217 us; the launch traced here: 212 us
  waiting for transfers between devices  81.8 us (38%)
  blocking collectives  52.2 us (24%)
  starting transfers between devices  22 us (10%)
  matrix products  18.6 us (9%)
  local copies, waits for them, and re-layouts  16.8 us (8%)
  between operations  14.3 us (7%)
  other arithmetic  6.83 us (3%)
    all_to_all x1, blocking collectives, shards(): lax.all_to_all(first_half, PLANE, 0, 0, tiled=True).astype(jnp.float32)  34.6 us
    all_gather x1, waiting for transfers between devices, shards(): features = lax.all_gather(grad_out, TP, axis=1, tiled=True)  27.2 us
    all_to_all x1, waiting for transfers between devices, shards(): shares = lax.all_to_all(own_half, PLANE, 0, 0, tiled=True)  18.3 us
    psum x1, blocking collectives, shards(): logit = lax.psum(partial_logit, TP)  17.7 us
    all_to_all x1, waiting for transfers between devices, shards(): proj = jnp.sum(lax.all_to_all(part, PLANE, 0, 0, tiled=True), axis=0)  12.5 us
    ppermute x1, waiting for transfers between devices, shards(): w_other = lax.ppermute(w_out, 'zl', swap)  11.7 us
    dot_general x1, matrix products, shards(): lax.dot_general(weighted, attn_out, (((0,), (0,)), ((), ())), preferred_e...  9.03 us
    dot_general x1, matrix products, shards(): jnp.dot(weighted, piece, preferred_element_type=jnp.float32)  8.83 us
  transfers between devices with their start and end apart: 8, of which 6 were waited for; matrix products, arithmetic and copies ran while one was open for 19% of the time, Pallas kernels for 0%

profile of v7, /device:TPU:96, one launch (start us, length us, event | category | flops | bytes accessed | tf_op | source)
XLA Modules:
  0.0 212.4 jit_solution(15189924631160578669)
XLA Ops:
  7.2 0.2 collective-permute-start.1
  7.4 1.9 collective-permute-start
  9.3 11.7 %collective-permute-done = bf16[144,512]{1,0:T(8,128)(2,1)S(1)} collective-permute-done((bf16[144,512]{1,0:T(8,128)(2,1)}, bf16[144,512]{1,0:T(8,128)(2,1)S(1)}, u32[]{:S(2)}, u32[]{:S(2)}) %collective-permute-start) | collective-permute-done | bytes 147488 | tf_op jit(solution)/shard_map/ppermute | solution.py:28
  21.0 1.3 reshape.157
  22.4 0.9 copy.21
  23.3 7.0 %all-to-all-start = ((bf16[16,16,2,144]{3,2,1,0:T(2,128)(2,1)}), bf16[16,16,2,144]{3,2,1,0:T(2,128)(2,1)S(1)}, u32[]{:S(2)}, u32[]{:S(2)}) async-start(bf16[16,16,2,144]{3,2,1,0:T(2,128)(2,1)} %bitcast.38), calls=%async_computation | async-start | bytes 524288 | tf_op jit(solution)/shard_map/all_to_all | solution.py:43
  30.4 0.8 fusion.18
  31.1 7.9 %all-to-all-done = bf16[16,16,2,144]{3,2,1,0:T(2,128)(2,1)S(1)} async-done(((bf16[16,16,2,144]{3,2,1,0:T(2,128)(2,1)}), bf16[16,16,2,144]{3,2,1,0:T(2,128)(2,1)S(1)}, u32[]{:S(2)}, u32[]{:S(2)}) %all-to-all-start) | async-done | bytes 147488 | tf_op jit(solution)/shard_map/all_to_all | solution.py:43
  39.0 0.2 reshape.158
  39.2 1.3 maximum_select_fusion
  40.5 0.4 convolution_bitcast_fusion
  40.9 0.4 convolution_bitcast_fusion.1
  41.3 0.1 pad_maximum_fusion
  41.4 1.4 copy.18
  42.7 3.7 %all-to-all-start.1 = ((f32[16,16,1152]{2,1,0:T(8,128)}), f32[16,16,1152]{2,1,0:T(8,128)S(1)}, u32[]{:S(2)}, u32[]{:S(2)}) async-start(f32[16,16,1152]{2,1,0:T(8,128)} %bitcast.6), calls=%async_computation.1 | async-start | bytes 2359296 | tf_op jit(solution)/shard_map/all_to_all | solution.py:52
  46.4 0.1 reshape.203
  46.5 2.0 gather_fusion.2
  48.6 0.1 reshape.206
  48.6 0.1 reshape.208
  48.7 2.0 gather_fusion.3
  50.8 0.1 reshape.211
  50.9 0.1 reshape.161
  51.0 0.1 reshape.160
  51.1 12.5 %all-to-all-done.1 = f32[16,16,1152]{2,1,0:T(8,128)S(1)} async-done(((f32[16,16,1152]{2,1,0:T(8,128)}), f32[16,16,1152]{2,1,0:T(8,128)S(1)}, u32[]{:S(2)}, u32[]{:S(2)}) %all-to-all-start.1) | async-done | bytes 1179680 | tf_op jit(solution)/shard_map/all_to_all | solution.py:52
  63.7 2.6 %broadcast_in_dim.4 = bf16[16,2,144,512]{3,2,1,0:T(8,128)(2,1)} broadcast(bf16[2,144,512]{2,1,0:T(8,128)(2,1)S(1)} %maximum_select_fusion.1), dimensions={1,2,3} | broadcast | bytes 5013504 | tf_op jit(solution)/shard_map/broadcast_in_dim | solution.py:33
  66.3 4.6 %all-to-all-start.3 = ((bf16[16,2,144,512]{3,2,1,0:T(8,128)(2,1)}), bf16[16,2,144,512]{3,2,1,0:T(8,128)(2,1)}, u32[]{:S(2)}, u32[]{:S(2)}) async-start(bf16[16,2,144,512]{3,2,1,0:T(8,128)(2,1)} %broadcast_in_dim.4), calls=%async_computation.3 | async-start | bytes 9437184 | tf_op jit(solution)/shard_map/all_to_all | solution.py:34
  71.1 0.8 gather_fusion.1
  71.9 0.8 gather_fusion
  72.7 0.2 fusion.12
  72.9 0.1 reduce_sum.67
  73.0 17.7 %psum.7 = f32[2,56]{1,0:T(2,128)S(1)} all-reduce(f32[2,56]{1,0:T(2,128)S(1)} %reduce_sum.67), channel_id=1, replica_groups=mesh['zl'=2,'y'=4,'x'=4,'zh'=4,'c'=2] {'zh','c'}, use_global_device_ids=true, to_apply=%region_2.4 | all-reduce | flops 112 | bytes 896 | tf_op jit(solution)/shard_map/psum | solution.py:62
  90.7 0.1 add_reduce_fusion.1
  90.8 0.1 select_reduce_fusion
  90.9 0.1 mul.106
  91.1 27.2 %all-gather.2.cloned.1.call-done = bf16[1024,4608]{0,1:T(8,128)(2,1)} async-done(((bf16[1024,576]{0,1:T(8,128)(2,1)}), bf16[1024,4608]{0,1:T(8,128)(2,1)}) %all-gather.2.cloned.1.call-update) | async-done | bytes 9437200 | tf_op jit(solution)/shard_map/all_gather | solution.py:31
  118.3 9.0 %fusion.2 = bf16[4608,512]{1,0:T(8,128)(2,1)S(1)} fusion(bf16[1024,512]{1,0:T(8,128)(2,1)S(1)} %copy-done, bf16[1024,4608]{0,1:T(8,128)(2,1)} %all-gather.2.cloned.1.call-done, f32[1024]{0:T(1024)S(1)} %mul.109), kind=kOutput, calls=%fused_computation.7 | convolution fusion | flops 4848353280 | bytes 15208448 | tf_op jit(solution)/shard_map/dot_general | solution.py:82
  127.3 1.7 broadcast_select_fusion
  129.0 4.1 %all-to-all-done.3 = bf16[16,2,144,512]{3,2,1,0:T(8,128)(2,1)} async-done(((bf16[16,2,144,512]{3,2,1,0:T(8,128)(2,1)}), bf16[16,2,144,512]{3,2,1,0:T(8,128)(2,1)}, u32[]{:S(2)}, u32[]{:S(2)}) %all-to-all-start.3) | async-done | bytes 4718624 | tf_op jit(solution)/shard_map/all_to_all | solution.py:34
  133.1 34.6 %all_to_all.25 = bf16[16,144,512]{2,1,0:T(8,128)(2,1)} all-to-all(bf16[16,144,512]{2,1,0:T(8,128)(2,1)S(1)} %bitcast.40), channel_id=1, replica_groups=mesh['zl'=2,'y'=4,'x'=4,'zh'=4,'c'=2] {'y','x'}, dimensions={0} | all-to-all | bytes 4718592 | tf_op jit(solution)/shard_map/all_to_all | solution.py:88
  167.7 3.7 %all-to-all-start.2 = ((bf16[16,144,512]{2,1,0:T(8,128)(2,1)}), bf16[16,144,512]{2,1,0:T(8,128)(2,1)S(1)}, u32[]{:S(2)}, u32[]{:S(2)}) async-start(bf16[16,144,512]{2,1,0:T(8,128)(2,1)} %bitcast.39), calls=%async_computation.2 | async-start | bytes 4718592 | tf_op jit(solution)/shard_map/all_to_all | solution.py:90
  171.4 2.8 %copy.19 = bf16[16,2,144,512]{3,2,0,1:T(8,128)(2,1)S(1)} copy(bf16[16,2,144,512]{3,2,1,0:T(8,128)(2,1)} %all-to-all-done.3) | data formatting | bytes 9437184 | tf_op jit(solution)/shard_map/all_to_all | solution.py:34
  174.2 0.3 copy-done.2
  174.5 1.0 convert_reduce_fusion
  175.5 0.8 collective-permute-start.2
  176.3 8.8 %fusion.3 = bf16[1024,512]{1,0:T(8,128)(2,1)} fusion(bf16[4608,512]{1,0:T(8,128)(2,1)S(1)} %bitcast.41, bf16[1024,4608]{0,1:T(8,128)(2,1)} %all-gather.2.cloned.1.call-done, f32[1024]{0:T(1024)S(1)} %mul.109), kind=kOutput, calls=%fused_computation.12 | convolution fusion | flops 4846518272 | bytes 15208448 | tf_op jit(solution)/shard_map/dot_general | solution.py:91
  185.2 18.3 %all-to-all-done.2 = bf16[16,144,512]{2,1,0:T(8,128)(2,1)S(1)} async-done(((bf16[16,144,512]{2,1,0:T(8,128)(2,1)}), bf16[16,144,512]{2,1,0:T(8,128)(2,1)S(1)}, u32[]{:S(2)}, u32[]{:S(2)}) %all-to-all-start.2) | async-done | bytes 2359328 | tf_op jit(solution)/shard_map/all_to_all | solution.py:90
  203.5 0.3 convert_reduce_fusion.1
  203.8 1.7 add_multiply_fusion
  (34 shorter events, 0.6 us)
Async XLA Ops:
  7.2 111.1 %copy-start = (bf16[1024,512]{1,0:T(8,128)(2,1)S(1)}, bf16[1024,512]{1,0:T(8,128)(2,1)}, u32[]{:S(2)}) copy-start(bf16[1024,512]{1,0:T(8,128)(2,1)} %param.19) | copy-start | bytes 3145732
  7.2 111.1 %all-gather.2.cloned.1.call-start = ((), (), s32[]{:S(2)}) async-start(), calls=%async_computation.5 | async-start | bytes 10616832 | tf_op jit(solution)/shard_map/all_gather | solution.py:31
  7.2 13.8 %collective-permute-start.1 = (bf16[2,144,576]{2,1,0:T(8,128)(2,1)}, bf16[2,144,576]{2,1,0:T(8,128)(2,1)S(1)}, u32[]{:S(2)}, u32[]{:S(2)}) collective-permute-start(bf16[2,144,576]{2,1,0:T(8,128)(2,1)} %param.15), channel_id=1, source_target_pairs={{0,128},{128,0},{1,129},{129,1},{2,130},{130,2},{3,131},{131,3},{4... | collective-permute-start | bytes 995336 | tf_op jit(solution)/shard_map/ppermute | solution.py:29
  7.4 13.6 %collective-permute-start = (bf16[144,512]{1,0:T(8,128)(2,1)}, bf16[144,512]{1,0:T(8,128)(2,1)S(1)}, u32[]{:S(2)}, u32[]{:S(2)}) collective-permute-start(bf16[144,512]{1,0:T(8,128)(2,1)} %param.21), channel_id=1, source_target_pairs={{0,128},{128,0},{1,129},{129,1},{2,130},{130,2},{3,131},{131,3},{4... | collective-permute-start | bytes 442376 | tf_op jit(solution)/shard_map/ppermute | solution.py:28
  23.3 15.7 %all-to-all-start = ((bf16[16,16,2,144]{3,2,1,0:T(2,128)(2,1)}), bf16[16,16,2,144]{3,2,1,0:T(2,128)(2,1)S(1)}, u32[]{:S(2)}, u32[]{:S(2)}) async-start(bf16[16,16,2,144]{3,2,1,0:T(2,128)(2,1)} %bitcast.38), calls=%async_computation | async-start | bytes 524288 | tf_op jit(solution)/shard_map/all_to_all | solution.py:43
  40.5 6.0 %copy-start.1 = (s32[2,8]{1,0:T(2,128)S(1)}, s32[2,8]{1,0:T(2,128)}, u32[]{:S(2)}) copy-start(s32[2,8]{1,0:T(2,128)} %param.13) | copy-start | bytes 196
  41.3 9.8 %copy-start.3 = (bf16[144,512]{1,0:T(8,128)(2,1)S(1)}, bf16[144,512]{1,0:T(8,128)(2,1)}, u32[]{:S(2)}) copy-start(bf16[144,512]{1,0:T(8,128)(2,1)} %param.21) | copy-start | bytes 442372
  42.7 20.9 %all-to-all-start.1 = ((f32[16,16,1152]{2,1,0:T(8,128)}), f32[16,16,1152]{2,1,0:T(8,128)S(1)}, u32[]{:S(2)}, u32[]{:S(2)}) async-start(f32[16,16,1152]{2,1,0:T(8,128)} %bitcast.6), calls=%async_computation.1 | async-start | bytes 2359296 | tf_op jit(solution)/shard_map/all_to_all | solution.py:52
  66.3 66.8 %all-to-all-start.3 = ((bf16[16,2,144,512]{3,2,1,0:T(8,128)(2,1)}), bf16[16,2,144,512]{3,2,1,0:T(8,128)(2,1)}, u32[]{:S(2)}, u32[]{:S(2)}) async-start(bf16[16,2,144,512]{3,2,1,0:T(8,128)(2,1)} %broadcast_in_dim.4), calls=%async_computation.3 | async-start | bytes 9437184 | tf_op jit(solution)/shard_map/all_to_all | solution.py:34
  70.9 1.8 copy-start.4
  70.9 1.8 copy-start.5
  70.9 20.0 %copy-start.6 = (f32[16]{0:T(128)S(1)}, f32[16]{0:T(128)}, u32[]{:S(2)}) copy-start(f32[16]{0:T(128)} %param.18) | copy-start | bytes 196
  167.7 35.8 %all-to-all-start.2 = ((bf16[16,144,512]{2,1,0:T(8,128)(2,1)}), bf16[16,144,512]{2,1,0:T(8,128)(2,1)S(1)}, u32[]{:S(2)}, u32[]{:S(2)}) async-start(bf16[16,144,512]{2,1,0:T(8,128)(2,1)} %bitcast.39), calls=%async_computation.2 | async-start | bytes 4718592 | tf_op jit(solution)/shard_map/all_to_all | solution.py:90
  171.4 3.1 %copy-start.2 = (bf16[16,144,512]{2,1,0:T(8,128)(2,1)S(1)}, bf16[16,144,512]{2,1,0:T(8,128)(2,1)}, u32[]{:S(2)}) copy-start(bf16[16,144,512]{2,1,0:T(8,128)(2,1)} %all_to_all.25) | copy-start | bytes 7077892
  175.5 28.3 %collective-permute-start.2 = (f32[144,512]{1,0:T(8,128)}, f32[144,512]{1,0:T(8,128)}, u32[]{:S(2)}, u32[]{:S(2)}) collective-permute-start(f32[144,512]{1,0:T(8,128)} %convert_reduce_fusion), channel_id=1, source_target_pairs={{0,128},{128,0},{1,129},{129,1},{2,130},{130,2},{3,131},{131,3},{4... | collective-permute-start | bytes 884744 | tf_op jit(solution)/shard_map/ppermute | solution.py:89
Sparse Core Ops, SparseCore 0:
  21.2 97.0 all-gather.1

commit v8 on v7

--- a/solution.py
+++ b/solution.py
@@ -25,10 +25,9 @@
     n_plane = lax.axis_size(PLANE)
     zl = lax.axis_index("zl")
     swap = [(k, (k + 1) % n_zl) for k in range(n_zl)]
+    features = lax.all_gather(grad_out, TP, axis=1, tiled=True)
     w_other = lax.ppermute(w_out, "zl", swap)
     other = lax.ppermute(pref_weight, "zl", swap)
-    grad_out, w_other, other = lax.optimization_barrier((grad_out, w_other, other))
-    features = lax.all_gather(grad_out, TP, axis=1, tiled=True)
     w_pair = jnp.where(zl == 0, jnp.stack([w_out, w_other]), jnp.stack([w_other, w_out]))
     copies = jnp.broadcast_to(w_pair[None], (n_plane,) + w_pair.shape)
     piece = lax.all_to_all(copies, PLANE, 0, 0, tiled=True)

time: 217 us -> 203 us (0.935)
  the two profiles are of different devices: /device:TPU:96 before, /device:TPU:32 now
where the time goes in v8:
time: 203 us; the launch traced here: 202 us
  waiting for transfers between devices  68.9 us (34%)
  blocking collectives  55.6 us (27%)
  starting transfers between devices  21.3 us (10%)
  matrix products  18.6 us (9%)
  local copies, waits for them, and re-layouts  16.8 us (8%)
  between operations  14.3 us (7%)
  other arithmetic  7.05 us (3%)
    all_to_all x1, blocking collectives, shards(): lax.all_to_all(first_half, PLANE, 0, 0, tiled=True).astype(jnp.float32)  35.5 us
    all_gather x1, waiting for transfers between devices, shards(): features = lax.all_gather(grad_out, TP, axis=1, tiled=True)  27.5 us
    psum x1, blocking collectives, shards(): logit = lax.psum(partial_logit, TP)  20.2 us
    all_to_all x1, waiting for transfers between devices, shards(): shares = lax.all_to_all(own_half, PLANE, 0, 0, tiled=True)  17.9 us
    all_to_all x1, waiting for transfers between devices, shards(): proj = jnp.sum(lax.all_to_all(part, PLANE, 0, 0, tiled=True), axis=0)  12.9 us
    dot_general x1, matrix products, shards(): lax.dot_general(weighted, attn_out, (((0,), (0,)), ((), ())), preferred_e...  9.03 us
    dot_general x1, matrix products, shards(): jnp.dot(weighted, piece, preferred_element_type=jnp.float32)  8.83 us
    all_to_all x1, waiting for transfers between devices, shards(): lax.all_to_all(cols, PLANE, 0, 0, tiled=True)  5.93 us
  transfers between devices with their start and end apart: 8, of which 5 were waited for; matrix products, arithmetic and copies ran while one was open for 20% of the time, Pallas kernels for 0%

profile of v8, /device:TPU:32, one launch (start us, length us, event | category | flops | bytes accessed | tf_op | source)
XLA Modules:
  0.0 202.5 jit_solution(12671128724214614446)
XLA Ops:
  7.2 0.7 all-gather.2.cloned.1.call-update
  7.9 1.9 collective-permute-start
  9.8 1.3 reshape.157
  11.1 0.9 copy.21
  12.1 5.3 %all-to-all-start = ((bf16[16,16,2,144]{3,2,1,0:T(2,128)(2,1)}), bf16[16,16,2,144]{3,2,1,0:T(2,128)(2,1)S(1)}, u32[]{:S(2)}, u32[]{:S(2)}) async-start(bf16[16,16,2,144]{3,2,1,0:T(2,128)(2,1)} %bitcast.38), calls=%async_computation | async-start | bytes 524288 | tf_op jit(solution)/shard_map/all_to_all | solution.py:42
  17.4 2.0 collective-permute-start.1
  19.4 0.8 fusion.18
  20.2 5.9 %all-to-all-done = bf16[16,16,2,144]{3,2,1,0:T(2,128)(2,1)S(1)} async-done(((bf16[16,16,2,144]{3,2,1,0:T(2,128)(2,1)}), bf16[16,16,2,144]{3,2,1,0:T(2,128)(2,1)S(1)}, u32[]{:S(2)}, u32[]{:S(2)}) %all-to-all-start) | async-done | bytes 147488 | tf_op jit(solution)/shard_map/all_to_all | solution.py:42
  26.1 0.2 reshape.158
  26.3 1.5 maximum_select_fusion
  27.8 0.4 convolution_bitcast_fusion
  28.2 0.4 convolution_bitcast_fusion.1
  28.6 0.1 pad_maximum_fusion
  28.7 1.4 copy.18
  30.0 3.7 %all-to-all-start.1 = ((f32[16,16,1152]{2,1,0:T(8,128)}), f32[16,16,1152]{2,1,0:T(8,128)S(1)}, u32[]{:S(2)}, u32[]{:S(2)}) async-start(f32[16,16,1152]{2,1,0:T(8,128)} %bitcast.6), calls=%async_computation.1 | async-start | bytes 2359296 | tf_op jit(solution)/shard_map/all_to_all | solution.py:51
  33.7 0.1 reshape.203
  33.8 2.0 gather_fusion.2
  35.9 0.1 reshape.206
  35.9 0.1 reshape.208
  36.0 2.0 gather_fusion.3
  38.1 0.1 reshape.211
  38.2 0.1 reshape.161
  38.3 0.1 reshape.160
  38.4 12.9 %all-to-all-done.1 = f32[16,16,1152]{2,1,0:T(8,128)S(1)} async-done(((f32[16,16,1152]{2,1,0:T(8,128)}), f32[16,16,1152]{2,1,0:T(8,128)S(1)}, u32[]{:S(2)}, u32[]{:S(2)}) %all-to-all-start.1) | async-done | bytes 1179680 | tf_op jit(solution)/shard_map/all_to_all | solution.py:51
  51.3 2.6 %broadcast_in_dim.4 = bf16[16,2,144,512]{3,2,1,0:T(8,128)(2,1)} broadcast(bf16[2,144,512]{2,1,0:T(8,128)(2,1)S(1)} %maximum_select_fusion.1), dimensions={1,2,3} | broadcast | bytes 5013504 | tf_op jit(solution)/shard_map/broadcast_in_dim | solution.py:32
  54.0 4.6 %all-to-all-start.3 = ((bf16[16,2,144,512]{3,2,1,0:T(8,128)(2,1)}), bf16[16,2,144,512]{3,2,1,0:T(8,128)(2,1)}, u32[]{:S(2)}, u32[]{:S(2)}) async-start(bf16[16,2,144,512]{3,2,1,0:T(8,128)(2,1)} %broadcast_in_dim.4), calls=%async_computation.3 | async-start | bytes 9437184 | tf_op jit(solution)/shard_map/all_to_all | solution.py:33
  58.7 0.1 fusion.17
  58.8 0.8 gather_fusion.1
  59.6 0.8 gather_fusion
  60.4 0.2 fusion.12
  60.6 0.1 reduce_sum.67
  60.7 20.2 %psum.7 = f32[2,56]{1,0:T(2,128)S(1)} all-reduce(f32[2,56]{1,0:T(2,128)S(1)} %reduce_sum.67), channel_id=1, replica_groups=mesh['zl'=2,'y'=4,'x'=4,'zh'=4,'c'=2] {'zh','c'}, use_global_device_ids=true, to_apply=%region_2.4 | all-reduce | flops 112 | bytes 896 | tf_op jit(solution)/shard_map/psum | solution.py:61
  80.8 0.1 add_reduce_fusion.1
  80.9 0.1 select_reduce_fusion
  81.0 0.1 mul.106
  81.3 27.5 %all-gather.2.cloned.1.call-done = bf16[1024,4608]{0,1:T(8,128)(2,1)} async-done(((bf16[1024,576]{0,1:T(8,128)(2,1)}), bf16[1024,4608]{0,1:T(8,128)(2,1)}) %all-gather.2.cloned.1.call-update) | async-done | bytes 9437200 | tf_op jit(solution)/shard_map/all_gather | solution.py:28
  108.8 9.0 %fusion.2 = bf16[4608,512]{1,0:T(8,128)(2,1)S(1)} fusion(bf16[1024,512]{1,0:T(8,128)(2,1)S(1)} %copy-done, bf16[1024,4608]{0,1:T(8,128)(2,1)} %all-gather.2.cloned.1.call-done, f32[1024]{0:T(1024)S(1)} %mul.109), kind=kOutput, calls=%fused_computation.7 | convolution fusion | flops 4848353280 | bytes 15208448 | tf_op jit(solution)/shard_map/dot_general | solution.py:81
  117.9 1.7 broadcast_select_fusion
  119.6 3.9 %all-to-all-done.3 = bf16[16,2,144,512]{3,2,1,0:T(8,128)(2,1)} async-done(((bf16[16,2,144,512]{3,2,1,0:T(8,128)(2,1)}), bf16[16,2,144,512]{3,2,1,0:T(8,128)(2,1)}, u32[]{:S(2)}, u32[]{:S(2)}) %all-to-all-start.3) | async-done | bytes 4718624 | tf_op jit(solution)/shard_map/all_to_all | solution.py:33
  123.4 35.5 %all_to_all.25 = bf16[16,144,512]{2,1,0:T(8,128)(2,1)} all-to-all(bf16[16,144,512]{2,1,0:T(8,128)(2,1)S(1)} %bitcast.40), channel_id=1, replica_groups=mesh['zl'=2,'y'=4,'x'=4,'zh'=4,'c'=2] {'y','x'}, dimensions={0} | all-to-all | bytes 4718592 | tf_op jit(solution)/shard_map/all_to_all | solution.py:87
  158.9 3.7 %all-to-all-start.2 = ((bf16[16,144,512]{2,1,0:T(8,128)(2,1)}), bf16[16,144,512]{2,1,0:T(8,128)(2,1)S(1)}, u32[]{:S(2)}, u32[]{:S(2)}) async-start(bf16[16,144,512]{2,1,0:T(8,128)(2,1)} %bitcast.39), calls=%async_computation.2 | async-start | bytes 4718592 | tf_op jit(solution)/shard_map/all_to_all | solution.py:89
  162.7 2.8 %copy.19 = bf16[16,2,144,512]{3,2,0,1:T(8,128)(2,1)S(1)} copy(bf16[16,2,144,512]{3,2,1,0:T(8,128)(2,1)} %all-to-all-done.3) | data formatting | bytes 9437184 | tf_op jit(solution)/shard_map/all_to_all | solution.py:33
  165.5 0.3 copy-done.2
  165.7 1.0 convert_reduce_fusion
  166.8 8.8 %fusion.3 = bf16[1024,512]{1,0:T(8,128)(2,1)} fusion(bf16[4608,512]{1,0:T(8,128)(2,1)S(1)} %bitcast.41, bf16[1024,4608]{0,1:T(8,128)(2,1)} %all-gather.2.cloned.1.call-done, f32[1024]{0:T(1024)S(1)} %mul.109), kind=kOutput, calls=%fused_computation.12 | convolution fusion | flops 4846518272 | bytes 15208448 | tf_op jit(solution)/shard_map/dot_general | solution.py:90
  175.6 17.9 %all-to-all-done.2 = bf16[16,144,512]{2,1,0:T(8,128)(2,1)S(1)} async-done(((bf16[16,144,512]{2,1,0:T(8,128)(2,1)}), bf16[16,144,512]{2,1,0:T(8,128)(2,1)S(1)}, u32[]{:S(2)}, u32[]{:S(2)}) %all-to-all-start.2) | async-done | bytes 2359328 | tf_op jit(solution)/shard_map/all_to_all | solution.py:89
  193.6 0.3 convert_reduce_fusion.1
  193.9 1.7 add_multiply_fusion
  (34 shorter events, 0.5 us)
Async XLA Ops:
  7.2 101.7 %copy-start = (bf16[1024,512]{1,0:T(8,128)(2,1)S(1)}, bf16[1024,512]{1,0:T(8,128)(2,1)}, u32[]{:S(2)}) copy-start(bf16[1024,512]{1,0:T(8,128)(2,1)} %param.19) | copy-start | bytes 3145732
  7.2 101.6 %all-gather.2.cloned.1.call-start = ((), (), s32[]{:S(2)}) async-start(), calls=%async_computation.5 | async-start | bytes 10616832 | tf_op jit(solution)/shard_map/all_gather | solution.py:28
  7.9 18.4 %collective-permute-start = (bf16[2,144,576]{2,1,0:T(8,128)(2,1)}, bf16[2,144,576]{2,1,0:T(8,128)(2,1)S(1)}, u32[]{:S(2)}, u32[]{:S(2)}) collective-permute-start(bf16[2,144,576]{2,1,0:T(8,128)(2,1)} %param.15), channel_id=1, source_target_pairs={{0,128},{128,0},{1,129},{129,1},{2,130},{130,2},{3,131},{131,3},{4... | collective-permute-start | bytes 995336 | tf_op jit(solution)/shard_map/ppermute | solution.py:30
  12.1 14.0 %all-to-all-start = ((bf16[16,16,2,144]{3,2,1,0:T(2,128)(2,1)}), bf16[16,16,2,144]{3,2,1,0:T(2,128)(2,1)S(1)}, u32[]{:S(2)}, u32[]{:S(2)}) async-start(bf16[16,16,2,144]{3,2,1,0:T(2,128)(2,1)} %bitcast.38), calls=%async_computation | async-start | bytes 524288 | tf_op jit(solution)/shard_map/all_to_all | solution.py:42
  17.4 21.0 %collective-permute-start.1 = (bf16[144,512]{1,0:T(8,128)(2,1)}, bf16[144,512]{1,0:T(8,128)(2,1)S(1)}, u32[]{:S(2)}, u32[]{:S(2)}) collective-permute-start(bf16[144,512]{1,0:T(8,128)(2,1)} %param.21), channel_id=1, source_target_pairs={{0,128},{128,0},{1,129},{129,1},{2,130},{130,2},{3,131},{131,3},{4... | collective-permute-start | bytes 442376 | tf_op jit(solution)/shard_map/ppermute | solution.py:29
  27.8 6.0 %copy-start.1 = (s32[2,8]{1,0:T(2,128)S(1)}, s32[2,8]{1,0:T(2,128)}, u32[]{:S(2)}) copy-start(s32[2,8]{1,0:T(2,128)} %param.13) | copy-start | bytes 196
  28.6 9.8 %copy-start.3 = (bf16[144,512]{1,0:T(8,128)(2,1)S(1)}, bf16[144,512]{1,0:T(8,128)(2,1)}, u32[]{:S(2)}) copy-start(bf16[144,512]{1,0:T(8,128)(2,1)} %param.21) | copy-start | bytes 442372
  30.0 21.3 %all-to-all-start.1 = ((f32[16,16,1152]{2,1,0:T(8,128)}), f32[16,16,1152]{2,1,0:T(8,128)S(1)}, u32[]{:S(2)}, u32[]{:S(2)}) async-start(f32[16,16,1152]{2,1,0:T(8,128)} %bitcast.6), calls=%async_computation.1 | async-start | bytes 2359296 | tf_op jit(solution)/shard_map/all_to_all | solution.py:51
  54.0 69.5 %all-to-all-start.3 = ((bf16[16,2,144,512]{3,2,1,0:T(8,128)(2,1)}), bf16[16,2,144,512]{3,2,1,0:T(8,128)(2,1)}, u32[]{:S(2)}, u32[]{:S(2)}) async-start(bf16[16,2,144,512]{3,2,1,0:T(8,128)(2,1)} %broadcast_in_dim.4), calls=%async_computation.3 | async-start | bytes 9437184 | tf_op jit(solution)/shard_map/all_to_all | solution.py:33
  58.5 1.8 copy-start.4
  58.6 1.8 copy-start.5
  58.6 22.6 %copy-start.6 = (f32[16]{0:T(128)S(1)}, f32[16]{0:T(128)}, u32[]{:S(2)}) copy-start(f32[16]{0:T(128)} %param.18) | copy-start | bytes 196
  158.9 34.6 %all-to-all-start.2 = ((bf16[16,144,512]{2,1,0:T(8,128)(2,1)}), bf16[16,144,512]{2,1,0:T(8,128)(2,1)S(1)}, u32[]{:S(2)}, u32[]{:S(2)}) async-start(bf16[16,144,512]{2,1,0:T(8,128)(2,1)} %bitcast.39), calls=%async_computation.2 | async-start | bytes 4718592 | tf_op jit(solution)/shard_map/all_to_all | solution.py:89
  162.7 3.1 %copy-start.2 = (bf16[16,144,512]{2,1,0:T(8,128)(2,1)S(1)}, bf16[16,144,512]{2,1,0:T(8,128)(2,1)}, u32[]{:S(2)}) copy-start(bf16[16,144,512]{2,1,0:T(8,128)(2,1)} %all_to_all.25) | copy-start | bytes 7077892
  166.8 27.1 %collective-permute-start.2 = (f32[144,512]{1,0:T(8,128)}, f32[144,512]{1,0:T(8,128)}, u32[]{:S(2)}, u32[]{:S(2)}) collective-permute-start(f32[144,512]{1,0:T(8,128)} %convert_reduce_fusion), channel_id=1, source_target_pairs={{0,128},{128,0},{1,129},{129,1},{2,130},{130,2},{3,131},{131,3},{4... | collective-permute-start | bytes 884744 | tf_op jit(solution)/shard_map/ppermute | solution.py:88
Sparse Core Ops, SparseCore 0:
  9.8 98.9 all-gather.1

commit v9 on v8

--- a/solution.py
+++ b/solution.py
@@ -26,12 +26,9 @@
     zl = lax.axis_index("zl")
     swap = [(k, (k + 1) % n_zl) for k in range(n_zl)]
     features = lax.all_gather(grad_out, TP, axis=1, tiled=True)
-    w_other = lax.ppermute(w_out, "zl", swap)
     other = lax.ppermute(pref_weight, "zl", swap)
-    w_pair = jnp.where(zl == 0, jnp.stack([w_out, w_other]), jnp.stack([w_other, w_out]))
-    copies = jnp.broadcast_to(w_pair[None], (n_plane,) + w_pair.shape)
-    piece = lax.all_to_all(copies, PLANE, 0, 0, tiled=True)
-    piece = piece.transpose(1, 0, 2, 3).reshape(-1, w_out.shape[1])
+    copies = jnp.broadcast_to(w_out[None], (n_plane,) + w_out.shape)
+    plane_w = lax.all_to_all(copies, PLANE, 0, 0, tiled=True).reshape(-1, w_out.shape[1])
 
     pair_w = jnp.where(
         zl == 0,
@@ -78,6 +75,13 @@
         .astype(jnp.bfloat16)
     )
     total_resp = resp_dev * n_dp
+    plane_w, features = lax.optimization_barrier((plane_w, features))
+    w_half = lax.ppermute(plane_w, "zl", swap)
+    piece = jnp.where(
+        zl == 0,
+        jnp.concatenate([plane_w, w_half], axis=0),
+        jnp.concatenate([w_half, plane_w], axis=0),
+    )
     full = lax.dot_general(
         weighted, attn_out, (((0,), (0,)), ((), ())), preferred_element_type=jnp.float32
     )

time: 203 us -> 224 us (1.10)
  the two profiles are of different devices: /device:TPU:32 before, /device:TPU:96 now
where the time goes in v9:
time: 224 us; the launch traced here: 223 us
  waiting for transfers between devices  110 us (49%)
  starting transfers between devices  31.5 us (14%)
  matrix products  22.2 us (10%)
  blocking collectives  21 us (9%)
  between operations  14.3 us (6%)
  local copies, waits for them, and re-layouts  14.1 us (6%)
  other arithmetic  9.44 us (4%)
    all_to_all x1, waiting for transfers between devices, shards(): lax.all_to_all(first_half, PLANE, 0, 0, tiled=True).astype(jnp.float32)  39.2 us
    ppermute x1, waiting for transfers between devices, shards(): other = lax.ppermute(pref_weight, 'zl', swap)  22.4 us
    psum x1, blocking collectives, shards(): logit = lax.psum(partial_logit, TP)  21 us
    all_to_all x1, waiting for transfers between devices, shards(): proj = jnp.sum(lax.all_to_all(part, PLANE, 0, 0, tiled=True), axis=0)  18.8 us
    all_to_all x1, waiting for transfers between devices, shards(): shares = lax.all_to_all(own_half, PLANE, 0, 0, tiled=True)  14.7 us
    dot_general x1, matrix products, shards(): jnp.dot(weighted, piece, preferred_element_type=jnp.float32)  12.5 us
    dot_general x1, matrix products, shards(): lax.dot_general(weighted, attn_out, (((0,), (0,)), ((), ())), preferred_e...  9.04 us
    all_to_all x1, starting transfers between devices, shards(): lax.all_to_all(first_half, PLANE, 0, 0, tiled=True).astype(jnp.float32)  7.95 us
  transfers between devices with their start and end apart: 9, of which 6 were waited for; matrix products, arithmetic and copies ran while one was open for 19% of the time, Pallas kernels for 0%

profile of v9, /device:TPU:96, one launch (start us, length us, event | category | flops | bytes accessed | tf_op | source)
XLA Modules:
  0.0 222.9 jit_solution(7646308260043725120)
XLA Ops:
  7.2 0.7 all-gather.2.cloned.1.call-update
  7.9 1.3 reshape.125
  9.2 0.9 copy.17
  10.2 7.0 %all-to-all-start = ((bf16[16,16,2,144]{3,2,1,0:T(2,128)(2,1)}), bf16[16,16,2,144]{3,2,1,0:T(2,128)(2,1)S(1)}, u32[]{:S(2)}, u32[]{:S(2)}) async-start(bf16[16,16,2,144]{3,2,1,0:T(2,128)(2,1)} %bitcast.33), calls=%async_computation | async-start | bytes 524288 | tf_op jit(solution)/shard_map/all_to_all | solution.py:39
  17.2 0.2 collective-permute-start
  17.4 0.8 fusion.25
  18.2 7.7 %all-to-all-done = bf16[16,16,2,144]{3,2,1,0:T(2,128)(2,1)S(1)} async-done(((bf16[16,16,2,144]{3,2,1,0:T(2,128)(2,1)}), bf16[16,16,2,144]{3,2,1,0:T(2,128)(2,1)S(1)}, u32[]{:S(2)}, u32[]{:S(2)}) %all-to-all-start) | async-done | bytes 147488 | tf_op jit(solution)/shard_map/all_to_all | solution.py:39
  25.9 0.2 reshape.126
  26.1 22.4 %collective-permute-done = bf16[2,144,576]{2,1,0:T(8,128)(2,1)S(1)} collective-permute-done((bf16[2,144,576]{2,1,0:T(8,128)(2,1)}, bf16[2,144,576]{2,1,0:T(8,128)(2,1)S(1)}, u32[]{:S(2)}, u32[]{:S(2)}) %collective-permute-start) | collective-permute-done | bytes 331808 | tf_op jit(solution)/shard_map/ppermute | solution.py:29
  48.4 1.3 maximum_select_fusion.4
  49.8 0.4 convolution_bitcast_fusion
  50.1 0.3 convolution_bitcast_fusion.1
  50.5 0.1 pad_maximum_fusion
  50.6 1.4 copy.15
  52.0 7.6 %all-to-all-start.1 = ((f32[16,16,1152]{2,1,0:T(8,128)}), f32[16,16,1152]{2,1,0:T(8,128)S(1)}, u32[]{:S(2)}, u32[]{:S(2)}) async-start(f32[16,16,1152]{2,1,0:T(8,128)} %bitcast.6), calls=%async_computation.1 | async-start | bytes 2359296 | tf_op jit(solution)/shard_map/all_to_all | solution.py:48
  59.6 0.1 reshape.171
  59.6 2.0 gather_fusion.2
  61.7 0.1 reshape.174
  61.8 0.1 reshape.176
  61.8 2.0 gather_fusion.3
  63.9 0.1 reshape.179
  64.0 0.1 reshape.129
  64.1 0.1 reshape.128
  64.2 18.8 %all-to-all-done.1 = f32[16,16,1152]{2,1,0:T(8,128)S(1)} async-done(((f32[16,16,1152]{2,1,0:T(8,128)}), f32[16,16,1152]{2,1,0:T(8,128)S(1)}, u32[]{:S(2)}, u32[]{:S(2)}) %all-to-all-start.1) | async-done | bytes 1179680 | tf_op jit(solution)/shard_map/all_to_all | solution.py:48
  83.1 1.6 broadcast_in_dim.4
  84.7 4.6 %all-to-all-start.3 = ((bf16[16,144,512]{2,1,0:T(8,128)(2,1)}), bf16[16,144,512]{2,1,0:T(8,128)(2,1)}, u32[]{:S(2)}, u32[]{:S(2)}) async-start(bf16[16,144,512]{2,1,0:T(8,128)(2,1)} %broadcast_in_dim.4), calls=%async_computation.3 | async-start | bytes 4718592 | tf_op jit(solution)/shard_map/all_to_all | solution.py:31
  89.4 0.1 fusion.24
  89.4 0.8 gather_fusion.1
  90.2 0.8 gather_fusion
  91.0 0.2 fusion.18
  91.3 0.1 reduce_sum.67
  91.3 21.0 %psum.7 = f32[2,56]{1,0:T(2,128)S(1)} all-reduce(f32[2,56]{1,0:T(2,128)S(1)} %reduce_sum.67), channel_id=1, replica_groups=mesh['zl'=2,'y'=4,'x'=4,'zh'=4,'c'=2] {'zh','c'}, use_global_device_ids=true, to_apply=%region_2.4 | all-reduce | flops 112 | bytes 896 | tf_op jit(solution)/shard_map/psum | solution.py:58
  112.3 0.1 add_reduce_fusion.1
  112.4 0.1 select_reduce_fusion
  112.5 0.1 mul.106
  112.8 9.0 %fusion.2 = bf16[4608,512]{1,0:T(8,128)(2,1)S(1)} fusion(bf16[1024,512]{1,0:T(8,128)(2,1)S(1)} %copy-done, bf16[1024,4608]{0,1:T(8,128)(2,1)} %all-gather.2.cloned.1.call-done, f32[1024]{0:T(1024)S(1)} %mul.109), kind=kOutput, calls=%fused_computation.7 | convolution fusion | flops 4848353280 | bytes 15208448 | tf_op jit(solution)/shard_map/dot_general | solution.py:85
  121.8 2.6 %broadcast_select_fusion = (bf16[2304,512]{1,0:T(8,128)(2,1)}, bf16[2304,512]{1,0:T(8,128)(2,1)}) fusion(pred[]{:T(512)S(6)} %eq.22, bf16[4608,512]{1,0:T(8,128)(2,1)S(1)} %fusion.2), kind=kLoop, calls=%fused_computation.17 | loop fusion | flops 2359296 | bytes 9437185 | tf_op jit(solution)/shard_map/jit(_where)/select_n | solution.py:89
  124.5 8.0 %all-to-all-start.4 = ((bf16[16,144,512]{2,1,0:T(8,128)(2,1)}), bf16[16,144,512]{2,1,0:T(8,128)(2,1)S(1)}, u32[]{:S(2)}, u32[]{:S(2)}) async-start(bf16[16,144,512]{2,1,0:T(8,128)(2,1)} %bitcast.35), calls=%async_computation.4 | async-start | bytes 4718592 | tf_op jit(solution)/shard_map/all_to_all | solution.py:91
  132.4 0.1 collective-permute-start.1
  132.5 39.2 %all-to-all-done.4 = bf16[16,144,512]{2,1,0:T(8,128)(2,1)S(1)} async-done(((bf16[16,144,512]{2,1,0:T(8,128)(2,1)}), bf16[16,144,512]{2,1,0:T(8,128)(2,1)S(1)}, u32[]{:S(2)}, u32[]{:S(2)}) %all-to-all-start.4) | async-done | bytes 2359328 | tf_op jit(solution)/shard_map/all_to_all | solution.py:91
  171.7 1.4 copy-done.2
  173.2 4.0 %all-to-all-start.2 = ((bf16[16,144,512]{2,1,0:T(8,128)(2,1)}), bf16[16,144,512]{2,1,0:T(8,128)(2,1)S(1)}, u32[]{:S(2)}, u32[]{:S(2)}) async-start(bf16[16,144,512]{2,1,0:T(8,128)(2,1)} %bitcast.34), calls=%async_computation.2 | async-start | bytes 4718592 | tf_op jit(solution)/shard_map/all_to_all | solution.py:93
  177.2 2.7 %convert_reduce_fusion = f32[144,512]{1,0:T(8,128)} fusion(bf16[16,144,512]{2,1,0:T(8,128)(2,1)} %copy-done.2), kind=kLoop, calls=%fused_computation.14 | loop fusion | flops 2285568 | bytes 2654208 | tf_op jit(solution)/shard_map/reduce_sum | solution.py:91
  179.9 7.0 %collective-permute-done.1 = bf16[2304,512]{1,0:T(8,128)(2,1)} collective-permute-done((bf16[2304,512]{1,0:T(8,128)(2,1)}, bf16[2304,512]{1,0:T(8,128)(2,1)}, u32[]{:S(2)}, u32[]{:S(2)}) %collective-permute-start.1) | collective-permute-done | bytes 2359328 | tf_op jit(solution)/shard_map/ppermute | solution.py:79
  186.9 12.5 %fusion.9 = bf16[1024,512]{1,0:T(8,128)(2,1)} fusion(bf16[2304,512]{1,0:T(8,128)(2,1)} %collective-permute-done.1, bf16[2304,512]{1,0:T(8,128)(2,1)} %bitcast.13, pred[]{:T(512)S(6)} %eq.22, bf16[1024,4608]{0,1:T(8,128)(2,1)} %all-gather.2.cloned.1.call-done, f32[1024]{0:T(1024)S(1)} %mul.109), kind=kOutput, calls=%fused_computation.19 | convolution fusion | flops 4867751936 | bytes 15208449 | tf_op jit(solution)/shard_map/dot_general | solution.py:94
  199.4 14.7 %all-to-all-done.2 = bf16[16,144,512]{2,1,0:T(8,128)(2,1)S(1)} async-done(((bf16[16,144,512]{2,1,0:T(8,128)(2,1)}), bf16[16,144,512]{2,1,0:T(8,128)(2,1)S(1)}, u32[]{:S(2)}, u32[]{:S(2)}) %all-to-all-start.2) | async-done | bytes 2359328 | tf_op jit(solution)/shard_map/all_to_all | solution.py:93
  214.0 0.3 convert_reduce_fusion.1
  214.4 1.7 add_multiply_fusion
  (33 shorter events, 0.4 us)
Async XLA Ops:
  7.2 105.6 %copy-start = (bf16[1024,512]{1,0:T(8,128)(2,1)S(1)}, bf16[1024,512]{1,0:T(8,128)(2,1)}, u32[]{:S(2)}) copy-start(bf16[1024,512]{1,0:T(8,128)(2,1)} %param.19) | copy-start | bytes 3145732
  7.2 105.6 %all-gather.2.cloned.1.call-start = ((), (), s32[]{:S(2)}) async-start(), calls=%async_computation.5 | async-start | bytes 10616832 | tf_op jit(solution)/shard_map/all_gather | solution.py:28
  10.2 15.7 %all-to-all-start = ((bf16[16,16,2,144]{3,2,1,0:T(2,128)(2,1)}), bf16[16,16,2,144]{3,2,1,0:T(2,128)(2,1)S(1)}, u32[]{:S(2)}, u32[]{:S(2)}) async-start(bf16[16,16,2,144]{3,2,1,0:T(2,128)(2,1)} %bitcast.33), calls=%async_computation | async-start | bytes 524288 | tf_op jit(solution)/shard_map/all_to_all | solution.py:39
  17.2 31.2 %collective-permute-start = (bf16[2,144,576]{2,1,0:T(8,128)(2,1)}, bf16[2,144,576]{2,1,0:T(8,128)(2,1)S(1)}, u32[]{:S(2)}, u32[]{:S(2)}) collective-permute-start(bf16[2,144,576]{2,1,0:T(8,128)(2,1)} %param.15), channel_id=1, source_target_pairs={{0,128},{128,0},{1,129},{129,1},{2,130},{130,2},{3,131},{131,3},{4... | collective-permute-start | bytes 995336 | tf_op jit(solution)/shard_map/ppermute | solution.py:29
  49.8 9.9 %copy-start.1 = (s32[2,8]{1,0:T(2,128)S(1)}, s32[2,8]{1,0:T(2,128)}, u32[]{:S(2)}) copy-start(s32[2,8]{1,0:T(2,128)} %param.13) | copy-start | bytes 196
  50.5 32.6 %copy-start.3 = (bf16[144,512]{1,0:T(8,128)(2,1)S(1)}, bf16[144,512]{1,0:T(8,128)(2,1)}, u32[]{:S(2)}) copy-start(bf16[144,512]{1,0:T(8,128)(2,1)} %param.21) | copy-start | bytes 442372
  52.0 31.1 %all-to-all-start.1 = ((f32[16,16,1152]{2,1,0:T(8,128)}), f32[16,16,1152]{2,1,0:T(8,128)S(1)}, u32[]{:S(2)}, u32[]{:S(2)}) async-start(f32[16,16,1152]{2,1,0:T(8,128)} %bitcast.6), calls=%async_computation.1 | async-start | bytes 2359296 | tf_op jit(solution)/shard_map/all_to_all | solution.py:48
  84.7 6.3 %copy-start.4 = (f32[576]{0:T(1024)S(1)}, f32[576]{0:T(1024)}, u32[]{:S(2)}) copy-start(f32[576]{0:T(1024)} %param.17) | copy-start | bytes 6916
  84.7 6.3 %copy-start.5 = (f32[576]{0:T(1024)S(1)}, f32[576]{0:T(1024)}, u32[]{:S(2)}) copy-start(f32[576]{0:T(1024)} %param.16) | copy-start | bytes 6916
  84.7 39.8 %all-to-all-start.3 = ((bf16[16,144,512]{2,1,0:T(8,128)(2,1)}), bf16[16,144,512]{2,1,0:T(8,128)(2,1)}, u32[]{:S(2)}, u32[]{:S(2)}) async-start(bf16[16,144,512]{2,1,0:T(8,128)(2,1)} %broadcast_in_dim.4), calls=%async_computation.3 | async-start | bytes 4718592 | tf_op jit(solution)/shard_map/all_to_all | solution.py:31
  89.3 23.3 %copy-start.6 = (f32[16]{0:T(128)S(1)}, f32[16]{0:T(128)}, u32[]{:S(2)}) copy-start(f32[16]{0:T(128)} %param.18) | copy-start | bytes 196
  124.5 47.3 %all-to-all-start.4 = ((bf16[16,144,512]{2,1,0:T(8,128)(2,1)}), bf16[16,144,512]{2,1,0:T(8,128)(2,1)S(1)}, u32[]{:S(2)}, u32[]{:S(2)}) async-start(bf16[16,144,512]{2,1,0:T(8,128)(2,1)} %bitcast.35), calls=%async_computation.4 | async-start | bytes 4718592 | tf_op jit(solution)/shard_map/all_to_all | solution.py:91
  132.4 54.5 %collective-permute-start.1 = (bf16[2304,512]{1,0:T(8,128)(2,1)}, bf16[2304,512]{1,0:T(8,128)(2,1)}, u32[]{:S(2)}, u32[]{:S(2)}) collective-permute-start(bf16[2304,512]{1,0:T(8,128)(2,1)} %bitcast.13), channel_id=1, source_target_pairs={{0,128},{128,0},{1,129},{129,1},{2,130},{130,2},{3,131},{131,3},{4... | collective-permute-start | bytes 7077896 | tf_op jit(solution)/shard_map/ppermute | solution.py:79
  171.7 1.4 copy-start.2
  173.2 40.9 %all-to-all-start.2 = ((bf16[16,144,512]{2,1,0:T(8,128)(2,1)}), bf16[16,144,512]{2,1,0:T(8,128)(2,1)S(1)}, u32[]{:S(2)}, u32[]{:S(2)}) async-start(bf16[16,144,512]{2,1,0:T(8,128)(2,1)} %bitcast.34), calls=%async_computation.2 | async-start | bytes 4718592 | tf_op jit(solution)/shard_map/all_to_all | solution.py:93
  179.9 34.4 %collective-permute-start.2 = (f32[144,512]{1,0:T(8,128)}, f32[144,512]{1,0:T(8,128)}, u32[]{:S(2)}, u32[]{:S(2)}) collective-permute-start(f32[144,512]{1,0:T(8,128)} %convert_reduce_fusion), channel_id=1, source_target_pairs={{0,128},{128,0},{1,129},{129,1},{2,130},{130,2},{3,131},{131,3},{4... | collective-permute-start | bytes 884744 | tf_op jit(solution)/shard_map/ppermute | solution.py:92
Sparse Core Ops, SparseCore 0:
  9.8 99.3 all-gather.1

commit v10 on v8

--- a/solution.py
+++ b/solution.py
@@ -29,9 +29,6 @@
     w_other = lax.ppermute(w_out, "zl", swap)
     other = lax.ppermute(pref_weight, "zl", swap)
     w_pair = jnp.where(zl == 0, jnp.stack([w_out, w_other]), jnp.stack([w_other, w_out]))
-    copies = jnp.broadcast_to(w_pair[None], (n_plane,) + w_pair.shape)
-    piece = lax.all_to_all(copies, PLANE, 0, 0, tiled=True)
-    piece = piece.transpose(1, 0, 2, 3).reshape(-1, w_out.shape[1])
 
     pair_w = jnp.where(
         zl == 0,
@@ -59,6 +56,9 @@
     hidden = jax.nn.gelu(pre + pref_bias)
     partial_logit = jnp.sum(hidden * pref_out, axis=-1)
     logit = lax.psum(partial_logit, TP)
+    w_pair, features, logit = lax.optimization_barrier((w_pair, features, logit))
+    piece = lax.all_gather(w_pair, PLANE, axis=0, tiled=False)
+    piece = piece.transpose(1, 0, 2, 3).reshape(-1, w_out.shape[1])
     prob = jax.nn.sigmoid(logit)
     numbers = jnp.arange(groups, dtype=jnp.int32)
     first = (pairs[:, :, 0][:, :, None] == numbers).astype(jnp.float32)

time: 203 us -> 237 us (1.17)
  the two profiles are of different devices: /device:TPU:32 before, /device:TPU:96 now
where the time goes in v10:
time: 237 us; the launch traced here: 236 us
  waiting for transfers between devices  81.9 us (35%)
  blocking collectives  78.5 us (33%)
  starting transfers between devices  20.1 us (8%)
  matrix products  18.6 us (8%)
  between operations  14.2 us (6%)
  local copies, waits for them, and re-layouts  14.1 us (6%)
  other arithmetic  8.18 us (3%)
    all_gather x1, waiting for transfers between devices, shards(): piece = lax.all_gather(w_pair, PLANE, axis=0, tiled=False)  45.7 us
    all_to_all x1, blocking collectives, shards(): lax.all_to_all(first_half, PLANE, 0, 0, tiled=True).astype(jnp.float32)  42.2 us
    psum x1, blocking collectives, shards(): logit = lax.psum(partial_logit, TP)  36.3 us
    ppermute x1, waiting for transfers between devices, shards(): other = lax.ppermute(pref_weight, 'zl', swap)  20 us
    all_to_all x1, waiting for transfers between devices, shards(): proj = jnp.sum(lax.all_to_all(part, PLANE, 0, 0, tiled=True), axis=0)  13.2 us
    dot_general x1, matrix products, shards(): lax.dot_general(weighted, attn_out, (((0,), (0,)), ((), ())), preferred_e...  9.04 us
    dot_general x1, matrix products, shards(): jnp.dot(weighted, piece, preferred_element_type=jnp.float32)  8.84 us
    all_to_all x1, starting transfers between devices, shards(): proj = jnp.sum(lax.all_to_all(part, PLANE, 0, 0, tiled=True), axis=0)  7.06 us
  transfers between devices with their start and end apart: 8, of which 5 were waited for; matrix products, arithmetic and copies ran while one was open for 17% of the time, Pallas kernels for 0%

profile of v10, /device:TPU:96, one launch (start us, length us, event | category | flops | bytes accessed | tf_op | source)
XLA Modules:
  0.0 235.6 jit_solution(6299026456971337201)
XLA Ops:
  7.2 0.7 all-gather.4.cloned.1.call-update
  7.9 0.2 collective-permute-start
  8.1 1.3 reshape.124
  9.4 0.9 copy.24
  10.4 7.0 %all-to-all-start = ((bf16[16,16,2,144]{3,2,1,0:T(2,128)(2,1)}), bf16[16,16,2,144]{3,2,1,0:T(2,128)(2,1)S(1)}, u32[]{:S(2)}, u32[]{:S(2)}) async-start(bf16[16,16,2,144]{3,2,1,0:T(2,128)(2,1)} %bitcast.39), calls=%async_computation | async-start | bytes 524288 | tf_op jit(solution)/shard_map/all_to_all | solution.py:39
  17.4 2.0 collective-permute-start.1
  19.4 0.8 fusion.18
  20.2 0.1 reshape.171
  20.3 2.2 gather_fusion.2
  22.5 0.1 reshape.174
  22.6 0.1 reshape.176
  22.7 2.2 gather_fusion.3
  24.9 0.1 reshape.179
  24.9 1.2 all-to-all-done
  26.1 0.2 reshape.125
  26.3 20.0 %collective-permute-done.1 = bf16[2,144,576]{2,1,0:T(8,128)(2,1)S(1)} collective-permute-done((bf16[2,144,576]{2,1,0:T(8,128)(2,1)}, bf16[2,144,576]{2,1,0:T(8,128)(2,1)S(1)}, u32[]{:S(2)}, u32[]{:S(2)}) %collective-permute-start.1) | collective-permute-done | bytes 331808 | tf_op jit(solution)/shard_map/ppermute | solution.py:30
  46.2 0.3 maximum_select_fusion
  46.5 0.4 convolution_bitcast_fusion
  46.9 0.3 convolution_bitcast_fusion.1
  47.3 0.1 pad_maximum_fusion
  47.3 1.4 copy.21
  48.7 7.1 %all-to-all-start.1 = ((f32[16,16,1152]{2,1,0:T(8,128)}), f32[16,16,1152]{2,1,0:T(8,128)S(1)}, u32[]{:S(2)}, u32[]{:S(2)}) async-start(f32[16,16,1152]{2,1,0:T(8,128)} %bitcast.7), calls=%async_computation.1 | async-start | bytes 2359296 | tf_op jit(solution)/shard_map/all_to_all | solution.py:48
  55.9 0.1 fusion.14
  55.9 0.1 reshape.128
  56.0 0.1 reshape.127
  56.2 0.7 maximum_select_fusion.1
  56.9 13.2 %all-to-all-done.1 = f32[16,16,1152]{2,1,0:T(8,128)S(1)} async-done(((f32[16,16,1152]{2,1,0:T(8,128)}), f32[16,16,1152]{2,1,0:T(8,128)S(1)}, u32[]{:S(2)}, u32[]{:S(2)}) %all-to-all-start.1) | async-done | bytes 1179680 | tf_op jit(solution)/shard_map/all_to_all | solution.py:48
  70.1 0.1 fusion.17
  70.2 0.8 gather_fusion.1
  71.0 0.8 gather_fusion
  71.8 0.2 fusion.12
  72.0 0.1 reduce_sum.67
  72.1 36.3 %psum.7 = f32[2,56]{1,0:T(2,128)S(1)} all-reduce(f32[2,56]{1,0:T(2,128)S(1)} %reduce_sum.67), channel_id=1, replica_groups=mesh['zl'=2,'y'=4,'x'=4,'zh'=4,'c'=2] {'zh','c'}, use_global_device_ids=true, to_apply=%region_2.4 | all-reduce | flops 112 | bytes 896 | tf_op jit(solution)/shard_map/psum | solution.py:58
  108.4 1.2 all-gather.4.cloned.1.call-done
  109.7 0.1 add_reduce_fusion.1
  109.8 0.1 select_reduce_fusion
  109.9 0.1 mul.106
  110.0 0.1 mul.108
  110.1 9.0 %fusion.2 = bf16[4608,512]{1,0:T(8,128)(2,1)S(1)} fusion(bf16[1024,512]{1,0:T(8,128)(2,1)S(1)} %copy-done, bf16[1024,4608]{0,1:T(8,128)(2,1)} %all-gather.4.cloned.1.call-done, f32[1024]{0:T(1024)S(1)} %mul.109), kind=kOutput, calls=%fused_computation.7 | convolution fusion | flops 4848353280 | bytes 15208448 | tf_op jit(solution)/shard_map/dot_general | solution.py:81
  119.2 1.7 broadcast_select_fusion
  120.9 42.2 %all_to_all.20 = bf16[16,144,512]{2,1,0:T(8,128)(2,1)} all-to-all(bf16[16,144,512]{2,1,0:T(8,128)(2,1)S(1)} %bitcast.41), channel_id=1, replica_groups=mesh['zl'=2,'y'=4,'x'=4,'zh'=4,'c'=2] {'y','x'}, dimensions={0} | all-to-all | bytes 4718592 | tf_op jit(solution)/shard_map/all_to_all | solution.py:87
  163.0 3.7 %all-to-all-start.2 = ((bf16[16,144,512]{2,1,0:T(8,128)(2,1)}), bf16[16,144,512]{2,1,0:T(8,128)(2,1)S(1)}, u32[]{:S(2)}, u32[]{:S(2)}) async-start(bf16[16,144,512]{2,1,0:T(8,128)(2,1)} %bitcast.40), calls=%async_computation.2 | async-start | bytes 4718592 | tf_op jit(solution)/shard_map/all_to_all | solution.py:89
  166.8 2.7 %convert_reduce_fusion = f32[144,512]{1,0:T(8,128)} fusion(bf16[16,144,512]{2,1,0:T(8,128)(2,1)} %all_to_all.20), kind=kLoop, calls=%fused_computation.8 | loop fusion | flops 2285568 | bytes 2654208 | tf_op jit(solution)/shard_map/reduce_sum | solution.py:87
  169.5 45.7 %all-gather.6.cloned.1.call-done = bf16[32,144,512]{2,1,0:T(8,128)(2,1)} async-done(((bf16[2,144,512]{2,1,0:T(8,128)(2,1)}), bf16[32,144,512]{2,1,0:T(8,128)(2,1)}) %all-gather.6.cloned.1.call-update) | async-done | bytes 4718608 | tf_op jit(solution)/shard_map/all_gather | solution.py:60
  215.2 2.6 %copy.22 = bf16[2,16,144,512]{3,2,1,0:T(8,128)(2,1)S(1)} copy(bf16[2,16,144,512]{3,2,0,1:T(8,128)(2,1)} %bitcast.42) | data formatting | bytes 9437184 | tf_op jit(solution)/shard_map/transpose | solution.py:61
  217.8 8.8 %fusion.3 = bf16[1024,512]{1,0:T(8,128)(2,1)} fusion(bf16[4608,512]{1,0:T(8,128)(2,1)S(1)} %bitcast.43, bf16[1024,4608]{0,1:T(8,128)(2,1)} %all-gather.4.cloned.1.call-done, f32[1024]{0:T(1024)S(1)} %mul.109), kind=kOutput, calls=%fused_computation.12 | convolution fusion | flops 4846518272 | bytes 15208448 | tf_op jit(solution)/shard_map/dot_general | solution.py:90
  226.7 0.3 convert_reduce_fusion.1
  227.0 1.7 add_multiply_fusion
  (34 shorter events, 0.3 us)
Async XLA Ops:
  7.2 102.9 %copy-start = (bf16[1024,512]{1,0:T(8,128)(2,1)S(1)}, bf16[1024,512]{1,0:T(8,128)(2,1)}, u32[]{:S(2)}) copy-start(bf16[1024,512]{1,0:T(8,128)(2,1)} %param.19) | copy-start | bytes 3145732
  7.2 39.1 %copy-start.2 = (bf16[2,144,576]{2,1,0:T(8,128)(2,1)S(1)}, bf16[2,144,576]{2,1,0:T(8,128)(2,1)}, u32[]{:S(2)}) copy-start(bf16[2,144,576]{2,1,0:T(8,128)(2,1)} %param.15) | copy-start | bytes 995332
  7.2 102.4 %all-gather.4.cloned.1.call-start = ((), (), s32[]{:S(2)}) async-start(), calls=%async_computation.4 | async-start | bytes 10616832 | tf_op jit(solution)/shard_map/all_gather | solution.py:28
  7.9 48.2 %collective-permute-start = (bf16[144,512]{1,0:T(8,128)(2,1)}, bf16[144,512]{1,0:T(8,128)(2,1)S(1)}, u32[]{:S(2)}, u32[]{:S(2)}) collective-permute-start(bf16[144,512]{1,0:T(8,128)(2,1)} %param.21), channel_id=1, source_target_pairs={{0,128},{128,0},{1,129},{129,1},{2,130},{130,2},{3,131},{131,3},{4... | collective-permute-start | bytes 442376 | tf_op jit(solution)/shard_map/ppermute | solution.py:29
  10.4 15.7 %all-to-all-start = ((bf16[16,16,2,144]{3,2,1,0:T(2,128)(2,1)}), bf16[16,16,2,144]{3,2,1,0:T(2,128)(2,1)S(1)}, u32[]{:S(2)}, u32[]{:S(2)}) async-start(bf16[16,16,2,144]{3,2,1,0:T(2,128)(2,1)} %bitcast.39), calls=%async_computation | async-start | bytes 524288 | tf_op jit(solution)/shard_map/all_to_all | solution.py:39
  17.4 28.8 %collective-permute-start.1 = (bf16[2,144,576]{2,1,0:T(8,128)(2,1)}, bf16[2,144,576]{2,1,0:T(8,128)(2,1)S(1)}, u32[]{:S(2)}, u32[]{:S(2)}) collective-permute-start(bf16[2,144,576]{2,1,0:T(8,128)(2,1)} %param.15), channel_id=1, source_target_pairs={{0,128},{128,0},{1,129},{129,1},{2,130},{130,2},{3,131},{131,3},{4... | collective-permute-start | bytes 995336 | tf_op jit(solution)/shard_map/ppermute | solution.py:30
  46.5 9.6 %copy-start.3 = (bf16[144,512]{1,0:T(8,128)(2,1)S(1)}, bf16[144,512]{1,0:T(8,128)(2,1)}, u32[]{:S(2)}) copy-start(bf16[144,512]{1,0:T(8,128)(2,1)} %param.21) | copy-start | bytes 442372
  48.7 23.1 %copy-start.4 = (f32[576]{0:T(1024)S(1)}, f32[576]{0:T(1024)}, u32[]{:S(2)}) copy-start(f32[576]{0:T(1024)} %param.17) | copy-start | bytes 6916
  48.7 23.1 %copy-start.5 = (f32[576]{0:T(1024)S(1)}, f32[576]{0:T(1024)}, u32[]{:S(2)}) copy-start(f32[576]{0:T(1024)} %param.16) | copy-start | bytes 6916
  48.7 61.0 %copy-start.1 = (s32[2,8]{1,0:T(2,128)S(1)}, s32[2,8]{1,0:T(2,128)}, u32[]{:S(2)}) copy-start(s32[2,8]{1,0:T(2,128)} %param.13) | copy-start | bytes 196
  48.7 61.2 %copy-start.6 = (f32[16]{0:T(128)S(1)}, f32[16]{0:T(128)}, u32[]{:S(2)}) copy-start(f32[16]{0:T(128)} %param.18) | copy-start | bytes 196
  48.7 21.3 %all-to-all-start.1 = ((f32[16,16,1152]{2,1,0:T(8,128)}), f32[16,16,1152]{2,1,0:T(8,128)S(1)}, u32[]{:S(2)}, u32[]{:S(2)}) async-start(f32[16,16,1152]{2,1,0:T(8,128)} %bitcast.7), calls=%async_computation.1 | async-start | bytes 2359296 | tf_op jit(solution)/shard_map/all_to_all | solution.py:48
  55.8 159.4 %all-gather.6.cloned.1.call-start = ((), (), s32[]{:S(2)}) async-start(), calls=%async_computation.5 | async-start | bytes 5013504 | tf_op jit(solution)/shard_map/all_gather | solution.py:60
  163.0 63.6 %all-to-all-start.2 = ((bf16[16,144,512]{2,1,0:T(8,128)(2,1)}), bf16[16,144,512]{2,1,0:T(8,128)(2,1)S(1)}, u32[]{:S(2)}, u32[]{:S(2)}) async-start(bf16[16,144,512]{2,1,0:T(8,128)(2,1)} %bitcast.40), calls=%async_computation.2 | async-start | bytes 4718592 | tf_op jit(solution)/shard_map/all_to_all | solution.py:89
  169.5 57.5 %collective-permute-start.2 = (f32[144,512]{1,0:T(8,128)}, f32[144,512]{1,0:T(8,128)}, u32[]{:S(2)}, u32[]{:S(2)}) collective-permute-start(f32[144,512]{1,0:T(8,128)} %convert_reduce_fusion), channel_id=1, source_target_pairs={{0,128},{128,0},{1,129},{129,1},{2,130},{130,2},{3,131},{131,3},{4... | collective-permute-start | bytes 884744 | tf_op jit(solution)/shard_map/ppermute | solution.py:88
Sparse Core Ops, SparseCore 0:
  9.8 99.7 all-gather.3
  112.6 102.5 all-gather.5

commit v11 on v8

--- a/solution.py
+++ b/solution.py
@@ -39,6 +39,7 @@
         jnp.concatenate([other, pref_weight], axis=1),
     )
     cols = embeds.reshape(resp_dev, n_zl, n_plane, rows_w).transpose(2, 0, 1, 3)
+    cols = cols.reshape(n_plane, resp_dev * n_zl * rows_w // 128, 128)
     cols = lax.all_to_all(cols, PLANE, 0, 0, tiled=True).reshape(n_plane * resp_dev, n_zl * rows_w)
     part = jnp.concatenate(
         [

time: 203 us -> 201 us (level)
  the two profiles are of different devices: /device:TPU:32 before, /device:TPU:96 now
where the time goes in v11:
time: 201 us; the launch traced here: 200 us
  waiting for transfers between devices  68.1 us (34%)
  blocking collectives  51.4 us (26%)
  starting transfers between devices  23 us (11%)
  matrix products  18.6 us (9%)
  local copies, waits for them, and re-layouts  17.3 us (9%)
  between operations  14.3 us (7%)
  other arithmetic  6.9 us (3%)
    all_to_all x1, blocking collectives, shards(): lax.all_to_all(first_half, PLANE, 0, 0, tiled=True).astype(jnp.float32)  32.7 us
    all_gather x1, waiting for transfers between devices, shards(): features = lax.all_gather(grad_out, TP, axis=1, tiled=True)  27.2 us
    psum x1, blocking collectives, shards(): logit = lax.psum(partial_logit, TP)  18.7 us
    all_to_all x1, waiting for transfers between devices, shards(): shares = lax.all_to_all(own_half, PLANE, 0, 0, tiled=True)  15.2 us
    all_to_all x1, waiting for transfers between devices, shards(): proj = jnp.sum(lax.all_to_all(part, PLANE, 0, 0, tiled=True), axis=0)  13 us
    dot_general x1, matrix products, shards(): lax.dot_general(weighted, attn_out, (((0,), (0,)), ((), ())), preferred_e...  9.03 us
    dot_general x1, matrix products, shards(): jnp.dot(weighted, piece, preferred_element_type=jnp.float32)  8.83 us
    all_to_all x1, starting transfers between devices, shards(): lax.all_to_all(cols, PLANE, 0, 0, tiled=True)  7.03 us
  transfers between devices with their start and end apart: 8, of which 5 were waited for; matrix products, arithmetic and copies ran while one was open for 20% of the time, Pallas kernels for 0%

profile of v11, /device:TPU:96, one launch (start us, length us, event | category | flops | bytes accessed | tf_op | source)
XLA Modules:
  0.0 199.5 jit_solution(1344475992000351544)
XLA Ops:
  7.2 0.7 all-gather.2.cloned.1.call-update
  7.9 0.2 collective-permute-start
  8.1 1.3 reshape.160
  9.4 0.2 copy.21
  9.7 1.1 reshape.161
  10.8 7.0 %all-to-all-start = ((bf16[16,36,128]{2,1,0:T(8,128)(2,1)}), bf16[16,36,128]{2,1,0:T(8,128)(2,1)S(1)}, u32[]{:S(2)}, u32[]{:S(2)}) async-start(bf16[16,36,128]{2,1,0:T(8,128)(2,1)} %reshape.161), calls=%async_computation | async-start | bytes 327680 | tf_op jit(solution)/shard_map/all_to_all | solution.py:43
  17.8 2.0 %collective-permute-start.1 = (bf16[144,512]{1,0:T(8,128)(2,1)}, bf16[144,512]{1,0:T(8,128)(2,1)S(1)}, u32[]{:S(2)}, u32[]{:S(2)}) collective-permute-start(bf16[144,512]{1,0:T(8,128)(2,1)} %param.21), channel_id=1, source_target_pairs={{0,128},{128,0},{1,129},{129,1},{2,130},{130,2},{3,131},{131,3},{4... | collective-permute-start | bytes 442376 | tf_op jit(solution)/shard_map/ppermute | solution.py:29
  19.8 0.8 fusion.18
  20.6 5.4 %all-to-all-done = bf16[16,36,128]{2,1,0:T(8,128)(2,1)S(1)} async-done(((bf16[16,36,128]{2,1,0:T(8,128)(2,1)}), bf16[16,36,128]{2,1,0:T(8,128)(2,1)S(1)}, u32[]{:S(2)}, u32[]{:S(2)}) %all-to-all-start) | async-done | bytes 147488 | tf_op jit(solution)/shard_map/all_to_all | solution.py:43
  26.0 0.3 reshape.162
  26.3 1.4 maximum_select_fusion
  27.7 0.4 convolution_bitcast_fusion
  28.0 0.4 convolution_bitcast_fusion.1
  28.5 1.4 copy.18
  29.9 3.7 %all-to-all-start.1 = ((f32[16,16,1152]{2,1,0:T(8,128)}), f32[16,16,1152]{2,1,0:T(8,128)S(1)}, u32[]{:S(2)}, u32[]{:S(2)}) async-start(f32[16,16,1152]{2,1,0:T(8,128)} %bitcast.6), calls=%async_computation.1 | async-start | bytes 2359296 | tf_op jit(solution)/shard_map/all_to_all | solution.py:52
  33.6 0.1 reshape.207
  33.7 2.0 %gather_fusion.2 = s32[112]{0:T(128)S(1)} fusion(s32[2,8]{1,0:T(2,128)S(1)} %copy-done.1, s32[112]{0:T(128)S(1)} %reshape.207), kind=kCustom, calls=%fused_computation.clone | custom fusion | bytes 1792 | tf_op jit(solution)/shard_map/jit(take_along_axis)/gather | solution.py:55
  35.7 0.1 reshape.210
  35.8 0.1 reshape.212
  35.9 2.0 %gather_fusion.3 = s32[112]{0:T(128)S(1)} fusion(s32[2,8]{1,0:T(2,128)S(1)} %copy-done.1, s32[112]{0:T(128)S(1)} %reshape.212), kind=kCustom, calls=%fused_computation.1.clone | custom fusion | bytes 1792 | tf_op jit(solution)/shard_map/jit(take_along_axis)/gather | solution.py:56
  37.9 0.1 reshape.215
  38.1 0.1 reshape.165
  38.1 0.1 reshape.164
  38.3 13.0 %all-to-all-done.1 = f32[16,16,1152]{2,1,0:T(8,128)S(1)} async-done(((f32[16,16,1152]{2,1,0:T(8,128)}), f32[16,16,1152]{2,1,0:T(8,128)S(1)}, u32[]{:S(2)}, u32[]{:S(2)}) %all-to-all-start.1) | async-done | bytes 1179680 | tf_op jit(solution)/shard_map/all_to_all | solution.py:52
  51.3 2.6 %broadcast_in_dim.4 = bf16[16,2,144,512]{3,2,1,0:T(8,128)(2,1)} broadcast(bf16[2,144,512]{2,1,0:T(8,128)(2,1)S(1)} %maximum_select_fusion.1), dimensions={1,2,3} | broadcast | bytes 5013504 | tf_op jit(solution)/shard_map/broadcast_in_dim | solution.py:32
  53.9 4.6 %all-to-all-start.3 = ((bf16[16,2,144,512]{3,2,1,0:T(8,128)(2,1)}), bf16[16,2,144,512]{3,2,1,0:T(8,128)(2,1)}, u32[]{:S(2)}, u32[]{:S(2)}) async-start(bf16[16,2,144,512]{3,2,1,0:T(8,128)(2,1)} %broadcast_in_dim.4), calls=%async_computation.3 | async-start | bytes 9437184 | tf_op jit(solution)/shard_map/all_to_all | solution.py:33
  58.7 0.8 gather_fusion.1
  59.5 0.8 gather_fusion
  60.3 0.2 fusion.12
  60.6 0.1 reduce_sum.67
  60.6 18.7 %psum.7 = f32[2,56]{1,0:T(2,128)S(1)} all-reduce(f32[2,56]{1,0:T(2,128)S(1)} %reduce_sum.67), channel_id=1, replica_groups=mesh['zl'=2,'y'=4,'x'=4,'zh'=4,'c'=2] {'zh','c'}, use_global_device_ids=true, to_apply=%region_2.4 | all-reduce | flops 112 | bytes 896 | tf_op jit(solution)/shard_map/psum | solution.py:62
  79.3 0.1 add_reduce_fusion.1
  79.4 0.1 select_reduce_fusion
  79.5 0.1 mul.106
  79.8 27.2 %all-gather.2.cloned.1.call-done = bf16[1024,4608]{0,1:T(8,128)(2,1)} async-done(((bf16[1024,576]{0,1:T(8,128)(2,1)}), bf16[1024,4608]{0,1:T(8,128)(2,1)}) %all-gather.2.cloned.1.call-update) | async-done | bytes 9437200 | tf_op jit(solution)/shard_map/all_gather | solution.py:28
  106.9 9.0 %fusion.2 = bf16[4608,512]{1,0:T(8,128)(2,1)S(1)} fusion(bf16[1024,512]{1,0:T(8,128)(2,1)S(1)} %copy-done, bf16[1024,4608]{0,1:T(8,128)(2,1)} %all-gather.2.cloned.1.call-done, f32[1024]{0:T(1024)S(1)} %mul.109), kind=kOutput, calls=%fused_computation.7 | convolution fusion | flops 4848353280 | bytes 15208448 | tf_op jit(solution)/shard_map/dot_general | solution.py:82
  116.0 1.7 broadcast_select_fusion
  117.7 6.7 %all-to-all-done.3 = bf16[16,2,144,512]{3,2,1,0:T(8,128)(2,1)} async-done(((bf16[16,2,144,512]{3,2,1,0:T(8,128)(2,1)}), bf16[16,2,144,512]{3,2,1,0:T(8,128)(2,1)}, u32[]{:S(2)}, u32[]{:S(2)}) %all-to-all-start.3) | async-done | bytes 4718624 | tf_op jit(solution)/shard_map/all_to_all | solution.py:33
  124.3 32.7 %all_to_all.25 = bf16[16,144,512]{2,1,0:T(8,128)(2,1)} all-to-all(bf16[16,144,512]{2,1,0:T(8,128)(2,1)S(1)} %bitcast.40), channel_id=1, replica_groups=mesh['zl'=2,'y'=4,'x'=4,'zh'=4,'c'=2] {'y','x'}, dimensions={0} | all-to-all | bytes 4718592 | tf_op jit(solution)/shard_map/all_to_all | solution.py:88
  157.0 3.7 %all-to-all-start.2 = ((bf16[16,144,512]{2,1,0:T(8,128)(2,1)}), bf16[16,144,512]{2,1,0:T(8,128)(2,1)S(1)}, u32[]{:S(2)}, u32[]{:S(2)}) async-start(bf16[16,144,512]{2,1,0:T(8,128)(2,1)} %bitcast.39), calls=%async_computation.2 | async-start | bytes 4718592 | tf_op jit(solution)/shard_map/all_to_all | solution.py:90
  160.8 2.8 %copy.19 = bf16[16,2,144,512]{3,2,0,1:T(8,128)(2,1)S(1)} copy(bf16[16,2,144,512]{3,2,1,0:T(8,128)(2,1)} %all-to-all-done.3) | data formatting | bytes 9437184 | tf_op jit(solution)/shard_map/all_to_all | solution.py:33
  163.6 0.3 copy-done.2
  163.8 1.0 convert_reduce_fusion
  164.9 1.7 collective-permute-start.2
  166.6 8.8 %fusion.3 = bf16[1024,512]{1,0:T(8,128)(2,1)} fusion(bf16[4608,512]{1,0:T(8,128)(2,1)S(1)} %bitcast.41, bf16[1024,4608]{0,1:T(8,128)(2,1)} %all-gather.2.cloned.1.call-done, f32[1024]{0:T(1024)S(1)} %mul.109), kind=kOutput, calls=%fused_computation.12 | convolution fusion | flops 4846518272 | bytes 15208448 | tf_op jit(solution)/shard_map/dot_general | solution.py:91
  175.4 15.2 %all-to-all-done.2 = bf16[16,144,512]{2,1,0:T(8,128)(2,1)S(1)} async-done(((bf16[16,144,512]{2,1,0:T(8,128)(2,1)}), bf16[16,144,512]{2,1,0:T(8,128)(2,1)S(1)}, u32[]{:S(2)}, u32[]{:S(2)}) %all-to-all-start.2) | async-done | bytes 2359328 | tf_op jit(solution)/shard_map/all_to_all | solution.py:90
  190.6 0.3 convert_reduce_fusion.1
  191.0 1.7 add_multiply_fusion
  (35 shorter events, 0.6 us)
Async XLA Ops:
  7.2 99.8 %copy-start = (bf16[1024,512]{1,0:T(8,128)(2,1)S(1)}, bf16[1024,512]{1,0:T(8,128)(2,1)}, u32[]{:S(2)}) copy-start(bf16[1024,512]{1,0:T(8,128)(2,1)} %param.19) | copy-start | bytes 3145732
  7.2 99.8 %all-gather.2.cloned.1.call-start = ((), (), s32[]{:S(2)}) async-start(), calls=%async_computation.5 | async-start | bytes 10616832 | tf_op jit(solution)/shard_map/all_gather | solution.py:28
  7.9 18.4 %collective-permute-start = (bf16[2,144,576]{2,1,0:T(8,128)(2,1)}, bf16[2,144,576]{2,1,0:T(8,128)(2,1)S(1)}, u32[]{:S(2)}, u32[]{:S(2)}) collective-permute-start(bf16[2,144,576]{2,1,0:T(8,128)(2,1)} %param.15), channel_id=1, source_target_pairs={{0,128},{128,0},{1,129},{129,1},{2,130},{130,2},{3,131},{131,3},{4... | collective-permute-start | bytes 995336 | tf_op jit(solution)/shard_map/ppermute | solution.py:30
  10.8 15.2 %all-to-all-start = ((bf16[16,36,128]{2,1,0:T(8,128)(2,1)}), bf16[16,36,128]{2,1,0:T(8,128)(2,1)S(1)}, u32[]{:S(2)}, u32[]{:S(2)}) async-start(bf16[16,36,128]{2,1,0:T(8,128)(2,1)} %reshape.161), calls=%async_computation | async-start | bytes 327680 | tf_op jit(solution)/shard_map/all_to_all | solution.py:43
  17.8 20.4 %collective-permute-start.1 = (bf16[144,512]{1,0:T(8,128)(2,1)}, bf16[144,512]{1,0:T(8,128)(2,1)S(1)}, u32[]{:S(2)}, u32[]{:S(2)}) collective-permute-start(bf16[144,512]{1,0:T(8,128)(2,1)} %param.21), channel_id=1, source_target_pairs={{0,128},{128,0},{1,129},{129,1},{2,130},{130,2},{3,131},{131,3},{4... | collective-permute-start | bytes 442376 | tf_op jit(solution)/shard_map/ppermute | solution.py:29
  27.7 6.0 %copy-start.1 = (s32[2,8]{1,0:T(2,128)S(1)}, s32[2,8]{1,0:T(2,128)}, u32[]{:S(2)}) copy-start(s32[2,8]{1,0:T(2,128)} %param.13) | copy-start | bytes 196
  28.4 9.8 %copy-start.3 = (bf16[144,512]{1,0:T(8,128)(2,1)S(1)}, bf16[144,512]{1,0:T(8,128)(2,1)}, u32[]{:S(2)}) copy-start(bf16[144,512]{1,0:T(8,128)(2,1)} %param.21) | copy-start | bytes 442372
  29.9 21.4 %all-to-all-start.1 = ((f32[16,16,1152]{2,1,0:T(8,128)}), f32[16,16,1152]{2,1,0:T(8,128)S(1)}, u32[]{:S(2)}, u32[]{:S(2)}) async-start(f32[16,16,1152]{2,1,0:T(8,128)} %bitcast.6), calls=%async_computation.1 | async-start | bytes 2359296 | tf_op jit(solution)/shard_map/all_to_all | solution.py:52
  53.9 70.4 %all-to-all-start.3 = ((bf16[16,2,144,512]{3,2,1,0:T(8,128)(2,1)}), bf16[16,2,144,512]{3,2,1,0:T(8,128)(2,1)}, u32[]{:S(2)}, u32[]{:S(2)}) async-start(bf16[16,2,144,512]{3,2,1,0:T(8,128)(2,1)} %broadcast_in_dim.4), calls=%async_computation.3 | async-start | bytes 9437184 | tf_op jit(solution)/shard_map/all_to_all | solution.py:33
  58.5 1.8 copy-start.4
  58.5 1.8 copy-start.5
  58.5 21.1 %copy-start.6 = (f32[16]{0:T(128)S(1)}, f32[16]{0:T(128)}, u32[]{:S(2)}) copy-start(f32[16]{0:T(128)} %param.18) | copy-start | bytes 196
  157.0 33.6 %all-to-all-start.2 = ((bf16[16,144,512]{2,1,0:T(8,128)(2,1)}), bf16[16,144,512]{2,1,0:T(8,128)(2,1)S(1)}, u32[]{:S(2)}, u32[]{:S(2)}) async-start(bf16[16,144,512]{2,1,0:T(8,128)(2,1)} %bitcast.39), calls=%async_computation.2 | async-start | bytes 4718592 | tf_op jit(solution)/shard_map/all_to_all | solution.py:90
  160.8 3.1 %copy-start.2 = (bf16[16,144,512]{2,1,0:T(8,128)(2,1)S(1)}, bf16[16,144,512]{2,1,0:T(8,128)(2,1)}, u32[]{:S(2)}) copy-start(bf16[16,144,512]{2,1,0:T(8,128)(2,1)} %all_to_all.25) | copy-start | bytes 7077892
  164.9 26.1 %collective-permute-start.2 = (f32[144,512]{1,0:T(8,128)}, f32[144,512]{1,0:T(8,128)}, u32[]{:S(2)}, u32[]{:S(2)}) collective-permute-start(f32[144,512]{1,0:T(8,128)} %convert_reduce_fusion), channel_id=1, source_target_pairs={{0,128},{128,0},{1,129},{129,1},{2,130},{130,2},{3,131},{131,3},{4... | collective-permute-start | bytes 884744 | tf_op jit(solution)/shard_map/ppermute | solution.py:89
Sparse Core Ops, SparseCore 0:
  9.8 97.0 all-gather.1

commit v12 on v11

--- a/solution.py
+++ b/solution.py
@@ -28,8 +28,10 @@
     features = lax.all_gather(grad_out, TP, axis=1, tiled=True)
     w_other = lax.ppermute(w_out, "zl", swap)
     other = lax.ppermute(pref_weight, "zl", swap)
-    w_pair = jnp.where(zl == 0, jnp.stack([w_out, w_other]), jnp.stack([w_other, w_out]))
-    copies = jnp.broadcast_to(w_pair[None], (n_plane,) + w_pair.shape)
+    shape = (n_plane, 2) + w_out.shape
+    first_w = jnp.broadcast_to(jnp.where(zl == 0, w_out, w_other)[None, None], shape)
+    second_w = jnp.broadcast_to(jnp.where(zl == 0, w_other, w_out)[None, None], shape)
+    copies = jnp.where(jnp.arange(2)[None, :, None, None] == 0, first_w, second_w)
     piece = lax.all_to_all(copies, PLANE, 0, 0, tiled=True)
     piece = piece.transpose(1, 0, 2, 3).reshape(-1, w_out.shape[1])
 

time: 201 us -> 203 us (level); the launches traced: 200 us -> 199 us
  blocking collectives: 51.4 us -> 48.3 us
  starting transfers between devices: 23 us -> 25.9 us
  local copies, waits for them, and re-layouts: 17.3 us -> 14.8 us
    all_to_all x1, waiting for transfers between devices: 5.4 us -> 0.82 us  [shards(): lax.all_to_all(cols, PLANE, 0, 0, tiled=True)]
    all_gather x1, waiting for transfers between devices: 27.2 us -> 31.4 us  [shards(): features = lax.all_gather(grad_out, TP, axis=1, tiled=True)]
    psum x1, blocking collectives: 18.7 us -> 15.3 us  [shards(): logit = lax.psum(partial_logit, TP)]
    broadcast_in_dim x1 -> x0, local copies, waits for them, and re-layouts: 2.65 us -> none  [shards(): copies = jnp.broadcast_to(w_pair[None], (n_plane,) + w_pair.shape)]
    all_to_all x1, starting transfers between devices: 3.7 us -> 6.32 us  [shards(): proj = jnp.sum(lax.all_to_all(part, PLANE, 0, 0, tiled=True), axis=0)]
    select_n x1 -> x2, other arithmetic: 0.03 us -> 2.52 us  [the longest x1 2.5 us: shards(): jnp.where(jnp.arange(2)[None, :, None, None] == 0, first_w, second_w)]
where the time goes in v12:
time: 203 us; the launch traced here: 199 us
  waiting for transfers between devices  69.2 us (34%)
  blocking collectives  48.3 us (24%)
  starting transfers between devices  25.9 us (13%)
  matrix products  18.5 us (9%)
  local copies, waits for them, and re-layouts  14.8 us (7%)
  between operations  14.3 us (7%)
  other arithmetic  8.27 us (4%)
    all_to_all x1, blocking collectives, shards(): lax.all_to_all(first_half, PLANE, 0, 0, tiled=True).astype(jnp.float32)  32.9 us
    all_gather x1, waiting for transfers between devices, shards(): features = lax.all_gather(grad_out, TP, axis=1, tiled=True)  31.4 us
    psum x1, blocking collectives, shards(): logit = lax.psum(partial_logit, TP)  15.3 us
    all_to_all x1, waiting for transfers between devices, shards(): shares = lax.all_to_all(own_half, PLANE, 0, 0, tiled=True)  15.2 us
    all_to_all x1, waiting for transfers between devices, shards(): proj = jnp.sum(lax.all_to_all(part, PLANE, 0, 0, tiled=True), axis=0)  15 us
    dot_general x1, matrix products, shards(): lax.dot_general(weighted, attn_out, (((0,), (0,)), ((), ())), preferred_e...  9.03 us
    dot_general x1, matrix products, shards(): jnp.dot(weighted, piece, preferred_element_type=jnp.float32)  8.76 us
    all_to_all x1, starting transfers between devices, shards(): lax.all_to_all(cols, PLANE, 0, 0, tiled=True)  7.03 us
  transfers between devices with their start and end apart: 8, of which 5 were waited for; matrix products, arithmetic and copies ran while one was open for 20% of the time, Pallas kernels for 0%

profile of v12, /device:TPU:96, one launch (start us, length us, event | category | flops | bytes accessed | tf_op | source)
XLA Modules:
  0.0 199.3 jit_solution(1869701061219474995)
XLA Ops:
  7.2 0.7 all-gather.2.cloned.1.call-update
  7.9 0.2 collective-permute-start
  8.1 1.3 reshape.134
  9.5 0.2 copy.21
  9.7 1.1 reshape.135
  10.8 7.0 %all-to-all-start = ((bf16[16,36,128]{2,1,0:T(8,128)(2,1)}), bf16[16,36,128]{2,1,0:T(8,128)(2,1)S(1)}, u32[]{:S(2)}, u32[]{:S(2)}) async-start(bf16[16,36,128]{2,1,0:T(8,128)(2,1)} %reshape.135), calls=%async_computation | async-start | bytes 327680 | tf_op jit(solution)/shard_map/all_to_all | solution.py:45
  17.8 2.0 %collective-permute-start.1 = (bf16[144,512]{1,0:T(8,128)(2,1)}, bf16[144,512]{1,0:T(8,128)(2,1)S(1)}, u32[]{:S(2)}, u32[]{:S(2)}) collective-permute-start(bf16[144,512]{1,0:T(8,128)(2,1)} %param.21), channel_id=1, source_target_pairs={{0,128},{128,0},{1,129},{129,1},{2,130},{130,2},{3,131},{131,3},{4... | collective-permute-start | bytes 442376 | tf_op jit(solution)/shard_map/ppermute | solution.py:29
  19.8 0.8 fusion.18
  20.6 0.1 reshape.181
  20.7 2.2 %gather_fusion.2 = s32[112]{0:T(128)S(1)} fusion(s32[2,8]{1,0:T(2,128)} %param.13, s32[112]{0:T(128)S(1)} %reshape.181), kind=kCustom, calls=%fused_computation.clone | custom fusion | bytes 1792 | tf_op jit(solution)/shard_map/jit(take_along_axis)/gather | solution.py:57
  22.9 0.1 reshape.184
  23.0 0.1 reshape.186
  23.1 2.0 %gather_fusion.3 = s32[112]{0:T(128)S(1)} fusion(s32[2,8]{1,0:T(2,128)S(1)} %copy-done.1, s32[112]{0:T(128)S(1)} %reshape.186), kind=kCustom, calls=%fused_computation.1.clone | custom fusion | bytes 1792 | tf_op jit(solution)/shard_map/jit(take_along_axis)/gather | solution.py:58
  25.1 0.1 reshape.189
  25.2 0.8 all-to-all-done
  26.0 0.3 reshape.136
  26.3 0.3 maximum_select_fusion
  26.6 0.3 convolution_bitcast_fusion
  27.0 0.3 convolution_bitcast_fusion.1
  27.4 1.4 copy.18
  28.8 6.3 %all-to-all-start.1 = ((f32[16,16,1152]{2,1,0:T(8,128)}), f32[16,16,1152]{2,1,0:T(8,128)S(1)}, u32[]{:S(2)}, u32[]{:S(2)}) async-start(f32[16,16,1152]{2,1,0:T(8,128)} %bitcast.6), calls=%async_computation.1 | async-start | bytes 2359296 | tf_op jit(solution)/shard_map/all_to_all | solution.py:54
  35.2 0.1 reshape.139
  35.3 0.1 reshape.138
  35.4 2.5 %broadcast_select_fusion = bf16[16,2,144,512]{3,2,1,0:T(8,128)(2,1)} fusion(pred[2]{0:T(512)(128)(4,1)S(1)} %iota_compare_fusion.3, bf16[144,512]{1,0:T(8,128)(2,1)S(1)} %get-tuple-element.14, bf16[144,512]{1,0:T(8,128)(2,1)S(1)} %get-tuple-element.13), kind=kLoop, calls=%fused_computation.10 | loop fusion | flops 2359296 | bytes 5013506 | tf_op jit(solution)/shard_map/jit(_where)/select_n | solution.py:34
  37.9 15.0 %all-to-all-done.1 = f32[16,16,1152]{2,1,0:T(8,128)S(1)} async-done(((f32[16,16,1152]{2,1,0:T(8,128)}), f32[16,16,1152]{2,1,0:T(8,128)S(1)}, u32[]{:S(2)}, u32[]{:S(2)}) %all-to-all-start.1) | async-done | bytes 1179680 | tf_op jit(solution)/shard_map/all_to_all | solution.py:54
  52.9 4.5 %all-to-all-start.3 = ((bf16[16,2,144,512]{3,2,1,0:T(8,128)(2,1)}), bf16[16,2,144,512]{3,2,1,0:T(8,128)(2,1)}, u32[]{:S(2)}, u32[]{:S(2)}) async-start(bf16[16,2,144,512]{3,2,1,0:T(8,128)(2,1)} %broadcast_select_fusion), calls=%async_computation.3 | async-start | bytes 9437184 | tf_op jit(solution)/shard_map/all_to_all | solution.py:35
  57.7 0.8 gather_fusion.1
  58.5 0.8 gather_fusion
  59.3 0.2 fusion.12
  59.5 0.1 reduce_sum.67
  59.6 15.3 %psum.7 = f32[2,56]{1,0:T(2,128)S(1)} all-reduce(f32[2,56]{1,0:T(2,128)S(1)} %reduce_sum.67), channel_id=1, replica_groups=mesh['zl'=2,'y'=4,'x'=4,'zh'=4,'c'=2] {'zh','c'}, use_global_device_ids=true, to_apply=%region_2.4 | all-reduce | flops 112 | bytes 896 | tf_op jit(solution)/shard_map/psum | solution.py:64
  75.0 0.1 add_reduce_fusion.1
  75.1 0.1 select_reduce_fusion
  75.2 0.1 mul.106
  75.4 31.4 %all-gather.2.cloned.1.call-done = bf16[1024,4608]{0,1:T(8,128)(2,1)} async-done(((bf16[1024,576]{0,1:T(8,128)(2,1)}), bf16[1024,4608]{0,1:T(8,128)(2,1)}) %all-gather.2.cloned.1.call-update) | async-done | bytes 9437200 | tf_op jit(solution)/shard_map/all_gather | solution.py:28
  106.9 9.0 %fusion.2 = bf16[4608,512]{1,0:T(8,128)(2,1)S(1)} fusion(bf16[1024,512]{1,0:T(8,128)(2,1)S(1)} %copy-done, bf16[1024,4608]{0,1:T(8,128)(2,1)} %all-gather.2.cloned.1.call-done, f32[1024]{0:T(1024)S(1)} %mul.109), kind=kOutput, calls=%fused_computation.7 | convolution fusion | flops 4848353280 | bytes 15208448 | tf_op jit(solution)/shard_map/dot_general | solution.py:84
  115.9 1.7 broadcast_select_fusion.1
  117.6 6.0 %all-to-all-done.3 = bf16[16,2,144,512]{3,2,1,0:T(8,128)(2,1)} async-done(((bf16[16,2,144,512]{3,2,1,0:T(8,128)(2,1)}), bf16[16,2,144,512]{3,2,1,0:T(8,128)(2,1)}, u32[]{:S(2)}, u32[]{:S(2)}) %all-to-all-start.3) | async-done | bytes 4718624 | tf_op jit(solution)/shard_map/all_to_all | solution.py:35
  123.6 32.9 %all_to_all.25 = bf16[16,144,512]{2,1,0:T(8,128)(2,1)} all-to-all(bf16[16,144,512]{2,1,0:T(8,128)(2,1)S(1)} %bitcast.38), channel_id=1, replica_groups=mesh['zl'=2,'y'=4,'x'=4,'zh'=4,'c'=2] {'y','x'}, dimensions={0} | all-to-all | bytes 4718592 | tf_op jit(solution)/shard_map/all_to_all | solution.py:90
  156.5 3.9 %all-to-all-start.2 = ((bf16[16,144,512]{2,1,0:T(8,128)(2,1)}), bf16[16,144,512]{2,1,0:T(8,128)(2,1)S(1)}, u32[]{:S(2)}, u32[]{:S(2)}) async-start(bf16[16,144,512]{2,1,0:T(8,128)(2,1)} %bitcast.37), calls=%async_computation.2 | async-start | bytes 4718592 | tf_op jit(solution)/shard_map/all_to_all | solution.py:92
  160.5 2.8 %copy.19 = bf16[16,2,144,512]{3,2,0,1:T(8,128)(2,1)S(1)} copy(bf16[16,2,144,512]{3,2,1,0:T(8,128)(2,1)} %all-to-all-done.3) | data formatting | bytes 9437184 | tf_op jit(solution)/shard_map/all_to_all | solution.py:35
  163.3 0.3 copy-done.2
  163.5 1.0 convert_reduce_fusion
  164.6 1.9 collective-permute-start.2
  166.4 8.8 %fusion.3 = bf16[1024,512]{1,0:T(8,128)(2,1)} fusion(bf16[4608,512]{1,0:T(8,128)(2,1)S(1)} %bitcast.39, bf16[1024,4608]{0,1:T(8,128)(2,1)} %all-gather.2.cloned.1.call-done, f32[1024]{0:T(1024)S(1)} %mul.109), kind=kOutput, calls=%fused_computation.13 | convolution fusion | flops 4846518272 | bytes 15208448 | tf_op jit(solution)/shard_map/dot_general | solution.py:93
  175.2 15.2 %all-to-all-done.2 = bf16[16,144,512]{2,1,0:T(8,128)(2,1)S(1)} async-done(((bf16[16,144,512]{2,1,0:T(8,128)(2,1)}), bf16[16,144,512]{2,1,0:T(8,128)(2,1)S(1)}, u32[]{:S(2)}, u32[]{:S(2)}) %all-to-all-start.2) | async-done | bytes 2359328 | tf_op jit(solution)/shard_map/all_to_all | solution.py:92
  190.4 0.3 convert_reduce_fusion.1
  190.8 1.7 add_multiply_fusion
  (38 shorter events, 0.6 us)
Async XLA Ops:
  7.2 99.7 %copy-start = (bf16[1024,512]{1,0:T(8,128)(2,1)S(1)}, bf16[1024,512]{1,0:T(8,128)(2,1)}, u32[]{:S(2)}) copy-start(bf16[1024,512]{1,0:T(8,128)(2,1)} %param.19) | copy-start | bytes 3145732
  7.2 19.1 %copy-start.3 = (bf16[2,144,576]{2,1,0:T(8,128)(2,1)S(1)}, bf16[2,144,576]{2,1,0:T(8,128)(2,1)}, u32[]{:S(2)}) copy-start(bf16[2,144,576]{2,1,0:T(8,128)(2,1)} %param.15) | copy-start | bytes 995332
  7.2 15.9 %copy-start.1 = (s32[2,8]{1,0:T(2,128)S(1)}, s32[2,8]{1,0:T(2,128)}, u32[]{:S(2)}) copy-start(s32[2,8]{1,0:T(2,128)} %param.13) | copy-start | bytes 196
  7.2 99.7 %all-gather.2.cloned.1.call-start = ((), (), s32[]{:S(2)}) async-start(), calls=%async_computation.5 | async-start | bytes 10616832 | tf_op jit(solution)/shard_map/all_gather | solution.py:28
  7.9 18.4 %collective-permute-start = (bf16[2,144,576]{2,1,0:T(8,128)(2,1)}, bf16[2,144,576]{2,1,0:T(8,128)(2,1)S(1)}, u32[]{:S(2)}, u32[]{:S(2)}) collective-permute-start(bf16[2,144,576]{2,1,0:T(8,128)(2,1)} %param.15), channel_id=1, source_target_pairs={{0,128},{128,0},{1,129},{129,1},{2,130},{130,2},{3,131},{131,3},{4... | collective-permute-start | bytes 995336 | tf_op jit(solution)/shard_map/ppermute | solution.py:30
  10.8 15.2 %all-to-all-start = ((bf16[16,36,128]{2,1,0:T(8,128)(2,1)}), bf16[16,36,128]{2,1,0:T(8,128)(2,1)S(1)}, u32[]{:S(2)}, u32[]{:S(2)}) async-start(bf16[16,36,128]{2,1,0:T(8,128)(2,1)} %reshape.135), calls=%async_computation | async-start | bytes 327680 | tf_op jit(solution)/shard_map/all_to_all | solution.py:45
  17.8 17.5 %collective-permute-start.1 = (bf16[144,512]{1,0:T(8,128)(2,1)}, bf16[144,512]{1,0:T(8,128)(2,1)S(1)}, u32[]{:S(2)}, u32[]{:S(2)}) collective-permute-start(bf16[144,512]{1,0:T(8,128)(2,1)} %param.21), channel_id=1, source_target_pairs={{0,128},{128,0},{1,129},{129,1},{2,130},{130,2},{3,131},{131,3},{4... | collective-permute-start | bytes 442376 | tf_op jit(solution)/shard_map/ppermute | solution.py:29
  26.6 8.8 %copy-start.4 = (bf16[144,512]{1,0:T(8,128)(2,1)S(1)}, bf16[144,512]{1,0:T(8,128)(2,1)}, u32[]{:S(2)}) copy-start(bf16[144,512]{1,0:T(8,128)(2,1)} %param.21) | copy-start | bytes 442372
  28.8 24.2 %all-to-all-start.1 = ((f32[16,16,1152]{2,1,0:T(8,128)}), f32[16,16,1152]{2,1,0:T(8,128)S(1)}, u32[]{:S(2)}, u32[]{:S(2)}) async-start(f32[16,16,1152]{2,1,0:T(8,128)} %bitcast.6), calls=%async_computation.1 | async-start | bytes 2359296 | tf_op jit(solution)/shard_map/all_to_all | solution.py:54
  52.9 70.7 %all-to-all-start.3 = ((bf16[16,2,144,512]{3,2,1,0:T(8,128)(2,1)}), bf16[16,2,144,512]{3,2,1,0:T(8,128)(2,1)}, u32[]{:S(2)}, u32[]{:S(2)}) async-start(bf16[16,2,144,512]{3,2,1,0:T(8,128)(2,1)} %broadcast_select_fusion), calls=%async_computation.3 | async-start | bytes 9437184 | tf_op jit(solution)/shard_map/all_to_all | solution.py:35
  57.5 1.8 copy-start.5
  57.5 1.8 copy-start.6
  57.5 17.7 %copy-start.7 = (f32[16]{0:T(128)S(1)}, f32[16]{0:T(128)}, u32[]{:S(2)}) copy-start(f32[16]{0:T(128)} %param.18) | copy-start | bytes 196
  156.5 33.9 %all-to-all-start.2 = ((bf16[16,144,512]{2,1,0:T(8,128)(2,1)}), bf16[16,144,512]{2,1,0:T(8,128)(2,1)S(1)}, u32[]{:S(2)}, u32[]{:S(2)}) async-start(bf16[16,144,512]{2,1,0:T(8,128)(2,1)} %bitcast.37), calls=%async_computation.2 | async-start | bytes 4718592 | tf_op jit(solution)/shard_map/all_to_all | solution.py:92
  160.5 3.1 %copy-start.2 = (bf16[16,144,512]{2,1,0:T(8,128)(2,1)S(1)}, bf16[16,144,512]{2,1,0:T(8,128)(2,1)}, u32[]{:S(2)}) copy-start(bf16[16,144,512]{2,1,0:T(8,128)(2,1)} %all_to_all.25) | copy-start | bytes 7077892
  164.6 26.2 %collective-permute-start.2 = (f32[144,512]{1,0:T(8,128)}, f32[144,512]{1,0:T(8,128)}, u32[]{:S(2)}, u32[]{:S(2)}) collective-permute-start(f32[144,512]{1,0:T(8,128)} %convert_reduce_fusion), channel_id=1, source_target_pairs={{0,128},{128,0},{1,129},{129,1},{2,130},{130,2},{3,131},{131,3},{4... | collective-permute-start | bytes 884744 | tf_op jit(solution)/shard_map/ppermute | solution.py:91
Sparse Core Ops, SparseCore 0:
  9.8 96.9 all-gather.1
